TPU v7x, 768 devices: a whole 4x8x12 slice. The times are simulated.
768 devices in a mesh: blk: 192 (over z, y, core), sub: 4 (over x).
Axes of the slice: x: 4, y: 8, z: 12, core: 2. Of those that a mesh axis runs over, the one named last changes fastest.
Arguments:
- adj_source: float32 [6, 6144, 2048], P(None, 'blk', 'sub'), may hold values from -6 to 6
- jac_diag: float32 [6, 6, 6144, 2048], P(None, None, 'blk', 'sub'), may hold values from -0.6 to 0.6
- face_weights: float32 [8, 6144, 2048], P(None, 'blk', 'sub'), may hold values from 0.02 to 0.12
- flux_jac: float32 [8, 6, 6], replicated, may hold values from -1.25 to 1.25
- face_link: int32 [192], replicated, may hold values 0 or 1
- node_grad: bfloat16 [3, 6, 6144, 2048], P(None, None, 'blk', 'sub'), may hold values from -2.5 to 2.5
- stiffness: float32 [6144, 2048], P(('blk', 'sub')), may hold values from 0.5 to 5
Outputs:
- adjoint: float32 [6, 6144, 2048], P(None, 'blk', 'sub')
- warp_adjoint: float32 [3, 6144, 2048], P(None, ('blk', 'sub'))
Inputs may be any that keep to these rules, and one draw needn't show every extreme that they name: `face_link`: 1 where a block's upper face meets the next block along the first grid direction, the last block's meeting the first.
All inputs are finite; a program needn't handle non-finite values.
Results may differ from a plain program's by a relative error of at most 0.0005.
Values sent between devices are 32-bit elements; how exact they have to be, the bound alone decides.
No kernel may reach another device: no remote copies, remote signals or barrier semaphores. Data moves between devices by JAX's collectives and lax.ppermute only.
A program may use at most 64 MiB of HBM per device.

v0:
```python
import numpy as np
import jax
import jax.numpy as jnp
from jax import lax
from jax.sharding import PartitionSpec as P
from jax.experimental import pallas as pl
from jax.experimental.pallas import tpu as pltpu

ITERS = 4
SWEEPS = 6


relax_factor = 0.8
couple_factor = 2.0 / 9.0
offsets_table = ((1, 0), (-1, 0), (2, 0), (-2, 0), (0, 1), (0, -1), (0, 2), (0, -2))
REACH = 2
LANES = 128


def ring_pairs(count, periodic):
    forward = [(i, i + 1) for i in range(count - 1)]
    if periodic:
        forward.append((count - 1, 0))
    backward = [(target, source) for source, target in forward]
    return forward, backward


TILE = 8


def flow_kernel(flux_ref, link_ref, tile_ref, out_ref, buf0, buf1):
    nf = out_ref.shape[0]
    rows_here = out_ref.shape[1]
    cols_here = out_ref.shape[2]
    width = tile_ref.shape[2]
    pad = 2 * TILE
    n_tiles = tile_ref.shape[1] // TILE
    jd0 = nf
    fw0 = nf + nf * nf
    link_above = link_ref[0]
    link_below = link_ref[1]
    bufs = (buf0, buf1)
    for iteration in range(ITERS):
        pin = tile_ref if iteration == 0 else bufs[(iteration - 1) % 2]
        pout = bufs[iteration % 2]
        last = iteration == ITERS - 1
        first = pad // TILE if last else 1
        stop = (pad + rows_here) // TILE if last else n_tiles - 1

        def body(t, carry, pin=pin, pout=pout):
            r0 = pl.multiple_of(t * TILE, TILE)
            win = [pin[g, pl.ds(r0 - TILE, 3 * TILE), :] for g in range(nf)]
            centre = [w[TILE : 2 * TILE] for w in win]
            rows = r0 - pad + lax.broadcasted_iota(jnp.int32, (TILE, width), 0)
            here = (rows + 2 * rows_here) // rows_here
            acc = []
            for f in range(nf):
                a = tile_ref[jd0 + f * nf, pl.ds(r0, TILE), :] * centre[0]
                for g in range(1, nf):
                    a = a + tile_ref[jd0 + f * nf + g, pl.ds(r0, TILE), :] * centre[g]
                acc.append(centre[f] + a)
            for direction in range(len(offsets_table)):
                row_step, col_step = offsets_table[direction]
                if row_step != 0:
                    shifted = [
                        pltpu.roll(w, (-row_step) % (3 * TILE), 0)[TILE : 2 * TILE] for w in win
                    ]
                    there = (rows + row_step + 2 * rows_here) // rows_here
                    link = jnp.where(jnp.minimum(here, there) < 2, link_below, link_above)
                    factor = jnp.where(here != there, link, 1.0)
                    shifted = [x * factor for x in shifted]
                else:
                    shifted = [pltpu.roll(c, (-col_step) % width, 1) for c in centre]
                weight = tile_ref[fw0 + direction, pl.ds(r0, TILE), :]
                for f in range(nf):
                    base = direction * nf * nf + f * nf
                    mixed = flux_ref[base] * shifted[0]
                    for g in range(1, nf):
                        mixed = mixed + flux_ref[base + g] * shifted[g]
                    acc[f] = acc[f] - weight * mixed
            for f in range(nf):
                src = tile_ref[f, pl.ds(r0, TILE), :]
                pout[f, pl.ds(r0, TILE), :] = centre[f] + relax_factor * (src - acc[f])
            return carry

        lax.fori_loop(first, stop, body, 0)
    final = bufs[(ITERS - 1) % 2]
    out_ref[...] = final[:, pad : pad + rows_here, 0:cols_here]


def flow_iterations(flux_flat, links, tile, nf, rows_here, cols_here):
    return pl.pallas_call(
        flow_kernel,
        out_shape=jax.ShapeDtypeStruct((nf, rows_here, cols_here), jnp.float32),
        in_specs=[
            pl.BlockSpec(memory_space=pltpu.SMEM),
            pl.BlockSpec(memory_space=pltpu.SMEM),
            pl.BlockSpec(memory_space=pltpu.VMEM),
        ],
        out_specs=pl.BlockSpec(memory_space=pltpu.VMEM),
        scratch_shapes=[pltpu.VMEM((nf,) + tile.shape[1:], jnp.float32)] * 2,
        compiler_params=pltpu.CompilerParams(vmem_limit_bytes=48 * 1024 * 1024),
    )(flux_flat, links, tile)


def local(adj_source, jac_diag, face_weights, flux_jac, face_link, node_grad, stiffness):
    block_index = lax.axis_index("blk")
    block_count = lax.axis_size("blk")
    link_above = face_link[block_index].astype(jnp.float32)
    link_below = face_link[(block_index + block_count - 1) % block_count].astype(jnp.float32)
    nf = adj_source.shape[0]
    rows_here = adj_source.shape[1]
    cols_here = adj_source.shape[2]
    deep = REACH * ITERS
    width = -(-(cols_here + 2 * deep) // LANES) * LANES

    stack = jnp.concatenate(
        [adj_source, jac_diag.reshape((nf * nf,) + jac_diag.shape[2:]), face_weights], axis=0
    )
    forward, backward = ring_pairs(block_count, True)
    from_below = lax.ppermute(stack[:, rows_here - deep :], "blk", forward)
    from_above = lax.ppermute(stack[:, :deep], "blk", backward)
    zero_rows = jnp.zeros((stack.shape[0], 2 * TILE - deep, cols_here), jnp.float32)
    tall = jnp.concatenate([zero_rows, from_below, stack, from_above, zero_rows], axis=1)
    sub_count = lax.axis_size("sub")
    forward, backward = ring_pairs(sub_count, True)
    from_left = lax.ppermute(jnp.swapaxes(tall[:, :, cols_here - deep :], 1, 2), "sub", forward)
    from_right = lax.ppermute(jnp.swapaxes(tall[:, :, :deep], 1, 2), "sub", backward)
    gap = jnp.zeros(tall.shape[:2] + (width - cols_here - 2 * deep,), jnp.float32)
    tile = jnp.concatenate(
        [tall, jnp.swapaxes(from_right, 1, 2), gap, jnp.swapaxes(from_left, 1, 2)], axis=2
    )
    links = jnp.stack([link_above, link_below])
    adjoint = flow_iterations(flux_jac.reshape(-1), links, tile, nf, rows_here, cols_here)

    sensitivity = jnp.einsum(
        "cfij,fij->cij", node_grad.astype(jnp.float32), adjoint, precision=lax.Precision.HIGHEST
    )
    moved = lax.all_to_all(sensitivity, "sub", split_axis=1, concat_axis=2, tiled=True)

    part_axis = ("blk", "sub")
    part_index = block_index * sub_count + lax.axis_index("sub")
    part_count = block_count * sub_count
    warp_rows = moved.shape[1]
    both = jnp.concatenate([moved, stiffness[None]], axis=0)
    forward, backward = ring_pairs(part_count, False)
    part_below = lax.ppermute(both, part_axis, forward)
    part_above = lax.ppermute(both, part_axis, backward)
    both_x = jnp.concatenate([both, part_above, part_below], axis=1)
    local_rows = np.arange(3 * warp_rows)
    local_rows = np.where(local_rows < 2 * warp_rows, local_rows, local_rows - 3 * warp_rows)
    global_rows = part_index * warp_rows + jnp.asarray(local_rows, jnp.int32)
    valid = ((global_rows >= 0) & (global_rows < part_count * warp_rows))[:, None]
    sens_x = both_x[:-1]
    stiff_x = jnp.where(valid, both_x[-1], 1.0)
    root_stiff = jnp.sqrt(stiff_x)
    base_term = sens_x / stiff_x[None]
    scale_term = couple_factor / root_stiff
    warp_adjoint = jnp.zeros_like(base_term)
    for sweep_index in range(SWEEPS):
        spread = jnp.where(valid[None], root_stiff[None] * warp_adjoint, 0.0)
        beside_all = (
            jnp.roll(spread, 1, 1) + jnp.roll(spread, -1, 1) + jnp.roll(spread, 1, 2) + jnp.roll(spread, -1, 2)
        )
        warp_adjoint = base_term + scale_term[None] * beside_all
    return (adjoint, warp_adjoint[:, :warp_rows])


def solution(mesh):
    placed = (
        P(None, "blk", "sub"),
        P(None, None, "blk", "sub"),
        P(None, "blk", "sub"),
        P(),
        P(),
        P(None, None, "blk", "sub"),
        P(("blk", "sub"), None),
    )
    return jax.shard_map(
        local,
        mesh=mesh,
        in_specs=placed,
        out_specs=(P(None, "blk", "sub"), P(None, ("blk", "sub"), None)),
        check_vma=False,
    )
```

profile of v0, /device:TPU:1, one launch (start us, length us, event | category | flops | bytes accessed | tf_op | source)
XLA Modules:
  0.0 108.7 jit_solution(3390009755030296016)
XLA Ops:
  0.6 2.3 %pad_maximum_fusion.1 = f32[50,32,512]{2,1,0:T(8,128)S(1)} fusion(f32[8,32,512]{2,1,0:T(8,128)} %param.10, f32[36,32,512]{2,1,0:T(8,128)} %bitcast.25, f32[6,32,512]{2,1,0:T(8,128)} %param.8), kind=kLoop, calls=%fused_computation.1 | loop fusion | flops 1638400 | bytes 6553600 | tf_op jit(solution)/shard_map/concatenate | solution.py:117
  3.0 1.3 %fusion.34 = (f32[50,8,512]{2,1,0:T(8,128)}, f32[50,8,512]{2,1,0:T(8,128)}) fusion(f32[50,32,512]{2,1,0:T(8,128)S(1)} %pad_maximum_fusion.1), kind=kLoop, calls=%fused_computation.65 | loop fusion | bytes 3276800 | tf_op jit(solution)/shard_map/slice | solution.py:122
  4.3 4.7 %collective-permute-start = (f32[50,8,512]{2,1,0:T(8,128)}, f32[50,8,512]{2,1,0:T(8,128)}, u32[]{:S(2)}, u32[]{:S(2)}) collective-permute-start(f32[50,8,512]{2,1,0:T(8,128)} %get-tuple-element.9), channel_id=1, source_target_pairs={{0,4},{4,8},{8,12},{12,16},{16,20},{20,24},{24,28},{28,32},{32,36}... | collective-permute-start | bytes 2457608 | tf_op jit(solution)/shard_map/ppermute | solution.py:121
  9.0 9.8 %collective-permute-start.1 = (f32[50,8,512]{2,1,0:T(8,128)}, f32[50,8,512]{2,1,0:T(8,128)}, u32[]{:S(2)}, u32[]{:S(2)}) collective-permute-start(f32[50,8,512]{2,1,0:T(8,128)} %get-tuple-element.8), channel_id=1, source_target_pairs={{4,0},{8,4},{12,8},{16,12},{20,16},{24,20},{28,24},{32,28},{36,32}... | collective-permute-start | bytes 2457608 | tf_op jit(solution)/shard_map/ppermute | solution.py:122
  18.8 0.6 fusion.59
  20.7 0.1 reshape.29.flux_ref
  21.0 1.2 %constant_dynamic-update-slice_fusion.2 = f32[50,64,512]{2,1,0:T(8,128)S(1)} fusion(f32[50,64,512]{2,1,0:T(8,128)S(1)} %broadcast_dynamic-update-slice_fusion, f32[50,8,512]{2,1,0:T(8,128)} %collective-permute-done), kind=kLoop, calls=%fused_computation.62 | loop fusion | bytes 1638400
  22.3 0.3 constant_dynamic-update-slice_fusion.1
  22.6 0.4 collective-permute-done.1
  23.0 1.2 %constant_dynamic-update-slice_fusion = f32[50,64,512]{2,1,0:T(8,128)S(1)} fusion(f32[50,64,512]{2,1,0:T(8,128)S(1)} %constant_dynamic-update-slice_fusion.1, f32[50,8,512]{2,1,0:T(8,128)} %collective-permute-done.1), kind=kLoop, calls=%fused_computation.60 | loop fusion | bytes 1638400
  24.3 0.6 slice_bitcast_fusion.1
  24.9 2.1 %copy-done = f32[50,64,512]{2,1,0:T(8,128)} copy-done((f32[50,64,512]{2,1,0:T(8,128)}, f32[50,64,512]{2,1,0:T(8,128)S(1)}, u32[]{:S(2)}) %copy-start) | copy-done | bytes 6553624
  27.0 0.5 copy.12
  27.5 4.4 %collective-permute-start.2 = (f32[50,8,64]{2,1,0:T(8,128)S(1)}, f32[50,8,64]{2,1,0:T(8,128)S(1)}, u32[]{:S(2)}, u32[]{:S(2)}) collective-permute-start(f32[50,8,64]{2,1,0:T(8,128)S(1)} %copy.12), channel_id=1, source_target_pairs={{1,0},{2,1},{3,2},{0,3},{5,4},{6,5},{7,6},{4,7},{9,8},{10,9},{11,1... | collective-permute-start | bytes 307208 | tf_op jit(solution)/shard_map/ppermute | solution.py:128
  31.9 0.5 copy.14
  32.3 1.9 %collective-permute-start.3 = (f32[50,8,64]{2,1,0:T(8,128)S(1)}, f32[50,8,64]{2,1,0:T(8,128)}, u32[]{:S(2)}, u32[]{:S(2)}) collective-permute-start(f32[50,8,64]{2,1,0:T(8,128)S(1)} %copy.14), channel_id=1, source_target_pairs={{0,1},{1,2},{2,3},{3,0},{4,5},{5,6},{6,7},{7,4},{8,9},{9,10},{10,1... | collective-permute-start | bytes 307208 | tf_op jit(solution)/shard_map/ppermute | solution.py:127
  34.4 0.2 collective-permute-done.2
  34.6 0.5 copy.13
  35.1 5.1 %collective-permute-done.3 = f32[50,8,64]{2,1,0:T(8,128)} collective-permute-done((f32[50,8,64]{2,1,0:T(8,128)S(1)}, f32[50,8,64]{2,1,0:T(8,128)}, u32[]{:S(2)}, u32[]{:S(2)}) %collective-permute-start.3) | collective-permute-done | bytes 102432 | tf_op jit(solution)/shard_map/ppermute | solution.py:127
  40.2 1.4 %copy.15 = f32[50,8,64]{1,2,0:T(8,128)S(1)} copy(f32[50,8,64]{2,1,0:T(8,128)} %collective-permute-done.3) | data formatting | bytes 204800 | tf_op jit(solution)/shard_map/ppermute | solution.py:127
  41.6 5.9 %pad_maximum_fusion.tile_ref = f32[50,64,640]{2,1,0:T(8,128)} fusion(f32[50,64,8]{2,1,0:T(8,128)S(1)} %bitcast.28, f32[50,64,8]{2,1,0:T(8,128)S(1)} %bitcast.27, f32[50,64,512]{2,1,0:T(8,128)} %copy-done, f32[640]{0:T(1024)S(1)} %pad.56.clone), kind=kLoop, calls=%fused_computation | loop fusion | flops 6144000 | bytes 14952960 | tf_op jit(solution)/shard_map/concatenate | solution.py:130
  47.5 19.9 %shard_map.95 = f32[6,32,512]{2,1,0:T(8,128)} custom-call(f32[288]{0:T(512)S(1)} %reshape.29.flux_ref, f32[2]{0:T(128)S(1)} %pad_maximum_fusion.8.link_ref, f32[50,64,640]{2,1,0:T(8,128)} %pad_maximum_fusion.tile_ref), custom_call_target="tpu_custom_call" | custom-call | tf_op jit(solution)/shard_map/pallas_call | solution.py:92
  67.4 1.1 %multiply_reduce_fusion = f32[32,512,3]{1,0,2:T(8,128)S(1)} fusion(f32[32,512,6]{1,0,2:T(8,128)} %bitcast.33, bf16[3,6,32,512]{3,2,1,0:T(8,128)(2,1)S(1)} %copy-done.4), kind=kLoop, calls=%fused_computation.4 | loop fusion | flops 835584 | bytes 1179648
  68.6 0.1 copy.27
  68.7 7.9 %all_to_all.18 = f32[3,32,512]{2,0,1:T(4,128)S(1)} all-to-all(f32[3,32,512]{2,0,1:T(4,128)S(1)} %bitcast.34), channel_id=1, replica_groups=mesh['blk'=192,'sub'=4] {'sub'}, dimensions={1} | all-to-all | bytes 393216 | tf_op jit(solution)/shard_map/all_to_all | solution.py:139
  76.7 17.2 %collective-permute-start.4 = (f32[4,8,2048]{2,1,0:T(8,128)S(1)}, f32[4,8,2048]{2,1,0:T(8,128)S(1)}, u32[]{:S(2)}, u32[]{:S(2)}) collective-permute-start(f32[4,8,2048]{2,1,0:T(8,128)S(1)} %pad_maximum_fusion.3), channel_id=1, source_target_pairs={{1,0},{2,1},{3,2},{4,3},{5,4},{6,5},{7,6},{8,7},{9,8},{10,9},{11,1... | collective-permute-start | bytes 786440 | tf_op jit(solution)/shard_map/ppermute | solution.py:148
  94.0 1.9 %collective-permute-start.5 = (f32[4,8,2048]{2,1,0:T(8,128)S(1)}, f32[4,8,2048]{2,1,0:T(8,128)S(1)}, u32[]{:S(2)}, u32[]{:S(2)}) collective-permute-start(f32[4,8,2048]{2,1,0:T(8,128)S(1)} %pad_maximum_fusion.3), channel_id=1, source_target_pairs={{0,1},{1,2},{2,3},{3,4},{4,5},{5,6},{6,7},{7,8},{8,9},{9,10},{10,1... | collective-permute-start | bytes 786440 | tf_op jit(solution)/shard_map/ppermute | solution.py:147
  95.9 1.3 %collective-permute-done.4 = f32[4,8,2048]{2,1,0:T(8,128)S(1)} collective-permute-done((f32[4,8,2048]{2,1,0:T(8,128)S(1)}, f32[4,8,2048]{2,1,0:T(8,128)S(1)}, u32[]{:S(2)}, u32[]{:S(2)}) %collective-permute-start.4) | collective-permute-done | bytes 262176 | tf_op jit(solution)/shard_map/ppermute | solution.py:148
  97.3 5.6 %collective-permute-done.5 = f32[4,8,2048]{2,1,0:T(8,128)S(1)} collective-permute-done((f32[4,8,2048]{2,1,0:T(8,128)S(1)}, f32[4,8,2048]{2,1,0:T(8,128)S(1)}, u32[]{:S(2)}, u32[]{:S(2)}) %collective-permute-start.5) | collective-permute-done | bytes 262176 | tf_op jit(solution)/shard_map/ppermute | solution.py:147
  102.9 0.1 multiply_bitcast_fusion
  103.0 0.1 broadcast_select_fusion
  103.2 0.2 fusion.55
  103.4 0.1 fusion.57
  103.7 0.4 fusion.5
  104.1 0.2 fusion.51
  104.4 0.1 fusion.53
  104.6 0.4 fusion.11
  105.0 0.2 fusion.47
  105.2 0.1 fusion.49
  105.4 0.4 fusion.17
  105.8 0.2 fusion.43
  106.0 0.1 fusion.45
  106.2 0.4 fusion.23
  106.6 0.2 fusion.39
  106.8 0.1 fusion.41
  107.1 0.4 fusion.29
  107.5 0.2 fusion.38
  107.9 0.8 slice_add_fusion
  (44 shorter events, 1.4 us)
Async XLA Ops:
  2.9 15.9 %copy-start.7 = (s32[192]{0:T(256)S(1)}, s32[192]{0:T(256)}, u32[]{:S(2)}) copy-start(s32[192]{0:T(256)} %param.12) | copy-start | bytes 2308
  2.9 17.8 %copy-start.6 = (f32[8,6,6]{2,0,1:T(8,128)S(1)}, f32[8,6,6]{2,0,1:T(8,128)}, u32[]{:S(2)}) copy-start(f32[8,6,6]{2,0,1:T(8,128)} %param.11) | copy-start | bytes 3460
  2.9 19.3 %copy-start.1 = (f32[6,6,32,512]{3,2,1,0:T(8,128)S(1)}, f32[6,6,32,512]{3,2,1,0:T(8,128)}, u32[]{:S(2)}) copy-start(f32[6,6,32,512]{3,2,1,0:T(8,128)} %param.9) | copy-start | bytes 7077892
  2.9 19.3 %copy-start.2 = (f32[8,32,512]{2,1,0:T(8,128)S(1)}, f32[8,32,512]{2,1,0:T(8,128)}, u32[]{:S(2)}) copy-start(f32[8,32,512]{2,1,0:T(8,128)} %param.10) | copy-start | bytes 1572868
  2.9 19.3 %copy-start.3 = (f32[6,32,512]{2,1,0:T(8,128)S(1)}, f32[6,32,512]{2,1,0:T(8,128)}, u32[]{:S(2)}) copy-start(f32[6,32,512]{2,1,0:T(8,128)} %param.8) | copy-start | bytes 1179652
  4.3 16.7 %collective-permute-start = (f32[50,8,512]{2,1,0:T(8,128)}, f32[50,8,512]{2,1,0:T(8,128)}, u32[]{:S(2)}, u32[]{:S(2)}) collective-permute-start(f32[50,8,512]{2,1,0:T(8,128)} %get-tuple-element.9), channel_id=1, source_target_pairs={{0,4},{4,8},{8,12},{12,16},{16,20},{20,24},{24,28},{28,32},{32,36}... | collective-permute-start | bytes 2457608 | tf_op jit(solution)/shard_map/ppermute | solution.py:121
  9.0 14.0 %collective-permute-start.1 = (f32[50,8,512]{2,1,0:T(8,128)}, f32[50,8,512]{2,1,0:T(8,128)}, u32[]{:S(2)}, u32[]{:S(2)}) collective-permute-start(f32[50,8,512]{2,1,0:T(8,128)} %get-tuple-element.8), channel_id=1, source_target_pairs={{4,0},{8,4},{12,8},{16,12},{20,16},{24,20},{28,24},{32,28},{36,32}... | collective-permute-start | bytes 2457608 | tf_op jit(solution)/shard_map/ppermute | solution.py:122
  24.3 2.8 %copy-start = (f32[50,64,512]{2,1,0:T(8,128)}, f32[50,64,512]{2,1,0:T(8,128)S(1)}, u32[]{:S(2)}) copy-start(f32[50,64,512]{2,1,0:T(8,128)S(1)} %broadcast_dynamic-update-slice_fusion.1) | copy-start | bytes 19660804
  27.5 7.1 %collective-permute-start.2 = (f32[50,8,64]{2,1,0:T(8,128)S(1)}, f32[50,8,64]{2,1,0:T(8,128)S(1)}, u32[]{:S(2)}, u32[]{:S(2)}) collective-permute-start(f32[50,8,64]{2,1,0:T(8,128)S(1)} %copy.12), channel_id=1, source_target_pairs={{1,0},{2,1},{3,2},{0,3},{5,4},{6,5},{7,6},{4,7},{9,8},{10,9},{11,1... | collective-permute-start | bytes 307208 | tf_op jit(solution)/shard_map/ppermute | solution.py:128
  32.3 7.8 %collective-permute-start.3 = (f32[50,8,64]{2,1,0:T(8,128)S(1)}, f32[50,8,64]{2,1,0:T(8,128)}, u32[]{:S(2)}, u32[]{:S(2)}) collective-permute-start(f32[50,8,64]{2,1,0:T(8,128)S(1)} %copy.14), channel_id=1, source_target_pairs={{0,1},{1,2},{2,3},{3,0},{4,5},{5,6},{6,7},{7,4},{8,9},{9,10},{10,1... | collective-permute-start | bytes 307208 | tf_op jit(solution)/shard_map/ppermute | solution.py:127
  47.5 19.9 %copy-start.4 = (bf16[3,6,32,512]{3,2,1,0:T(8,128)(2,1)S(1)}, bf16[3,6,32,512]{3,2,1,0:T(8,128)(2,1)}, u32[]{:S(2)}) copy-start(bf16[3,6,32,512]{3,2,1,0:T(8,128)(2,1)} %param.13) | copy-start | bytes 1769476
  47.5 29.2 %copy-start.5 = (f32[8,2048]{1,0:T(8,128)S(1)}, f32[8,2048]{1,0:T(8,128)}, u32[]{:S(2)}) copy-start(f32[8,2048]{1,0:T(8,128)} %param.14) | copy-start | bytes 196612
  47.5 48.4 %copy-start.8 = (s32[24]{0:T(128)S(1)}, s32[24]{0:T(128)}, u32[]{:S(2)}) copy-start(s32[24]{0:T(128)} %constant.41.clone) | copy-start | bytes 292
  76.7 20.5 %collective-permute-start.4 = (f32[4,8,2048]{2,1,0:T(8,128)S(1)}, f32[4,8,2048]{2,1,0:T(8,128)S(1)}, u32[]{:S(2)}, u32[]{:S(2)}) collective-permute-start(f32[4,8,2048]{2,1,0:T(8,128)S(1)} %pad_maximum_fusion.3), channel_id=1, source_target_pairs={{1,0},{2,1},{3,2},{4,3},{5,4},{6,5},{7,6},{8,7},{9,8},{10,9},{11,1... | collective-permute-start | bytes 786440 | tf_op jit(solution)/shard_map/ppermute | solution.py:148
  94.0 8.9 %collective-permute-start.5 = (f32[4,8,2048]{2,1,0:T(8,128)S(1)}, f32[4,8,2048]{2,1,0:T(8,128)S(1)}, u32[]{:S(2)}, u32[]{:S(2)}) collective-permute-start(f32[4,8,2048]{2,1,0:T(8,128)S(1)} %pad_maximum_fusion.3), channel_id=1, source_target_pairs={{0,1},{1,2},{2,3},{3,4},{4,5},{5,6},{6,7},{7,8},{8,9},{9,10},{10,1... | collective-permute-start | bytes 786440 | tf_op jit(solution)/shard_map/ppermute | solution.py:147
where the time goes:
time: 109 us
  starting transfers between devices  39.9 us (37%)
  Pallas kernels  19.9 us (18%)
  local copies, waits for them, and re-layouts  13.2 us (12%)
  other arithmetic  12.8 us (12%)
  waiting for transfers between devices  12.6 us (12%)
  blocking collectives  7.92 us (7%)
  between operations  2.41 us (2%)
    pallas_call x1, Pallas kernels, flow_iterations(): pl.pallas_call(flow_kernel, out_shape=jax.ShapeDtypeStruct((nf, rows_here...  19.9 us
    ppermute x1, starting transfers between devices, local(): part_above = lax.ppermute(both, part_axis, backward)  17.2 us
    ppermute x1, starting transfers between devices, local(): from_above = lax.ppermute(stack[:, :deep], 'blk', backward)  9.75 us
    all_to_all x1, blocking collectives, local(): lax.all_to_all(sensitivity, 'sub', split_axis=1, concat_axis=2, tiled=True)  7.92 us
    concatenate x1, other arithmetic, local(): jnp.concatenate([tall, jnp.swapaxes(from_right, 1, 2), gap, jnp.swapaxes(...  5.94 us
    ppermute x1, waiting for transfers between devices, local(): part_below = lax.ppermute(both, part_axis, forward)  5.61 us
    ppermute x1, waiting for transfers between devices, local(): lax.ppermute(jnp.swapaxes(tall[:, :, cols_here - deep:], 1, 2), 'sub', fo...  5.1 us
    ppermute x1, starting transfers between devices, local(): from_below = lax.ppermute(stack[:, rows_here - deep:], 'blk', forward)  4.72 us
  transfers between devices with their start and end apart: 6, of which 5 were waited for; matrix products, arithmetic and copies ran while one was open for 3% of the time, Pallas kernels for 0%

commit v1 on v0

--- a/solution.py
+++ b/solution.py
@@ -117,19 +117,33 @@
     stack = jnp.concatenate(
         [adj_source, jac_diag.reshape((nf * nf,) + jac_diag.shape[2:]), face_weights], axis=0
     )
-    forward, backward = ring_pairs(block_count, True)
-    from_below = lax.ppermute(stack[:, rows_here - deep :], "blk", forward)
-    from_above = lax.ppermute(stack[:, :deep], "blk", backward)
+    sub_count = lax.axis_size("sub")
+
+    def send(piece, row_move, col_move):
+        pairs = [
+            (b * sub_count + c, ((b + row_move) % block_count) * sub_count + (c + col_move) % sub_count)
+            for b in range(block_count)
+            for c in range(sub_count)
+        ]
+        return lax.ppermute(piece, ("blk", "sub"), pairs)
+
+    low_rows = stack[:, rows_here - deep :]
+    high_rows = stack[:, :deep]
+    from_below = send(low_rows, 1, 0)
+    from_above = send(high_rows, -1, 0)
+    from_left = jnp.swapaxes(send(jnp.swapaxes(stack[:, :, cols_here - deep :], 1, 2), 0, 1), 1, 2)
+    from_right = jnp.swapaxes(send(jnp.swapaxes(stack[:, :, :deep], 1, 2), 0, -1), 1, 2)
+    below_left = send(low_rows[:, :, cols_here - deep :], 1, 1)
+    below_right = send(low_rows[:, :, :deep], 1, -1)
+    above_left = send(high_rows[:, :, cols_here - deep :], -1, 1)
+    above_right = send(high_rows[:, :, :deep], -1, -1)
     zero_rows = jnp.zeros((stack.shape[0], 2 * TILE - deep, cols_here), jnp.float32)
+    zero_strip = zero_rows[:, :, :deep]
     tall = jnp.concatenate([zero_rows, from_below, stack, from_above, zero_rows], axis=1)
-    sub_count = lax.axis_size("sub")
-    forward, backward = ring_pairs(sub_count, True)
-    from_left = lax.ppermute(jnp.swapaxes(tall[:, :, cols_here - deep :], 1, 2), "sub", forward)
-    from_right = lax.ppermute(jnp.swapaxes(tall[:, :, :deep], 1, 2), "sub", backward)
+    right = jnp.concatenate([zero_strip, below_right, from_right, above_right, zero_strip], axis=1)
+    left = jnp.concatenate([zero_strip, below_left, from_left, above_left, zero_strip], axis=1)
     gap = jnp.zeros(tall.shape[:2] + (width - cols_here - 2 * deep,), jnp.float32)
-    tile = jnp.concatenate(
-        [tall, jnp.swapaxes(from_right, 1, 2), gap, jnp.swapaxes(from_left, 1, 2)], axis=2
-    )
+    tile = jnp.concatenate([tall, right, gap, left], axis=2)
     links = jnp.stack([link_above, link_below])
     adjoint = flow_iterations(flux_jac.reshape(-1), links, tile, nf, rows_here, cols_here)
 

time: 109 us -> 139 us (1.28)
  local copies, waits for them, and re-layouts: 13.2 us -> 33.3 us
  starting transfers between devices: 39.9 us -> 51.4 us
  waiting for transfers between devices: 12.6 us -> 6.78 us
  blocking collectives: 7.92 us -> 10.3 us
  other arithmetic: 12.8 us -> 14.6 us
    ppermute x4 -> x8, starting transfers between devices: 20.8 us -> 40.1 us  [send(): return lax.ppermute(piece, ('blk', 'sub'), pairs)]
    unnamed x22 -> x32, local copies, waits for them, and re-layouts: 4.66 us -> 15.4 us
    ppermute x1, starting transfers between devices: 17.2 us -> 9.17 us  [local(): part_above = lax.ppermute(both, part_axis, backward)]
    ppermute x4 -> x8, waiting for transfers between devices: 5.68 us -> 0.02 us  [send(): return lax.ppermute(piece, ('blk', 'sub'), pairs)]
    transpose x3, local copies, waits for them, and re-layouts: 1.57 us -> 6.16 us  [the longest x2 3.84 us: local(): jnp.swapaxes(stack[:, :, :deep], 1, 2)]
    all_to_all x1, blocking collectives: 7.92 us -> 10.3 us  [local(): lax.all_to_all(sensitivity, 'sub', split_axis=1, concat_axis=2, tiled=True)]
    unnamed x2, other arithmetic: 1.46 us -> 3.24 us
    concatenate x1 -> x3, local copies, waits for them, and re-layouts: 0.07 us -> 1.56 us  [the longest x1 0.76 us: local(): jnp.concatenate([zero_strip, below_left, from_left, above_left, zero_stri...]
  transfers between devices with their start and end apart: 6 -> 10, of which waited for: 5 -> 2; matrix products, arithmetic and copies ran while one was open for 3% -> 21% of each run, Pallas kernels for 0% -> 0%
where the time goes in v1:
time: 139 us; the launch traced here: 138 us
  starting transfers between devices  51.4 us (37%)
  local copies, waits for them, and re-layouts  33.3 us (24%)
  Pallas kernels  19.9 us (14%)
  other arithmetic  14.6 us (11%)
  blocking collectives  10.3 us (7%)
  waiting for transfers between devices  6.78 us (5%)
  between operations  2.22 us (2%)
    ppermute x8, starting transfers between devices, send(): return lax.ppermute(piece, ('blk', 'sub'), pairs)  40.1 us
    pallas_call x1, Pallas kernels, flow_iterations(): pl.pallas_call(flow_kernel, out_shape=jax.ShapeDtypeStruct((nf, rows_here...  19.9 us
    unnamed x32, local copies, waits for them, and re-layouts  15.4 us
    all_to_all x1, blocking collectives, local(): lax.all_to_all(sensitivity, 'sub', split_axis=1, concat_axis=2, tiled=True)  10.3 us
    ppermute x1, starting transfers between devices, local(): part_above = lax.ppermute(both, part_axis, backward)  9.17 us
    concatenate x1, other arithmetic, local(): tile = jnp.concatenate([tall, right, gap, left], axis=2)  5.92 us
    ppermute x1, waiting for transfers between devices, local(): part_below = lax.ppermute(both, part_axis, forward)  5.61 us
    transpose x2, local copies, waits for them, and re-layouts, local(): jnp.swapaxes(stack[:, :, :deep], 1, 2)  3.84 us
  transfers between devices with their start and end apart: 10, of which 2 were waited for; matrix products, arithmetic and copies ran while one was open for 21% of the time, Pallas kernels for 0%

profile of v1, /device:TPU:1, one launch (start us, length us, event | category | flops | bytes accessed | tf_op | source)
XLA Modules:
  0.0 138.4 jit_solution(13987828041340172007)
XLA Ops:
  0.6 2.2 %pad_maximum_fusion.1 = f32[50,32,512]{2,1,0:T(8,128)S(1)} fusion(f32[8,32,512]{2,1,0:T(8,128)} %param.10, f32[36,32,512]{2,1,0:T(8,128)} %bitcast.27, f32[6,32,512]{2,1,0:T(8,128)} %param.8), kind=kLoop, calls=%fused_computation.1 | loop fusion | flops 1638400 | bytes 6553600 | tf_op jit(solution)/shard_map/concatenate | solution.py:117
  2.9 0.9 fusion.35
  3.8 6.8 %collective-permute-start.2 = (f32[50,8,8]{2,1,0:T(8,128)}, f32[50,8,8]{2,1,0:T(8,128)}, u32[]{:S(2)}, u32[]{:S(2)}) collective-permute-start(f32[50,8,8]{2,1,0:T(8,128)} %get-tuple-element.10), channel_id=1, source_target_pairs={{0,7},{1,4},{2,5},{3,6},{4,11},{5,8},{6,9},{7,10},{8,15},{9,12},{1... | collective-permute-start | bytes 38408 | tf_op jit(solution)/shard_map/ppermute | solution.py:128
  10.6 1.5 %slice_bitcast_fusion.1 = (f32[50,8,32]{1,2,0:T(8,128)}, f32[50,8,32]{1,2,0:T(8,128)}) fusion(f32[50,32,512]{2,1,0:T(8,128)S(1)} %pad_maximum_fusion.1), kind=kLoop, calls=%fused_computation.4 | loop fusion | bytes 204800 | tf_op jit(solution)/shard_map/transpose | solution.py:135
  12.1 2.4 %copy.24 = f32[50,8,32]{0,2,1:T(8,128)} copy(f32[50,8,32]{1,2,0:T(8,128)} %get-tuple-element.12) | data formatting | bytes 102400 | tf_op jit(solution)/shard_map/transpose | solution.py:135
  14.4 2.4 %collective-permute-start.3 = (f32[50,8,32]{0,2,1:T(8,128)}, f32[50,8,32]{0,2,1:T(8,128)}, u32[]{:S(2)}, u32[]{:S(2)}) collective-permute-start(f32[50,8,32]{0,2,1:T(8,128)} %copy.24), channel_id=1, source_target_pairs={{0,3},{1,0},{2,1},{3,2},{4,7},{5,4},{6,5},{7,6},{8,11},{9,8},{10,9... | collective-permute-start | bytes 153608 | tf_op jit(solution)/shard_map/ppermute | solution.py:128
  16.9 1.9 %collective-permute-start.4 = (f32[50,8,8]{2,1,0:T(8,128)}, f32[50,8,8]{2,1,0:T(8,128)}, u32[]{:S(2)}, u32[]{:S(2)}) collective-permute-start(f32[50,8,8]{2,1,0:T(8,128)} %get-tuple-element.8), channel_id=1, source_target_pairs={{0,767},{1,764},{2,765},{3,766},{4,3},{5,0},{6,1},{7,2},{8,7},{9,4... | collective-permute-start | bytes 38408 | tf_op jit(solution)/shard_map/ppermute | solution.py:128
  18.8 4.5 %collective-permute-start.5 = (f32[50,8,8]{2,1,0:T(8,128)}, f32[50,8,8]{2,1,0:T(8,128)}, u32[]{:S(2)}, u32[]{:S(2)}) collective-permute-start(f32[50,8,8]{2,1,0:T(8,128)} %get-tuple-element.9), channel_id=1, source_target_pairs={{0,5},{1,6},{2,7},{3,4},{4,9},{5,10},{6,11},{7,8},{8,13},{9,14},{1... | collective-permute-start | bytes 38408 | tf_op jit(solution)/shard_map/ppermute | solution.py:128
  23.4 2.3 %copy.26 = f32[50,8,32]{0,2,1:T(8,128)} copy(f32[50,8,32]{1,2,0:T(8,128)} %get-tuple-element.13) | data formatting | bytes 102400 | tf_op jit(solution)/shard_map/transpose | solution.py:134
  25.7 5.7 %collective-permute-start.6 = (f32[50,8,32]{0,2,1:T(8,128)}, f32[50,8,32]{0,2,1:T(8,128)}, u32[]{:S(2)}, u32[]{:S(2)}) collective-permute-start(f32[50,8,32]{0,2,1:T(8,128)} %copy.26), channel_id=1, source_target_pairs={{0,1},{1,2},{2,3},{3,0},{4,5},{5,6},{6,7},{7,4},{8,9},{9,10},{10,1... | collective-permute-start | bytes 153608 | tf_op jit(solution)/shard_map/ppermute | solution.py:128
  31.5 0.7 broadcast_dynamic-update-slice_fusion.2
  32.2 0.7 broadcast_dynamic-update-slice_fusion.3
  32.9 1.3 fusion.34
  34.2 1.0 broadcast_dynamic-update-slice_fusion
  35.2 0.6 fusion.60
  37.4 10.1 %collective-permute-start.7 = (f32[50,8,8]{2,1,0:T(8,128)S(1)}, f32[50,8,8]{2,1,0:T(8,128)}, u32[]{:S(2)}, u32[]{:S(2)}) collective-permute-start(f32[50,8,8]{2,1,0:T(8,128)S(1)} %get-tuple-element.11), channel_id=1, source_target_pairs={{0,765},{1,766},{2,767},{3,764},{4,1},{5,2},{6,3},{7,0},{8,5},{9,6... | collective-permute-start | bytes 38408 | tf_op jit(solution)/shard_map/ppermute | solution.py:128
  47.5 1.7 %constant_dynamic-update-slice_fusion.4 = f32[50,64,8]{2,1,0:T(8,128)} fusion(f32[50,64,8]{2,1,0:T(8,128)} %broadcast_dynamic-update-slice_fusion.2, f32[50,8,8]{2,1,0:T(8,128)} %collective-permute-done.2), kind=kLoop, calls=%fused_computation.70 | loop fusion | bytes 409600
  49.2 1.9 %collective-permute-start = (f32[50,8,512]{2,1,0:T(8,128)}, f32[50,8,512]{2,1,0:T(8,128)}, u32[]{:S(2)}, u32[]{:S(2)}) collective-permute-start(f32[50,8,512]{2,1,0:T(8,128)} %get-tuple-element.7), channel_id=1, source_target_pairs={{0,4},{1,5},{2,6},{3,7},{4,8},{5,9},{6,10},{7,11},{8,12},{9,13},{1... | collective-permute-start | bytes 2457608 | tf_op jit(solution)/shard_map/ppermute | solution.py:128
  51.1 1.7 %constant_dynamic-update-slice_fusion.6 = f32[50,64,8]{2,1,0:T(8,128)} fusion(f32[50,64,8]{2,1,0:T(8,128)} %broadcast_dynamic-update-slice_fusion.3, f32[50,8,8]{2,1,0:T(8,128)} %collective-permute-done.5), kind=kLoop, calls=%fused_computation.72 | loop fusion | bytes 409600
  52.8 6.7 %collective-permute-start.1 = (f32[50,8,512]{2,1,0:T(8,128)}, f32[50,8,512]{2,1,0:T(8,128)}, u32[]{:S(2)}, u32[]{:S(2)}) collective-permute-start(f32[50,8,512]{2,1,0:T(8,128)} %get-tuple-element.6), channel_id=1, source_target_pairs={{0,764},{1,765},{2,766},{3,767},{4,0},{5,1},{6,2},{7,3},{8,4},{9,5... | collective-permute-start | bytes 2457608 | tf_op jit(solution)/shard_map/ppermute | solution.py:128
  59.5 1.6 %copy.25 = f32[50,8,32]{1,2,0:T(8,128)S(1)} copy(f32[50,8,32]{0,2,1:T(8,128)} %collective-permute-done.3) | data formatting | bytes 102400 | tf_op jit(solution)/shard_map/ppermute | solution.py:128
  61.1 1.0 bitcast_dynamic-update-slice_fusion.1
  62.1 1.7 %copy.27 = f32[50,8,32]{1,2,0:T(8,128)S(1)} copy(f32[50,8,32]{0,2,1:T(8,128)} %collective-permute-done.6) | data formatting | bytes 102400 | tf_op jit(solution)/shard_map/ppermute | solution.py:128
  63.8 1.0 bitcast_dynamic-update-slice_fusion
  64.8 1.7 %constant_dynamic-update-slice_fusion.3 = f32[50,64,8]{2,1,0:T(8,128)} fusion(f32[50,64,8]{2,1,0:T(8,128)} %bitcast_dynamic-update-slice_fusion.1, f32[50,8,8]{2,1,0:T(8,128)} %collective-permute-done.4), kind=kLoop, calls=%fused_computation.69 | loop fusion | bytes 409600
  66.4 0.7 broadcast_dynamic-update-slice_fusion.5
  67.2 1.7 %constant_dynamic-update-slice_fusion.5 = f32[50,64,8]{2,1,0:T(8,128)} fusion(f32[50,64,8]{2,1,0:T(8,128)} %bitcast_dynamic-update-slice_fusion, f32[50,8,8]{2,1,0:T(8,128)} %collective-permute-done.7), kind=kLoop, calls=%fused_computation.71 | loop fusion | bytes 409600
  68.8 0.8 broadcast_dynamic-update-slice_fusion.4
  69.6 2.1 %constant_dynamic-update-slice_fusion.2 = f32[50,64,512]{2,1,0:T(8,128)} fusion(f32[50,64,512]{2,1,0:T(8,128)} %broadcast_dynamic-update-slice_fusion, f32[50,8,512]{2,1,0:T(8,128)} %collective-permute-done), kind=kLoop, calls=%fused_computation.68 | loop fusion | bytes 1638400
  71.7 2.1 %constant_dynamic-update-slice_fusion.1 = f32[50,64,512]{2,1,0:T(8,128)} fusion(f32[50,64,512]{2,1,0:T(8,128)} %constant_dynamic-update-slice_fusion.2, f32[8,32,512]{2,1,0:T(8,128)S(1)} %copy-done.1, f32[36,32,512]{2,1,0:T(8,128)S(1)} %bitcast.28, f32[6,32,512]{2,1,0:T(8,128)S(1)} %copy-done.4), kind=kLoop, calls=%fused_computation.67 | loop fusion | flops 1638400 | bytes 6553600
  73.8 2.2 %constant_dynamic-update-slice_fusion = f32[50,64,512]{2,1,0:T(8,128)} fusion(f32[50,64,512]{2,1,0:T(8,128)} %constant_dynamic-update-slice_fusion.1, f32[50,8,512]{2,1,0:T(8,128)} %collective-permute-done.1), kind=kLoop, calls=%fused_computation.66 | loop fusion | bytes 1638400
  76.0 1.0 broadcast_dynamic-update-slice_fusion.1
  77.0 5.9 %pad_maximum_fusion.tile_ref = f32[50,64,640]{2,1,0:T(8,128)} fusion(f32[50,64,8]{2,1,0:T(8,128)S(1)} %copy-done.2, f32[50,64,8]{2,1,0:T(8,128)S(1)} %copy-done.3, f32[50,64,512]{2,1,0:T(8,128)} %broadcast_dynamic-update-slice_fusion.1, f32[640]{0:T(1024)S(1)} %pad.56.clone), kind=kLoop, calls=%fused_computation | loop fusion | flops 6144000 | bytes 14952960 | tf_op jit(solution)/shard_map/concatenate | solution.py:146
  82.9 19.9 %shard_map.95 = f32[6,32,512]{2,1,0:T(8,128)} custom-call(f32[288]{0:T(512)S(1)} %reshape.29.flux_ref, f32[2]{0:T(128)S(1)} %pad_maximum_fusion.8.link_ref, f32[50,64,640]{2,1,0:T(8,128)} %pad_maximum_fusion.tile_ref), custom_call_target="tpu_custom_call" | custom-call | tf_op jit(solution)/shard_map/pallas_call | solution.py:92
  102.8 1.1 multiply_reduce_fusion
  104.1 10.3 %all_to_all.18 = f32[3,32,512]{2,0,1:T(4,128)S(1)} all-to-all(f32[3,32,512]{2,0,1:T(4,128)S(1)} %bitcast.34), channel_id=1, replica_groups=mesh['blk'=192,'sub'=4] {'sub'}, dimensions={1} | all-to-all | bytes 393216 | tf_op jit(solution)/shard_map/all_to_all | solution.py:153
  114.4 9.2 %collective-permute-start.8 = (f32[4,8,2048]{2,1,0:T(8,128)S(1)}, f32[4,8,2048]{2,1,0:T(8,128)S(1)}, u32[]{:S(2)}, u32[]{:S(2)}) collective-permute-start(f32[4,8,2048]{2,1,0:T(8,128)S(1)} %pad_maximum_fusion.3), channel_id=1, source_target_pairs={{1,0},{2,1},{3,2},{4,3},{5,4},{6,5},{7,6},{8,7},{9,8},{10,9},{11,1... | collective-permute-start | bytes 786440 | tf_op jit(solution)/shard_map/ppermute | solution.py:162
  123.6 2.1 %collective-permute-start.9 = (f32[4,8,2048]{2,1,0:T(8,128)S(1)}, f32[4,8,2048]{2,1,0:T(8,128)S(1)}, u32[]{:S(2)}, u32[]{:S(2)}) collective-permute-start(f32[4,8,2048]{2,1,0:T(8,128)S(1)} %pad_maximum_fusion.3), channel_id=1, source_target_pairs={{0,1},{1,2},{2,3},{3,4},{4,5},{5,6},{6,7},{7,8},{8,9},{9,10},{10,1... | collective-permute-start | bytes 786440 | tf_op jit(solution)/shard_map/ppermute | solution.py:161
  125.8 1.2 collective-permute-done.8
  126.9 5.6 %collective-permute-done.9 = f32[4,8,2048]{2,1,0:T(8,128)S(1)} collective-permute-done((f32[4,8,2048]{2,1,0:T(8,128)S(1)}, f32[4,8,2048]{2,1,0:T(8,128)S(1)}, u32[]{:S(2)}, u32[]{:S(2)}) %collective-permute-start.9) | collective-permute-done | bytes 262176 | tf_op jit(solution)/shard_map/ppermute | solution.py:161
  132.8 0.2 fusion.56
  133.4 0.4 fusion.5
  134.2 0.4 fusion.11
  135.1 0.4 fusion.17
  135.9 0.4 fusion.23
  136.8 0.4 fusion.29
  137.3 0.2 fusion.39
  137.6 0.8 slice_add_fusion
  (65 shorter events, 3.1 us)
Async XLA Ops:
  3.8 33.6 %collective-permute-start.2 = (f32[50,8,8]{2,1,0:T(8,128)}, f32[50,8,8]{2,1,0:T(8,128)}, u32[]{:S(2)}, u32[]{:S(2)}) collective-permute-start(f32[50,8,8]{2,1,0:T(8,128)} %get-tuple-element.10), channel_id=1, source_target_pairs={{0,7},{1,4},{2,5},{3,6},{4,11},{5,8},{6,9},{7,10},{8,15},{9,12},{1... | collective-permute-start | bytes 38408 | tf_op jit(solution)/shard_map/ppermute | solution.py:128
  12.1 23.2 %copy-start.8 = (s32[192]{0:T(256)S(1)}, s32[192]{0:T(256)}, u32[]{:S(2)}) copy-start(s32[192]{0:T(256)} %param.12) | copy-start | bytes 2308
  12.1 25.1 %copy-start.7 = (f32[8,6,6]{2,0,1:T(8,128)S(1)}, f32[8,6,6]{2,0,1:T(8,128)}, u32[]{:S(2)}) copy-start(f32[8,6,6]{2,0,1:T(8,128)} %param.11) | copy-start | bytes 3460
  14.4 38.3 %collective-permute-start.3 = (f32[50,8,32]{0,2,1:T(8,128)}, f32[50,8,32]{0,2,1:T(8,128)}, u32[]{:S(2)}, u32[]{:S(2)}) collective-permute-start(f32[50,8,32]{0,2,1:T(8,128)} %copy.24), channel_id=1, source_target_pairs={{0,3},{1,0},{2,1},{3,2},{4,7},{5,4},{6,5},{7,6},{8,11},{9,8},{10,9... | collective-permute-start | bytes 153608 | tf_op jit(solution)/shard_map/ppermute | solution.py:128
  16.9 47.9 %collective-permute-start.4 = (f32[50,8,8]{2,1,0:T(8,128)}, f32[50,8,8]{2,1,0:T(8,128)}, u32[]{:S(2)}, u32[]{:S(2)}) collective-permute-start(f32[50,8,8]{2,1,0:T(8,128)} %get-tuple-element.8), channel_id=1, source_target_pairs={{0,767},{1,764},{2,765},{3,766},{4,3},{5,0},{6,1},{7,2},{8,7},{9,4... | collective-permute-start | bytes 38408 | tf_op jit(solution)/shard_map/ppermute | solution.py:128
  18.8 30.3 %collective-permute-start.5 = (f32[50,8,8]{2,1,0:T(8,128)}, f32[50,8,8]{2,1,0:T(8,128)}, u32[]{:S(2)}, u32[]{:S(2)}) collective-permute-start(f32[50,8,8]{2,1,0:T(8,128)} %get-tuple-element.9), channel_id=1, source_target_pairs={{0,5},{1,6},{2,7},{3,4},{4,9},{5,10},{6,11},{7,8},{8,13},{9,14},{1... | collective-permute-start | bytes 38408 | tf_op jit(solution)/shard_map/ppermute | solution.py:128
  25.7 36.4 %collective-permute-start.6 = (f32[50,8,32]{0,2,1:T(8,128)}, f32[50,8,32]{0,2,1:T(8,128)}, u32[]{:S(2)}, u32[]{:S(2)}) collective-permute-start(f32[50,8,32]{0,2,1:T(8,128)} %copy.26), channel_id=1, source_target_pairs={{0,1},{1,2},{2,3},{3,0},{4,5},{5,6},{6,7},{7,4},{8,9},{9,10},{10,1... | collective-permute-start | bytes 153608 | tf_op jit(solution)/shard_map/ppermute | solution.py:128
  37.4 29.8 %collective-permute-start.7 = (f32[50,8,8]{2,1,0:T(8,128)S(1)}, f32[50,8,8]{2,1,0:T(8,128)}, u32[]{:S(2)}, u32[]{:S(2)}) collective-permute-start(f32[50,8,8]{2,1,0:T(8,128)S(1)} %get-tuple-element.11), channel_id=1, source_target_pairs={{0,765},{1,766},{2,767},{3,764},{4,1},{5,2},{6,3},{7,0},{8,5},{9,6... | collective-permute-start | bytes 38408 | tf_op jit(solution)/shard_map/ppermute | solution.py:128
  49.2 20.4 %collective-permute-start = (f32[50,8,512]{2,1,0:T(8,128)}, f32[50,8,512]{2,1,0:T(8,128)}, u32[]{:S(2)}, u32[]{:S(2)}) collective-permute-start(f32[50,8,512]{2,1,0:T(8,128)} %get-tuple-element.7), channel_id=1, source_target_pairs={{0,4},{1,5},{2,6},{3,7},{4,8},{5,9},{6,10},{7,11},{8,12},{9,13},{1... | collective-permute-start | bytes 2457608 | tf_op jit(solution)/shard_map/ppermute | solution.py:128
  52.8 21.0 %collective-permute-start.1 = (f32[50,8,512]{2,1,0:T(8,128)}, f32[50,8,512]{2,1,0:T(8,128)}, u32[]{:S(2)}, u32[]{:S(2)}) collective-permute-start(f32[50,8,512]{2,1,0:T(8,128)} %get-tuple-element.6), channel_id=1, source_target_pairs={{0,764},{1,765},{2,766},{3,767},{4,0},{5,1},{6,2},{7,3},{8,4},{9,5... | collective-permute-start | bytes 2457608 | tf_op jit(solution)/shard_map/ppermute | solution.py:128
  61.1 10.6 %copy-start = (f32[6,6,32,512]{3,2,1,0:T(8,128)S(1)}, f32[6,6,32,512]{3,2,1,0:T(8,128)}, u32[]{:S(2)}) copy-start(f32[6,6,32,512]{3,2,1,0:T(8,128)} %param.9) | copy-start | bytes 7077892
  63.8 7.9 %copy-start.1 = (f32[8,32,512]{2,1,0:T(8,128)S(1)}, f32[8,32,512]{2,1,0:T(8,128)}, u32[]{:S(2)}) copy-start(f32[8,32,512]{2,1,0:T(8,128)} %param.10) | copy-start | bytes 1572868
  63.8 7.9 %copy-start.4 = (f32[6,32,512]{2,1,0:T(8,128)S(1)}, f32[6,32,512]{2,1,0:T(8,128)}, u32[]{:S(2)}) copy-start(f32[6,32,512]{2,1,0:T(8,128)} %param.8) | copy-start | bytes 1179652
  71.7 5.3 %copy-start.2 = (f32[50,64,8]{2,1,0:T(8,128)S(1)}, f32[50,64,8]{2,1,0:T(8,128)}, u32[]{:S(2)}) copy-start(f32[50,64,8]{2,1,0:T(8,128)} %broadcast_dynamic-update-slice_fusion.4) | copy-start | bytes 307204
  71.7 5.3 %copy-start.3 = (f32[50,64,8]{2,1,0:T(8,128)S(1)}, f32[50,64,8]{2,1,0:T(8,128)}, u32[]{:S(2)}) copy-start(f32[50,64,8]{2,1,0:T(8,128)} %broadcast_dynamic-update-slice_fusion.5) | copy-start | bytes 307204
  82.9 19.9 %copy-start.5 = (bf16[3,6,32,512]{3,2,1,0:T(8,128)(2,1)S(1)}, bf16[3,6,32,512]{3,2,1,0:T(8,128)(2,1)}, u32[]{:S(2)}) copy-start(bf16[3,6,32,512]{3,2,1,0:T(8,128)(2,1)} %param.13) | copy-start | bytes 1769476
  82.9 31.5 %copy-start.6 = (f32[8,2048]{1,0:T(8,128)S(1)}, f32[8,2048]{1,0:T(8,128)}, u32[]{:S(2)}) copy-start(f32[8,2048]{1,0:T(8,128)} %param.14) | copy-start | bytes 196612
  82.9 42.8 %copy-start.9 = (s32[24]{0:T(128)S(1)}, s32[24]{0:T(128)}, u32[]{:S(2)}) copy-start(s32[24]{0:T(128)} %constant.42.clone) | copy-start | bytes 292
  114.4 12.5 %collective-permute-start.8 = (f32[4,8,2048]{2,1,0:T(8,128)S(1)}, f32[4,8,2048]{2,1,0:T(8,128)S(1)}, u32[]{:S(2)}, u32[]{:S(2)}) collective-permute-start(f32[4,8,2048]{2,1,0:T(8,128)S(1)} %pad_maximum_fusion.3), channel_id=1, source_target_pairs={{1,0},{2,1},{3,2},{4,3},{5,4},{6,5},{7,6},{8,7},{9,8},{10,9},{11,1... | collective-permute-start | bytes 786440 | tf_op jit(solution)/shard_map/ppermute | solution.py:162
  123.6 8.9 %collective-permute-start.9 = (f32[4,8,2048]{2,1,0:T(8,128)S(1)}, f32[4,8,2048]{2,1,0:T(8,128)S(1)}, u32[]{:S(2)}, u32[]{:S(2)}) collective-permute-start(f32[4,8,2048]{2,1,0:T(8,128)S(1)} %pad_maximum_fusion.3), channel_id=1, source_target_pairs={{0,1},{1,2},{2,3},{3,4},{4,5},{5,6},{6,7},{7,8},{8,9},{9,10},{10,1... | collective-permute-start | bytes 786440 | tf_op jit(solution)/shard_map/ppermute | solution.py:161

commit v2 on v0

--- a/solution.py
+++ b/solution.py
@@ -1,3 +1,4 @@
+import functools
 import numpy as np
 import jax
 import jax.numpy as jnp
@@ -146,24 +147,51 @@
     forward, backward = ring_pairs(part_count, False)
     part_below = lax.ppermute(both, part_axis, forward)
     part_above = lax.ppermute(both, part_axis, backward)
-    both_x = jnp.concatenate([both, part_above, part_below], axis=1)
-    local_rows = np.arange(3 * warp_rows)
-    local_rows = np.where(local_rows < 2 * warp_rows, local_rows, local_rows - 3 * warp_rows)
-    global_rows = part_index * warp_rows + jnp.asarray(local_rows, jnp.int32)
-    valid = ((global_rows >= 0) & (global_rows < part_count * warp_rows))[:, None]
-    sens_x = both_x[:-1]
-    stiff_x = jnp.where(valid, both_x[-1], 1.0)
-    root_stiff = jnp.sqrt(stiff_x)
-    base_term = sens_x / stiff_x[None]
+    warp_adjoint = warp_sweeps(part_index.reshape(1), both, part_above, part_below, part_count)
+    return (adjoint, warp_adjoint)
+
+
+def warp_kernel(part_count, index_ref, mid_ref, above_ref, below_ref, out_ref):
+    ncomp = out_ref.shape[0]
+    warp_rows = out_ref.shape[1]
+    cols = out_ref.shape[2]
+    tall_rows = 3 * warp_rows
+    rows = lax.broadcasted_iota(jnp.int32, (tall_rows, cols), 0)
+    local_rows = jnp.where(rows < 2 * warp_rows, rows, rows - tall_rows)
+    global_rows = index_ref[0] * warp_rows + local_rows
+    valid = (global_rows >= 0) & (global_rows < part_count * warp_rows)
+
+    def field(c):
+        return jnp.concatenate([mid_ref[c], above_ref[c], below_ref[c]], axis=0)
+
+    stiff = jnp.where(valid, field(ncomp), 1.0)
+    root_stiff = jnp.sqrt(stiff)
     scale_term = couple_factor / root_stiff
-    warp_adjoint = jnp.zeros_like(base_term)
+    base_term = [field(c) / stiff for c in range(ncomp)]
+    warp = [jnp.zeros((tall_rows, cols), jnp.float32) for c in range(ncomp)]
     for sweep_index in range(SWEEPS):
-        spread = jnp.where(valid[None], root_stiff[None] * warp_adjoint, 0.0)
-        beside_all = (
-            jnp.roll(spread, 1, 1) + jnp.roll(spread, -1, 1) + jnp.roll(spread, 1, 2) + jnp.roll(spread, -1, 2)
-        )
-        warp_adjoint = base_term + scale_term[None] * beside_all
-    return (adjoint, warp_adjoint[:, :warp_rows])
+        for c in range(ncomp):
+            spread = jnp.where(valid, root_stiff * warp[c], 0.0)
+            beside_all = (
+                pltpu.roll(spread, 1, 0)
+                + pltpu.roll(spread, tall_rows - 1, 0)
+                + pltpu.roll(spread, 1, 1)
+                + pltpu.roll(spread, cols - 1, 1)
+            )
+            warp[c] = base_term[c] + scale_term * beside_all
+    for c in range(ncomp):
+        out_ref[c] = warp[c][:warp_rows]
+
+
+def warp_sweeps(index, mid, above, below, part_count):
+    ncomp = mid.shape[0] - 1
+    return pl.pallas_call(
+        functools.partial(warp_kernel, part_count),
+        out_shape=jax.ShapeDtypeStruct((ncomp,) + mid.shape[1:], jnp.float32),
+        in_specs=[pl.BlockSpec(memory_space=pltpu.SMEM)]
+        + [pl.BlockSpec(memory_space=pltpu.VMEM)] * 3,
+        out_specs=pl.BlockSpec(memory_space=pltpu.VMEM),
+    )(index, mid, above, below)
 
 
 def solution(mesh):

time: 109 us -> 108 us (level)
  Pallas kernels: 19.9 us -> 23.6 us
  other arithmetic: 12.8 us -> 9.71 us
  local copies, waits for them, and re-layouts: 13.2 us -> 11.2 us
    pallas_call x0 -> x1, Pallas kernels: none -> 3.76 us  [warp_sweeps(): pl.pallas_call(functools.partial(warp_kernel, part_count), out_shape=jax....]
    slice x25 -> x0, local copies, waits for them, and re-layouts: 2.6 us -> none  [the longest x10 1.49 us: local(): jnp.roll(spread, -1, 2)]
    select_n x6 -> x0, other arithmetic: 2.01 us -> none  [local(): spread = jnp.where(valid[None], root_stiff[None] * warp_adjoint, 0.0)]
    unnamed x22 -> x26, local copies, waits for them, and re-layouts: 4.66 us -> 5.39 us
where the time goes in v2:
time: 108 us; the launch traced here: 107 us
  starting transfers between devices  39.9 us (37%)
  Pallas kernels  23.6 us (22%)
  waiting for transfers between devices  12.6 us (12%)
  local copies, waits for them, and re-layouts  11.2 us (10%)
  other arithmetic  9.71 us (9%)
  blocking collectives  7.92 us (7%)
  between operations  2.24 us (2%)
    pallas_call x1, Pallas kernels, flow_iterations(): pl.pallas_call(flow_kernel, out_shape=jax.ShapeDtypeStruct((nf, rows_here...  19.9 us
    ppermute x1, starting transfers between devices, local(): part_above = lax.ppermute(both, part_axis, backward)  17.2 us
    ppermute x1, starting transfers between devices, local(): from_above = lax.ppermute(stack[:, :deep], 'blk', backward)  9.75 us
    all_to_all x1, blocking collectives, local(): lax.all_to_all(sensitivity, 'sub', split_axis=1, concat_axis=2, tiled=True)  7.92 us
    concatenate x1, other arithmetic, local(): jnp.concatenate([tall, jnp.swapaxes(from_right, 1, 2), gap, jnp.swapaxes(...  5.89 us
    ppermute x1, waiting for transfers between devices, local(): part_below = lax.ppermute(both, part_axis, forward)  5.6 us
    unnamed x26, local copies, waits for them, and re-layouts  5.39 us
    ppermute x1, waiting for transfers between devices, local(): lax.ppermute(jnp.swapaxes(tall[:, :, cols_here - deep:], 1, 2), 'sub', fo...  5.1 us
  transfers between devices with their start and end apart: 6, of which 5 were waited for; matrix products, arithmetic and copies ran while one was open for 3% of the time, Pallas kernels for 0%

profile of v2, /device:TPU:1, one launch (start us, length us, event | category | flops | bytes accessed | tf_op | source)
XLA Modules:
  0.0 107.3 jit_solution(15132271651747797999)
XLA Ops:
  0.6 2.3 %pad_maximum_fusion.1 = f32[50,32,512]{2,1,0:T(8,128)S(1)} fusion(f32[8,32,512]{2,1,0:T(8,128)} %param.9, f32[36,32,512]{2,1,0:T(8,128)} %bitcast.19, f32[6,32,512]{2,1,0:T(8,128)} %param.7), kind=kLoop, calls=%fused_computation.1 | loop fusion | flops 1638400 | bytes 6553600 | tf_op jit(solution)/shard_map/concatenate | solution.py:118
  2.9 0.0 copy-start.10
  2.9 0.0 copy-start.9
  2.9 0.0 copy-start.1
  2.9 0.0 copy-start.2
  2.9 0.0 copy-start.3
  3.0 1.3 %fusion = (f32[50,8,512]{2,1,0:T(8,128)}, f32[50,8,512]{2,1,0:T(8,128)}) fusion(f32[50,32,512]{2,1,0:T(8,128)S(1)} %pad_maximum_fusion.1), kind=kLoop, calls=%fused_computation.13 | loop fusion | bytes 3276800 | tf_op jit(solution)/shard_map/slice | solution.py:123
  4.3 4.7 %collective-permute-start = (f32[50,8,512]{2,1,0:T(8,128)}, f32[50,8,512]{2,1,0:T(8,128)}, u32[]{:S(2)}, u32[]{:S(2)}) collective-permute-start(f32[50,8,512]{2,1,0:T(8,128)} %get-tuple-element.5), channel_id=1, source_target_pairs={{0,4},{4,8},{8,12},{12,16},{16,20},{20,24},{24,28},{28,32},{32,36}... | collective-permute-start | bytes 2457608 | tf_op jit(solution)/shard_map/ppermute | solution.py:122
  9.0 9.8 %collective-permute-start.1 = (f32[50,8,512]{2,1,0:T(8,128)}, f32[50,8,512]{2,1,0:T(8,128)}, u32[]{:S(2)}, u32[]{:S(2)}) collective-permute-start(f32[50,8,512]{2,1,0:T(8,128)} %get-tuple-element.4), channel_id=1, source_target_pairs={{4,0},{8,4},{12,8},{16,12},{20,16},{24,20},{28,24},{32,28},{36,32}... | collective-permute-start | bytes 2457608 | tf_op jit(solution)/shard_map/ppermute | solution.py:123
  18.8 0.0 copy-done.10
  18.8 0.6 fusion.1
  20.7 0.0 copy-done.9
  20.7 0.1 reshape.17.flux_ref
  20.9 0.1 pad.4.clone
  20.9 0.1 broadcast_dynamic-update-slice_fusion
  21.0 0.0 collective-permute-done
  21.0 1.2 %constant_dynamic-update-slice_fusion.2 = f32[50,64,512]{2,1,0:T(8,128)S(1)} fusion(f32[50,64,512]{2,1,0:T(8,128)S(1)} %broadcast_dynamic-update-slice_fusion, f32[50,8,512]{2,1,0:T(8,128)} %collective-permute-done), kind=kLoop, calls=%fused_computation.11 | loop fusion | bytes 1638400
  22.2 0.0 copy-done.1
  22.3 0.0 copy-done.2
  22.3 0.3 constant_dynamic-update-slice_fusion.1
  22.6 0.4 collective-permute-done.1
  23.0 1.2 %constant_dynamic-update-slice_fusion = f32[50,64,512]{2,1,0:T(8,128)S(1)} fusion(f32[50,64,512]{2,1,0:T(8,128)S(1)} %constant_dynamic-update-slice_fusion.1, f32[50,8,512]{2,1,0:T(8,128)} %collective-permute-done.1), kind=kLoop, calls=%fused_computation.9 | loop fusion | bytes 1638400
  24.2 0.1 broadcast_dynamic-update-slice_fusion.1
  24.3 0.6 slice_bitcast_fusion.1
  24.9 2.1 %copy-done = f32[50,64,512]{2,1,0:T(8,128)} copy-done((f32[50,64,512]{2,1,0:T(8,128)}, f32[50,64,512]{2,1,0:T(8,128)S(1)}, u32[]{:S(2)}) %copy-start) | copy-done | bytes 6553624
  27.1 0.5 copy.11
  27.5 4.4 %collective-permute-start.2 = (f32[50,8,64]{2,1,0:T(8,128)S(1)}, f32[50,8,64]{2,1,0:T(8,128)S(1)}, u32[]{:S(2)}, u32[]{:S(2)}) collective-permute-start(f32[50,8,64]{2,1,0:T(8,128)S(1)} %copy.11), channel_id=1, source_target_pairs={{1,0},{2,1},{3,2},{0,3},{5,4},{6,5},{7,6},{4,7},{9,8},{10,9},{11,1... | collective-permute-start | bytes 307208 | tf_op jit(solution)/shard_map/ppermute | solution.py:129
  31.9 0.5 copy.13
  32.4 1.9 %collective-permute-start.3 = (f32[50,8,64]{2,1,0:T(8,128)S(1)}, f32[50,8,64]{2,1,0:T(8,128)}, u32[]{:S(2)}, u32[]{:S(2)}) collective-permute-start(f32[50,8,64]{2,1,0:T(8,128)S(1)} %copy.13), channel_id=1, source_target_pairs={{0,1},{1,2},{2,3},{3,0},{4,5},{5,6},{6,7},{7,4},{8,9},{9,10},{10,1... | collective-permute-start | bytes 307208 | tf_op jit(solution)/shard_map/ppermute | solution.py:128
  34.3 0.1 pad_maximum_fusion.3.link_ref
  34.4 0.2 collective-permute-done.2
  34.6 0.5 copy.12
  35.1 5.1 %collective-permute-done.3 = f32[50,8,64]{2,1,0:T(8,128)} collective-permute-done((f32[50,8,64]{2,1,0:T(8,128)S(1)}, f32[50,8,64]{2,1,0:T(8,128)}, u32[]{:S(2)}, u32[]{:S(2)}) %collective-permute-start.3) | collective-permute-done | bytes 102432 | tf_op jit(solution)/shard_map/ppermute | solution.py:128
  40.2 1.4 %copy.14 = f32[50,8,64]{1,2,0:T(8,128)S(1)} copy(f32[50,8,64]{2,1,0:T(8,128)} %collective-permute-done.3) | data formatting | bytes 204800 | tf_op jit(solution)/shard_map/ppermute | solution.py:128
  41.6 5.9 %pad_maximum_fusion.tile_ref = f32[50,64,640]{2,1,0:T(8,128)} fusion(f32[50,64,8]{2,1,0:T(8,128)S(1)} %bitcast.22, f32[50,64,8]{2,1,0:T(8,128)S(1)} %bitcast.21, f32[50,64,512]{2,1,0:T(8,128)} %copy-done, f32[640]{0:T(1024)S(1)} %pad.4.clone), kind=kLoop, calls=%fused_computation | loop fusion | flops 6144000 | bytes 14952960 | tf_op jit(solution)/shard_map/concatenate | solution.py:131
  47.5 19.9 %shard_map.86 = f32[6,32,512]{2,1,0:T(8,128)} custom-call(f32[288]{0:T(512)S(1)} %reshape.17.flux_ref, f32[2]{0:T(128)S(1)} %pad_maximum_fusion.3.link_ref, f32[50,64,640]{2,1,0:T(8,128)} %pad_maximum_fusion.tile_ref), custom_call_target="tpu_custom_call" | custom-call | tf_op jit(solution)/shard_map/pallas_call | solution.py:93
  67.4 1.1 %multiply_reduce_fusion = f32[32,512,3]{1,0,2:T(8,128)S(1)} fusion(f32[32,512,6]{1,0,2:T(8,128)} %bitcast.23, bf16[3,6,32,512]{3,2,1,0:T(8,128)(2,1)S(1)} %copy-done.5), kind=kLoop, calls=%fused_computation.4 | loop fusion | flops 835584 | bytes 1179648
  68.5 0.1 copy.26
  68.7 7.9 %all_to_all.18 = f32[3,32,512]{2,0,1:T(4,128)S(1)} all-to-all(f32[3,32,512]{2,0,1:T(4,128)S(1)} %bitcast.24), channel_id=1, replica_groups=mesh['blk'=192,'sub'=4] {'sub'}, dimensions={1} | all-to-all | bytes 393216 | tf_op jit(solution)/shard_map/all_to_all | solution.py:140
  76.6 0.1 copy.15
  76.7 0.0 copy-done.8
  76.7 17.2 %collective-permute-start.4 = (f32[4,8,2048]{2,1,0:T(8,128)S(1)}, f32[4,8,2048]{2,1,0:T(8,128)S(1)}, u32[]{:S(2)}, u32[]{:S(2)}) collective-permute-start(f32[4,8,2048]{2,1,0:T(8,128)S(1)} %pad_maximum_fusion.2.mid_ref), channel_id=1, source_target_pairs={{1,0},{2,1},{3,2},{4,3},{5,4},{6,5},{7,6},{8,7},{9,8},{10,9},{11,1... | collective-permute-start | bytes 786440 | tf_op jit(solution)/shard_map/ppermute | solution.py:149
  94.0 1.9 %collective-permute-start.5 = (f32[4,8,2048]{2,1,0:T(8,128)S(1)}, f32[4,8,2048]{2,1,0:T(8,128)S(1)}, u32[]{:S(2)}, u32[]{:S(2)}) collective-permute-start(f32[4,8,2048]{2,1,0:T(8,128)S(1)} %pad_maximum_fusion.2.mid_ref), channel_id=1, source_target_pairs={{0,1},{1,2},{2,3},{3,4},{4,5},{5,6},{6,7},{7,8},{8,9},{9,10},{10,1... | collective-permute-start | bytes 786440 | tf_op jit(solution)/shard_map/ppermute | solution.py:148
  95.9 1.4 %collective-permute-done.4.above_ref = f32[4,8,2048]{2,1,0:T(8,128)S(1)} collective-permute-done((f32[4,8,2048]{2,1,0:T(8,128)S(1)}, f32[4,8,2048]{2,1,0:T(8,128)S(1)}, u32[]{:S(2)}, u32[]{:S(2)}) %collective-permute-start.4) | collective-permute-done | bytes 262176 | tf_op jit(solution)/shard_map/ppermute | solution.py:149
  97.3 5.6 %collective-permute-done.5.below_ref = f32[4,8,2048]{2,1,0:T(8,128)S(1)} collective-permute-done((f32[4,8,2048]{2,1,0:T(8,128)S(1)}, f32[4,8,2048]{2,1,0:T(8,128)S(1)}, u32[]{:S(2)}, u32[]{:S(2)}) %collective-permute-start.5) | collective-permute-done | bytes 262176 | tf_op jit(solution)/shard_map/ppermute | solution.py:148
  102.9 0.0 copy-done.6
  102.9 0.7 copy-done.7
  103.6 3.8 %shard_map.87 = f32[3,8,2048]{2,1,0:T(8,128)} custom-call(s32[1]{0:T(128)} %bitcast.7.index_ref, f32[4,8,2048]{2,1,0:T(8,128)} %copy-done.4, f32[4,8,2048]{2,1,0:T(8,128)} %copy-done.6, f32[4,8,2048]{2,1,0:T(8,128)} %copy-done.7), custom_call_target="tpu_custom_call" | custom-call | tf_op jit(solution)/shard_map/pallas_call | solution.py:188
  (12 shorter events, 0.1 us)
Async XLA Ops:
  2.9 15.9 %copy-start.10 = (s32[192]{0:T(256)S(1)}, s32[192]{0:T(256)}, u32[]{:S(2)}) copy-start(s32[192]{0:T(256)} %param.11) | copy-start | bytes 2308
  2.9 17.8 %copy-start.9 = (f32[8,6,6]{2,0,1:T(8,128)S(1)}, f32[8,6,6]{2,0,1:T(8,128)}, u32[]{:S(2)}) copy-start(f32[8,6,6]{2,0,1:T(8,128)} %param.10) | copy-start | bytes 3460
  2.9 19.3 %copy-start.1 = (f32[6,6,32,512]{3,2,1,0:T(8,128)S(1)}, f32[6,6,32,512]{3,2,1,0:T(8,128)}, u32[]{:S(2)}) copy-start(f32[6,6,32,512]{3,2,1,0:T(8,128)} %param.8) | copy-start | bytes 7077892
  2.9 19.3 %copy-start.2 = (f32[8,32,512]{2,1,0:T(8,128)S(1)}, f32[8,32,512]{2,1,0:T(8,128)}, u32[]{:S(2)}) copy-start(f32[8,32,512]{2,1,0:T(8,128)} %param.9) | copy-start | bytes 1572868
  2.9 19.3 %copy-start.3 = (f32[6,32,512]{2,1,0:T(8,128)S(1)}, f32[6,32,512]{2,1,0:T(8,128)}, u32[]{:S(2)}) copy-start(f32[6,32,512]{2,1,0:T(8,128)} %param.7) | copy-start | bytes 1179652
  4.3 16.7 %collective-permute-start = (f32[50,8,512]{2,1,0:T(8,128)}, f32[50,8,512]{2,1,0:T(8,128)}, u32[]{:S(2)}, u32[]{:S(2)}) collective-permute-start(f32[50,8,512]{2,1,0:T(8,128)} %get-tuple-element.5), channel_id=1, source_target_pairs={{0,4},{4,8},{8,12},{12,16},{16,20},{20,24},{24,28},{28,32},{32,36}... | collective-permute-start | bytes 2457608 | tf_op jit(solution)/shard_map/ppermute | solution.py:122
  9.0 14.0 %collective-permute-start.1 = (f32[50,8,512]{2,1,0:T(8,128)}, f32[50,8,512]{2,1,0:T(8,128)}, u32[]{:S(2)}, u32[]{:S(2)}) collective-permute-start(f32[50,8,512]{2,1,0:T(8,128)} %get-tuple-element.4), channel_id=1, source_target_pairs={{4,0},{8,4},{12,8},{16,12},{20,16},{24,20},{28,24},{32,28},{36,32}... | collective-permute-start | bytes 2457608 | tf_op jit(solution)/shard_map/ppermute | solution.py:123
  24.3 2.8 %copy-start = (f32[50,64,512]{2,1,0:T(8,128)}, f32[50,64,512]{2,1,0:T(8,128)S(1)}, u32[]{:S(2)}) copy-start(f32[50,64,512]{2,1,0:T(8,128)S(1)} %broadcast_dynamic-update-slice_fusion.1) | copy-start | bytes 19660804
  27.5 7.1 %collective-permute-start.2 = (f32[50,8,64]{2,1,0:T(8,128)S(1)}, f32[50,8,64]{2,1,0:T(8,128)S(1)}, u32[]{:S(2)}, u32[]{:S(2)}) collective-permute-start(f32[50,8,64]{2,1,0:T(8,128)S(1)} %copy.11), channel_id=1, source_target_pairs={{1,0},{2,1},{3,2},{0,3},{5,4},{6,5},{7,6},{4,7},{9,8},{10,9},{11,1... | collective-permute-start | bytes 307208 | tf_op jit(solution)/shard_map/ppermute | solution.py:129
  32.4 7.8 %collective-permute-start.3 = (f32[50,8,64]{2,1,0:T(8,128)S(1)}, f32[50,8,64]{2,1,0:T(8,128)}, u32[]{:S(2)}, u32[]{:S(2)}) collective-permute-start(f32[50,8,64]{2,1,0:T(8,128)S(1)} %copy.13), channel_id=1, source_target_pairs={{0,1},{1,2},{2,3},{3,0},{4,5},{5,6},{6,7},{7,4},{8,9},{9,10},{10,1... | collective-permute-start | bytes 307208 | tf_op jit(solution)/shard_map/ppermute | solution.py:128
  47.5 19.9 %copy-start.5 = (bf16[3,6,32,512]{3,2,1,0:T(8,128)(2,1)S(1)}, bf16[3,6,32,512]{3,2,1,0:T(8,128)(2,1)}, u32[]{:S(2)}) copy-start(bf16[3,6,32,512]{3,2,1,0:T(8,128)(2,1)} %param.12) | copy-start | bytes 1769476
  47.5 29.2 %copy-start.8 = (f32[8,2048]{1,0:T(8,128)S(1)}, f32[8,2048]{1,0:T(8,128)}, u32[]{:S(2)}) copy-start(f32[8,2048]{1,0:T(8,128)} %param.13) | copy-start | bytes 196612
  76.7 26.1 %copy-start.4 = (f32[4,8,2048]{2,1,0:T(8,128)}, f32[4,8,2048]{2,1,0:T(8,128)S(1)}, u32[]{:S(2)}) copy-start(f32[4,8,2048]{2,1,0:T(8,128)S(1)} %pad_maximum_fusion.2.mid_ref) | copy-start | bytes 786436
  76.7 20.5 %collective-permute-start.4 = (f32[4,8,2048]{2,1,0:T(8,128)S(1)}, f32[4,8,2048]{2,1,0:T(8,128)S(1)}, u32[]{:S(2)}, u32[]{:S(2)}) collective-permute-start(f32[4,8,2048]{2,1,0:T(8,128)S(1)} %pad_maximum_fusion.2.mid_ref), channel_id=1, source_target_pairs={{1,0},{2,1},{3,2},{4,3},{5,4},{6,5},{7,6},{8,7},{9,8},{10,9},{11,1... | collective-permute-start | bytes 786440 | tf_op jit(solution)/shard_map/ppermute | solution.py:149
  94.0 8.9 %collective-permute-start.5 = (f32[4,8,2048]{2,1,0:T(8,128)S(1)}, f32[4,8,2048]{2,1,0:T(8,128)S(1)}, u32[]{:S(2)}, u32[]{:S(2)}) collective-permute-start(f32[4,8,2048]{2,1,0:T(8,128)S(1)} %pad_maximum_fusion.2.mid_ref), channel_id=1, source_target_pairs={{0,1},{1,2},{2,3},{3,4},{4,5},{5,6},{6,7},{7,8},{8,9},{9,10},{10,1... | collective-permute-start | bytes 786440 | tf_op jit(solution)/shard_map/ppermute | solution.py:148
  97.3 5.6 %copy-start.6 = (f32[4,8,2048]{2,1,0:T(8,128)}, f32[4,8,2048]{2,1,0:T(8,128)S(1)}, u32[]{:S(2)}) copy-start(f32[4,8,2048]{2,1,0:T(8,128)S(1)} %collective-permute-done.4.above_ref) | copy-start | bytes 786436
  102.9 0.7 copy-start.7

commit v3 on v2

--- a/solution.py
+++ b/solution.py
@@ -29,15 +29,35 @@
 TILE = 8
 
 
-def flow_kernel(flux_ref, link_ref, tile_ref, out_ref, buf0, buf1):
+def flow_kernel(flux_ref, link_ref, adj_hbm, jd_hbm, fw_hbm, below_hbm, above_hbm, edge_hbm,
+                out_ref, tile_ref, buf0, buf1, sems):
     nf = out_ref.shape[0]
     rows_here = out_ref.shape[1]
     cols_here = out_ref.shape[2]
     width = tile_ref.shape[2]
     pad = 2 * TILE
+    halo = below_hbm.shape[1]
+    n_fields = tile_ref.shape[0]
     n_tiles = tile_ref.shape[1] // TILE
     jd0 = nf
     fw0 = nf + nf * nf
+    copies = [
+        pltpu.make_async_copy(adj_hbm, tile_ref.at[0:jd0, pad : pad + rows_here, 0:cols_here], sems.at[0]),
+        pltpu.make_async_copy(jd_hbm, tile_ref.at[jd0:fw0, pad : pad + rows_here, 0:cols_here], sems.at[1]),
+        pltpu.make_async_copy(fw_hbm, tile_ref.at[fw0:n_fields, pad : pad + rows_here, 0:cols_here], sems.at[2]),
+        pltpu.make_async_copy(below_hbm, tile_ref.at[:, pad - halo : pad, 0:cols_here], sems.at[3]),
+        pltpu.make_async_copy(
+            above_hbm, tile_ref.at[:, pad + rows_here : pad + rows_here + halo, 0:cols_here], sems.at[4]
+        ),
+        pltpu.make_async_copy(edge_hbm, tile_ref.at[:, :, cols_here:width], sems.at[5]),
+    ]
+    for copy in copies:
+        copy.start()
+    for copy in copies:
+        copy.wait()
+    zeros = jnp.zeros((n_fields, pad - halo, cols_here), jnp.float32)
+    tile_ref[:, 0 : pad - halo, 0:cols_here] = zeros
+    tile_ref[:, pad + rows_here + halo :, 0:cols_here] = zeros
     link_above = link_ref[0]
     link_below = link_ref[1]
     bufs = (buf0, buf1)
@@ -89,19 +109,27 @@
     out_ref[...] = final[:, pad : pad + rows_here, 0:cols_here]
 
 
-def flow_iterations(flux_flat, links, tile, nf, rows_here, cols_here):
+def flow_iterations(flux_flat, links, adj, jd, fw, below, above, edge, width):
+    nf, rows_here, cols_here = adj.shape
+    n_fields = below.shape[0]
+    tile_shape = (n_fields, rows_here + 4 * TILE, width)
     return pl.pallas_call(
         flow_kernel,
         out_shape=jax.ShapeDtypeStruct((nf, rows_here, cols_here), jnp.float32),
         in_specs=[
             pl.BlockSpec(memory_space=pltpu.SMEM),
             pl.BlockSpec(memory_space=pltpu.SMEM),
-            pl.BlockSpec(memory_space=pltpu.VMEM),
+        ]
+        + [pl.BlockSpec(memory_space=pl.ANY)] * 6,
+        out_specs=pl.BlockSpec(memory_space=pltpu.VMEM),
+        scratch_shapes=[
+            pltpu.VMEM(tile_shape, jnp.float32),
+            pltpu.VMEM((nf,) + tile_shape[1:], jnp.float32),
+            pltpu.VMEM((nf,) + tile_shape[1:], jnp.float32),
+            pltpu.SemaphoreType.DMA((6,)),
         ],
-        out_specs=pl.BlockSpec(memory_space=pltpu.VMEM),
-        scratch_shapes=[pltpu.VMEM((nf,) + tile.shape[1:], jnp.float32)] * 2,
         compiler_params=pltpu.CompilerParams(vmem_limit_bytes=48 * 1024 * 1024),
-    )(flux_flat, links, tile)
+    )(flux_flat, links, adj, jd, fw, below, above, edge)
 
 
 def local(adj_source, jac_diag, face_weights, flux_jac, face_link, node_grad, stiffness):
@@ -115,24 +143,29 @@
     deep = REACH * ITERS
     width = -(-(cols_here + 2 * deep) // LANES) * LANES
 
-    stack = jnp.concatenate(
-        [adj_source, jac_diag.reshape((nf * nf,) + jac_diag.shape[2:]), face_weights], axis=0
-    )
+    fields = [adj_source, jac_diag.reshape((nf * nf,) + jac_diag.shape[2:]), face_weights]
     forward, backward = ring_pairs(block_count, True)
-    from_below = lax.ppermute(stack[:, rows_here - deep :], "blk", forward)
-    from_above = lax.ppermute(stack[:, :deep], "blk", backward)
-    zero_rows = jnp.zeros((stack.shape[0], 2 * TILE - deep, cols_here), jnp.float32)
-    tall = jnp.concatenate([zero_rows, from_below, stack, from_above, zero_rows], axis=1)
+    from_below = lax.ppermute(
+        jnp.concatenate([x[:, rows_here - deep :] for x in fields], axis=0), "blk", forward
+    )
+    from_above = lax.ppermute(jnp.concatenate([x[:, :deep] for x in fields], axis=0), "blk", backward)
     sub_count = lax.axis_size("sub")
     forward, backward = ring_pairs(sub_count, True)
-    from_left = lax.ppermute(jnp.swapaxes(tall[:, :, cols_here - deep :], 1, 2), "sub", forward)
-    from_right = lax.ppermute(jnp.swapaxes(tall[:, :, :deep], 1, 2), "sub", backward)
-    gap = jnp.zeros(tall.shape[:2] + (width - cols_here - 2 * deep,), jnp.float32)
-    tile = jnp.concatenate(
-        [tall, jnp.swapaxes(from_right, 1, 2), gap, jnp.swapaxes(from_left, 1, 2)], axis=2
-    )
+
+    def column_strip(lo, hi):
+        middle = jnp.concatenate([x[:, :, lo:hi] for x in fields], axis=0)
+        strip = jnp.concatenate([from_below[:, :, lo:hi], middle, from_above[:, :, lo:hi]], axis=1)
+        return jnp.swapaxes(strip, 1, 2)
+
+    from_left = lax.ppermute(column_strip(cols_here - deep, cols_here), "sub", forward)
+    from_right = lax.ppermute(column_strip(0, deep), "sub", backward)
+    gap = jnp.zeros(from_left.shape[:1] + from_left.shape[2:] + (width - cols_here - 2 * deep,), jnp.float32)
+    edge = jnp.concatenate([jnp.swapaxes(from_right, 1, 2), gap, jnp.swapaxes(from_left, 1, 2)], axis=2)
+    edge = jnp.pad(edge, ((0, 0), (2 * TILE - deep, 2 * TILE - deep), (0, 0)))
     links = jnp.stack([link_above, link_below])
-    adjoint = flow_iterations(flux_jac.reshape(-1), links, tile, nf, rows_here, cols_here)
+    adjoint = flow_iterations(
+        flux_jac.reshape(-1), links, fields[0], fields[1], fields[2], from_below, from_above, edge, width
+    )
 
     sensitivity = jnp.einsum(
         "cfij,fij->cij", node_grad.astype(jnp.float32), adjoint, precision=lax.Precision.HIGHEST

time: 108 us -> 107 us (level)
  local copies, waits for them, and re-layouts: 11.2 us -> 15.1 us
  waiting for transfers between devices: 12.6 us -> 10.1 us
  other arithmetic: 9.71 us -> 8.55 us
    unnamed x26 -> x21, local copies, waits for them, and re-layouts: 5.39 us -> 0.79 us
    concatenate x2 -> x3, other arithmetic: 8.15 us -> 4 us  [the longest x1 2.04 us: local(): jnp.concatenate([jnp.swapaxes(from_right, 1, 2), gap, jnp.swapaxes(from_l...]
    slice x1 -> x8, local copies, waits for them, and re-layouts: 1.33 us -> 4.66 us  [the longest x3 2.3 us: column_strip(): middle = jnp.concatenate([x[:, :, lo:hi] for x in fields], axis=0)]
    transpose x0 -> x2, other arithmetic: none -> 3.29 us  [column_strip(): return jnp.swapaxes(strip, 1, 2)]
    transpose x3 -> x2, local copies, waits for them, and re-layouts: 1.57 us -> 4.36 us  [column_strip(): return jnp.swapaxes(strip, 1, 2)]
    ppermute x4, waiting for transfers between devices: 5.68 us -> 3.12 us  [the longest x1 3.11 us: local(): lax.ppermute(column_strip(cols_here - deep, cols_here), 'sub', forward)]
    ppermute x2, local copies, waits for them, and re-layouts: 1.92 us -> 4.08 us  [the longest x1 2.5 us: local(): from_right = lax.ppermute(column_strip(0, deep), 'sub', backward)]
  transfers between devices with their start and end apart: 6 -> 6, of which waited for: 5 -> 3; matrix products, arithmetic and copies ran while one was open for 3% -> 10% of each run, Pallas kernels for 0% -> 0%
where the time goes in v3:
time: 107 us; the launch traced here: 106 us
  starting transfers between devices  39.5 us (37%)
  Pallas kernels  22.6 us (21%)
  local copies, waits for them, and re-layouts  15.1 us (14%)
  waiting for transfers between devices  10.1 us (9%)
  other arithmetic  8.55 us (8%)
  blocking collectives  7.92 us (7%)
  between operations  2.14 us (2%)
    pallas_call x1, Pallas kernels, flow_iterations(): pl.pallas_call(flow_kernel, out_shape=jax.ShapeDtypeStruct((nf, rows_here...  18.9 us
    ppermute x1, starting transfers between devices, local(): part_above = lax.ppermute(both, part_axis, backward)  17 us
    ppermute x1, starting transfers between devices, local(): lax.ppermute(jnp.concatenate([x[:, :deep] for x in fields], axis=0), 'blk...  9.74 us
    all_to_all x1, blocking collectives, local(): lax.all_to_all(sensitivity, 'sub', split_axis=1, concat_axis=2, tiled=True)  7.92 us
    ppermute x1, waiting for transfers between devices, local(): part_below = lax.ppermute(both, part_axis, forward)  5.6 us
    ppermute x1, starting transfers between devices, local(): lax.ppermute(jnp.concatenate([x[:, rows_here - deep:] for x in fields], a...  4.71 us
    transpose x2, local copies, waits for them, and re-layouts, column_strip(): return jnp.swapaxes(strip, 1, 2)  4.36 us
    ppermute x1, starting transfers between devices, local(): from_right = lax.ppermute(column_strip(0, deep), 'sub', backward)  4.2 us
  transfers between devices with their start and end apart: 6, of which 3 were waited for; matrix products, arithmetic and copies ran while one was open for 10% of the time, Pallas kernels for 0%

profile of v3, /device:TPU:1, one launch (start us, length us, event | category | flops | bytes accessed | tf_op | source)
XLA Modules:
  0.0 106.0 jit_solution(13153338762319049551)
XLA Ops:
  0.6 0.0 copy-start
  0.6 0.0 copy-start.1
  0.6 1.4 %fusion.1 = (f32[36,8,512]{2,1,0:T(8,128)S(1)}, f32[36,8,512]{2,1,0:T(8,128)S(1)}) fusion(f32[36,32,512]{2,1,0:T(8,128)} %bitcast.19), kind=kLoop, calls=%fused_computation.10 | loop fusion | bytes 2359296 | tf_op jit(solution)/shard_map/slice | solution.py:151
  2.1 0.0 copy-done
  2.1 0.0 copy-done.1
  2.2 0.9 pad_maximum_fusion.1
  3.1 4.7 %collective-permute-start = (f32[50,8,512]{2,1,0:T(8,128)}, f32[50,8,512]{2,1,0:T(8,128)S(1)}, u32[]{:S(2)}, u32[]{:S(2)}) collective-permute-start(f32[50,8,512]{2,1,0:T(8,128)} %pad_maximum_fusion.1), channel_id=1, source_target_pairs={{0,4},{4,8},{8,12},{12,16},{16,20},{20,24},{24,28},{28,32},{32,36}... | collective-permute-start | bytes 2457608 | tf_op jit(solution)/shard_map/ppermute | solution.py:148
  7.8 1.0 pad_maximum_fusion.2
  8.8 9.7 %collective-permute-start.1 = (f32[50,8,512]{2,1,0:T(8,128)}, f32[50,8,512]{2,1,0:T(8,128)S(1)}, u32[]{:S(2)}, u32[]{:S(2)}) collective-permute-start(f32[50,8,512]{2,1,0:T(8,128)} %pad_maximum_fusion.2), channel_id=1, source_target_pairs={{4,0},{8,4},{12,8},{16,12},{20,16},{24,20},{28,24},{32,28},{36,32}... | collective-permute-start | bytes 2457608 | tf_op jit(solution)/shard_map/ppermute | solution.py:151
  18.6 0.7 fusion.6
  19.3 0.0 copy-done.9
  19.3 0.6 fusion.8
  21.2 0.0 copy-done.8
  21.2 0.1 reshape.17.flux_ref
  21.4 0.1 pad.8.clone
  21.4 0.1 fusion.4
  21.5 1.5 %fusion = (f32[36,32,8]{2,1,0:T(8,128)S(1)}, f32[36,32,8]{2,1,0:T(8,128)S(1)}) fusion(f32[36,32,512]{2,1,0:T(8,128)} %bitcast.20), kind=kLoop, calls=%fused_computation.9 | loop fusion | bytes 147456 | tf_op jit(solution)/shard_map/slice | solution.py:156
  23.0 0.0 copy-start.4
  23.0 0.0 collective-permute-done.below_hbm
  23.0 0.1 fusion.2
  23.2 0.0 collective-permute-done.1.above_hbm
  23.2 0.8 fusion.3
  24.0 1.1 %maximum_bitcast_fusion = f32[50,8,48]{1,2,0:T(8,128)} fusion(f32[50,8,8]{2,1,0:T(8,128)S(1)} %get-tuple-element.8, f32[8,32,8]{2,1,0:T(8,128)S(1)} %get-tuple-element.10, f32[36,32,8]{2,1,0:T(8,128)S(1)} %get-tuple-element.2, f32[6,32,8]{2,1,0:T(8,128)S(1)} %copy-done.4, f32[50,8,8]{2,1,0:T(8,128)S(1)} %get-tuple-element.6), kind=kLoop, calls=%fused_computation | loop fusion | flops 76800 | bytes 153600 | tf_op jit(solution)/shard_map/transpose | solution.py:158
  25.1 2.5 %copy.43 = f32[50,8,48]{0,2,1:T(8,128)} copy(f32[50,8,48]{1,2,0:T(8,128)} %maximum_bitcast_fusion) | data formatting | bytes 153600 | tf_op jit(solution)/shard_map/transpose | solution.py:158
  27.6 4.2 %collective-permute-start.2 = (f32[50,8,48]{0,2,1:T(8,128)}, f32[50,8,48]{0,2,1:T(8,128)}, u32[]{:S(2)}, u32[]{:S(2)}) collective-permute-start(f32[50,8,48]{0,2,1:T(8,128)} %copy.43), channel_id=1, source_target_pairs={{1,0},{2,1},{3,2},{0,3},{5,4},{6,5},{7,6},{4,7},{9,8},{10,9},{11,1... | collective-permute-start | bytes 230408 | tf_op jit(solution)/shard_map/ppermute | solution.py:161
  31.8 2.1 %maximum_bitcast_fusion.1 = f32[50,8,48]{1,2,0:T(8,128)} fusion(f32[50,8,8]{2,1,0:T(8,128)} %get-tuple-element.9, f32[8,32,8]{2,1,0:T(8,128)S(1)} %get-tuple-element.11, f32[36,32,8]{2,1,0:T(8,128)S(1)} %get-tuple-element.3, f32[6,32,8]{2,1,0:T(8,128)} %get-tuple-element.15, f32[50,8,8]{2,1,0:T(8,128)S(1)} %get-tuple-element.7), kind=kLoop, calls=%fused_computation.1 | loop fusion | flops 76800 | bytes 153600 | tf_op jit(solution)/shard_map/transpose | solution.py:158
  34.0 1.8 %copy.45 = f32[50,8,48]{0,2,1:T(8,128)S(1)} copy(f32[50,8,48]{1,2,0:T(8,128)} %maximum_bitcast_fusion.1) | data formatting | bytes 153600 | tf_op jit(solution)/shard_map/transpose | solution.py:158
  35.8 1.9 %collective-permute-start.3 = (f32[50,8,48]{0,2,1:T(8,128)S(1)}, f32[50,8,48]{0,2,1:T(8,128)S(1)}, u32[]{:S(2)}, u32[]{:S(2)}) collective-permute-start(f32[50,8,48]{0,2,1:T(8,128)S(1)} %copy.45), channel_id=1, source_target_pairs={{0,1},{1,2},{2,3},{3,0},{4,5},{5,6},{6,7},{7,4},{8,9},{9,10},{10,1... | collective-permute-start | bytes 230408 | tf_op jit(solution)/shard_map/ppermute | solution.py:160
  37.8 0.1 pad_maximum_fusion.4.link_ref
  37.8 0.0 collective-permute-done.2
  37.8 2.5 %copy.44 = f32[50,8,48]{1,2,0:T(8,128)} copy(f32[50,8,48]{0,2,1:T(8,128)} %collective-permute-done.2) | data formatting | bytes 153600 | tf_op jit(solution)/shard_map/ppermute | solution.py:161
  40.3 3.1 %collective-permute-done.3 = f32[50,8,48]{0,2,1:T(8,128)S(1)} collective-permute-done((f32[50,8,48]{0,2,1:T(8,128)S(1)}, f32[50,8,48]{0,2,1:T(8,128)S(1)}, u32[]{:S(2)}, u32[]{:S(2)}) %collective-permute-start.3) | collective-permute-done | bytes 76832 | tf_op jit(solution)/shard_map/ppermute | solution.py:160
  43.5 1.6 %copy.46 = f32[50,8,48]{1,2,0:T(8,128)} copy(f32[50,8,48]{0,2,1:T(8,128)S(1)} %collective-permute-done.3) | data formatting | bytes 153600 | tf_op jit(solution)/shard_map/ppermute | solution.py:160
  45.0 2.0 %pad_maximum_fusion = f32[50,48,128]{2,1,0:T(8,128)S(1)} fusion(f32[50,48,8]{2,1,0:T(8,128)} %bitcast.23, f32[50,48,8]{2,1,0:T(8,128)} %bitcast.22, f32[128]{0:T(128)S(1)} %pad.8.clone), kind=kLoop, calls=%fused_computation.2 | loop fusion | flops 614400 | bytes 1382912 | tf_op jit(solution)/shard_map/concatenate | solution.py:163
  47.1 0.2 pad.4.edge_hbm
  47.3 0.0 copy-start.3
  47.3 18.9 %shard_map.86 = f32[6,32,512]{2,1,0:T(8,128)} custom-call(f32[288]{0:T(512)S(1)} %reshape.17.flux_ref, f32[2]{0:T(128)S(1)} %pad_maximum_fusion.4.link_ref, f32[6,32,512]{2,1,0:T(8,128)S(1)} %copy-done.1, f32[36,32,512]{2,1,0:T(8,128)} %bitcast.21, f32[8,32,512]{2,1,0:T(8,128)S(1)} %copy-done, f32[50,8,512]{2,1,0:T(8,128)S(1)} %collective-permute-done.below_hbm, ...), custom_call_target="tpu_custom_call" | custom-call | tf_op jit(solution)/shard_map/pallas_call | solution.py:116
  66.2 0.0 copy-start.7
  66.2 1.2 %multiply_reduce_fusion = f32[32,512,3]{1,0,2:T(8,128)S(1)} fusion(f32[32,512,6]{1,0,2:T(8,128)} %bitcast.24, bf16[3,6,32,512]{3,2,1,0:T(8,128)(2,1)S(1)} %copy-done.3), kind=kLoop, calls=%fused_computation.3 | loop fusion | flops 835584 | bytes 1179648
  67.4 0.1 copy.58
  67.5 7.9 %all_to_all.18 = f32[3,32,512]{2,0,1:T(4,128)S(1)} all-to-all(f32[3,32,512]{2,0,1:T(4,128)S(1)} %bitcast.25), channel_id=1, replica_groups=mesh['blk'=192,'sub'=4] {'sub'}, dimensions={1} | all-to-all | bytes 393216 | tf_op jit(solution)/shard_map/all_to_all | solution.py:173
  75.5 0.1 copy.47
  75.6 17.0 %collective-permute-start.4 = (f32[4,8,2048]{2,1,0:T(8,128)S(1)}, f32[4,8,2048]{2,1,0:T(8,128)S(1)}, u32[]{:S(2)}, u32[]{:S(2)}) collective-permute-start(f32[4,8,2048]{2,1,0:T(8,128)S(1)} %pad_maximum_fusion.3.mid_ref), channel_id=1, source_target_pairs={{1,0},{2,1},{3,2},{4,3},{5,4},{6,5},{7,6},{8,7},{9,8},{10,9},{11,1... | collective-permute-start | bytes 786440 | tf_op jit(solution)/shard_map/ppermute | solution.py:182
  92.6 1.9 %collective-permute-start.5 = (f32[4,8,2048]{2,1,0:T(8,128)S(1)}, f32[4,8,2048]{2,1,0:T(8,128)S(1)}, u32[]{:S(2)}, u32[]{:S(2)}) collective-permute-start(f32[4,8,2048]{2,1,0:T(8,128)S(1)} %pad_maximum_fusion.3.mid_ref), channel_id=1, source_target_pairs={{0,1},{1,2},{2,3},{3,4},{4,5},{5,6},{6,7},{7,8},{8,9},{9,10},{10,1... | collective-permute-start | bytes 786440 | tf_op jit(solution)/shard_map/ppermute | solution.py:181
  94.5 1.4 %collective-permute-done.4.above_ref = f32[4,8,2048]{2,1,0:T(8,128)S(1)} collective-permute-done((f32[4,8,2048]{2,1,0:T(8,128)S(1)}, f32[4,8,2048]{2,1,0:T(8,128)S(1)}, u32[]{:S(2)}, u32[]{:S(2)}) %collective-permute-start.4) | collective-permute-done | bytes 262176 | tf_op jit(solution)/shard_map/ppermute | solution.py:182
  95.9 5.6 %collective-permute-done.5.below_ref = f32[4,8,2048]{2,1,0:T(8,128)S(1)} collective-permute-done((f32[4,8,2048]{2,1,0:T(8,128)S(1)}, f32[4,8,2048]{2,1,0:T(8,128)S(1)}, u32[]{:S(2)}, u32[]{:S(2)}) %collective-permute-start.5) | collective-permute-done | bytes 262176 | tf_op jit(solution)/shard_map/ppermute | solution.py:181
  101.5 0.7 copy-done.6
  102.2 3.8 %shard_map.87 = f32[3,8,2048]{2,1,0:T(8,128)} custom-call(s32[1]{0:T(128)} %bitcast.7.index_ref, f32[4,8,2048]{2,1,0:T(8,128)} %copy-done.2, f32[4,8,2048]{2,1,0:T(8,128)} %copy-done.5, f32[4,8,2048]{2,1,0:T(8,128)} %copy-done.6), custom_call_target="tpu_custom_call" | custom-call | tf_op jit(solution)/shard_map/pallas_call | solution.py:221
  (15 shorter events, 0.1 us)
Async XLA Ops:
  0.6 1.4 %copy-start = (f32[8,32,512]{2,1,0:T(8,128)S(1)}, f32[8,32,512]{2,1,0:T(8,128)}, u32[]{:S(2)}) copy-start(f32[8,32,512]{2,1,0:T(8,128)} %fw_hbm.1) | copy-start | bytes 1572868
  0.6 1.5 %copy-start.1 = (f32[6,32,512]{2,1,0:T(8,128)S(1)}, f32[6,32,512]{2,1,0:T(8,128)}, u32[]{:S(2)}) copy-start(f32[6,32,512]{2,1,0:T(8,128)} %adj_hbm.1) | copy-start | bytes 1179652
  3.1 16.2 %copy-start.9 = (s32[192]{0:T(256)S(1)}, s32[192]{0:T(256)}, u32[]{:S(2)}) copy-start(s32[192]{0:T(256)} %param.11) | copy-start | bytes 2308
  3.1 18.1 %copy-start.8 = (f32[8,6,6]{2,0,1:T(8,128)S(1)}, f32[8,6,6]{2,0,1:T(8,128)}, u32[]{:S(2)}) copy-start(f32[8,6,6]{2,0,1:T(8,128)} %param.10) | copy-start | bytes 3460
  3.1 19.9 %collective-permute-start = (f32[50,8,512]{2,1,0:T(8,128)}, f32[50,8,512]{2,1,0:T(8,128)S(1)}, u32[]{:S(2)}, u32[]{:S(2)}) collective-permute-start(f32[50,8,512]{2,1,0:T(8,128)} %pad_maximum_fusion.1), channel_id=1, source_target_pairs={{0,4},{4,8},{8,12},{12,16},{16,20},{20,24},{24,28},{28,32},{32,36}... | collective-permute-start | bytes 2457608 | tf_op jit(solution)/shard_map/ppermute | solution.py:148
  8.8 14.3 %collective-permute-start.1 = (f32[50,8,512]{2,1,0:T(8,128)}, f32[50,8,512]{2,1,0:T(8,128)S(1)}, u32[]{:S(2)}, u32[]{:S(2)}) collective-permute-start(f32[50,8,512]{2,1,0:T(8,128)} %pad_maximum_fusion.2), channel_id=1, source_target_pairs={{4,0},{8,4},{12,8},{16,12},{20,16},{24,20},{28,24},{32,28},{36,32}... | collective-permute-start | bytes 2457608 | tf_op jit(solution)/shard_map/ppermute | solution.py:151
  23.0 1.0 copy-start.4
  27.6 10.2 %collective-permute-start.2 = (f32[50,8,48]{0,2,1:T(8,128)}, f32[50,8,48]{0,2,1:T(8,128)}, u32[]{:S(2)}, u32[]{:S(2)}) collective-permute-start(f32[50,8,48]{0,2,1:T(8,128)} %copy.43), channel_id=1, source_target_pairs={{1,0},{2,1},{3,2},{0,3},{5,4},{6,5},{7,6},{4,7},{9,8},{10,9},{11,1... | collective-permute-start | bytes 230408 | tf_op jit(solution)/shard_map/ppermute | solution.py:161
  35.8 7.6 %collective-permute-start.3 = (f32[50,8,48]{0,2,1:T(8,128)S(1)}, f32[50,8,48]{0,2,1:T(8,128)S(1)}, u32[]{:S(2)}, u32[]{:S(2)}) collective-permute-start(f32[50,8,48]{0,2,1:T(8,128)S(1)} %copy.45), channel_id=1, source_target_pairs={{0,1},{1,2},{2,3},{3,0},{4,5},{5,6},{6,7},{7,4},{8,9},{9,10},{10,1... | collective-permute-start | bytes 230408 | tf_op jit(solution)/shard_map/ppermute | solution.py:160
  47.3 18.9 %copy-start.3 = (bf16[3,6,32,512]{3,2,1,0:T(8,128)(2,1)S(1)}, bf16[3,6,32,512]{3,2,1,0:T(8,128)(2,1)}, u32[]{:S(2)}) copy-start(bf16[3,6,32,512]{3,2,1,0:T(8,128)(2,1)} %param.12) | copy-start | bytes 1769476
  66.2 9.3 %copy-start.7 = (f32[8,2048]{1,0:T(8,128)S(1)}, f32[8,2048]{1,0:T(8,128)}, u32[]{:S(2)}) copy-start(f32[8,2048]{1,0:T(8,128)} %param.13) | copy-start | bytes 196612
  75.6 25.9 %copy-start.2 = (f32[4,8,2048]{2,1,0:T(8,128)}, f32[4,8,2048]{2,1,0:T(8,128)S(1)}, u32[]{:S(2)}) copy-start(f32[4,8,2048]{2,1,0:T(8,128)S(1)} %pad_maximum_fusion.3.mid_ref) | copy-start | bytes 786436
  75.6 20.3 %collective-permute-start.4 = (f32[4,8,2048]{2,1,0:T(8,128)S(1)}, f32[4,8,2048]{2,1,0:T(8,128)S(1)}, u32[]{:S(2)}, u32[]{:S(2)}) collective-permute-start(f32[4,8,2048]{2,1,0:T(8,128)S(1)} %pad_maximum_fusion.3.mid_ref), channel_id=1, source_target_pairs={{1,0},{2,1},{3,2},{4,3},{5,4},{6,5},{7,6},{8,7},{9,8},{10,9},{11,1... | collective-permute-start | bytes 786440 | tf_op jit(solution)/shard_map/ppermute | solution.py:182
  92.6 8.9 %collective-permute-start.5 = (f32[4,8,2048]{2,1,0:T(8,128)S(1)}, f32[4,8,2048]{2,1,0:T(8,128)S(1)}, u32[]{:S(2)}, u32[]{:S(2)}) collective-permute-start(f32[4,8,2048]{2,1,0:T(8,128)S(1)} %pad_maximum_fusion.3.mid_ref), channel_id=1, source_target_pairs={{0,1},{1,2},{2,3},{3,4},{4,5},{5,6},{6,7},{7,8},{8,9},{9,10},{10,1... | collective-permute-start | bytes 786440 | tf_op jit(solution)/shard_map/ppermute | solution.py:181
  95.9 5.6 %copy-start.5 = (f32[4,8,2048]{2,1,0:T(8,128)}, f32[4,8,2048]{2,1,0:T(8,128)S(1)}, u32[]{:S(2)}) copy-start(f32[4,8,2048]{2,1,0:T(8,128)S(1)} %collective-permute-done.4.above_ref) | copy-start | bytes 786436
  101.5 0.7 copy-start.6

commit v4 on v3

--- a/solution.py
+++ b/solution.py
@@ -27,9 +27,58 @@
 
 
 TILE = 8
-
-
-def flow_kernel(flux_ref, link_ref, adj_hbm, jd_hbm, fw_hbm, below_hbm, above_hbm, edge_hbm,
+STRIPS = 16
+
+
+def pack_kernel(adj_lo, adj_hi, jd_lo, jd_hi, fw_lo, fw_hi, below_lo, below_hi, above_lo, above_hi,
+                low_ref, high_ref):
+    strip = low_ref.shape[2] // STRIPS
+    lanes = low_ref.shape[2]
+    lane = lax.broadcasted_iota(jnp.int32, low_ref.shape[1:], 1)
+    low = [jnp.zeros(low_ref.shape[1:], jnp.float32) for _ in range(low_ref.shape[0])]
+    high = [jnp.zeros(high_ref.shape[1:], jnp.float32) for _ in range(high_ref.shape[0])]
+    index = 0
+    for lo_ref, hi_ref in ((adj_lo, adj_hi), (jd_lo, jd_hi), (fw_lo, fw_hi)):
+        for f in range(lo_ref.shape[0]):
+            group, slot = divmod(index, STRIPS)
+            lo = jnp.concatenate([below_lo[index], lo_ref[f], above_lo[index]], axis=0)
+            hi = jnp.concatenate([below_hi[index], hi_ref[f], above_hi[index]], axis=0)
+            keep = (lane >= strip * slot) & (lane < strip * (slot + 1))
+            low[group] = jnp.where(keep, pltpu.roll(lo, (strip * slot) % lanes, 1), low[group])
+            high[group] = jnp.where(
+                keep, pltpu.roll(hi, (strip * slot - (lanes - strip)) % lanes, 1), high[group]
+            )
+            index += 1
+    for group in range(low_ref.shape[0]):
+        low_ref[group] = low[group]
+        high_ref[group] = high[group]
+
+
+def pack_strips(fields, below, above, deep):
+    rows_here, cols_here = fields[0].shape[1:]
+    n_fields = below.shape[0]
+    groups = -(-n_fields // STRIPS)
+    last = cols_here // LANES - 1
+
+    def chunk(x, c):
+        return pl.BlockSpec((x.shape[0], x.shape[1], LANES), lambda i: (0, 0, c))
+
+    specs = []
+    args = []
+    for x in list(fields) + [below, above]:
+        specs += [chunk(x, 0), chunk(x, last)]
+        args += [x, x]
+    out = jax.ShapeDtypeStruct((groups, rows_here + 2 * deep, LANES), jnp.float32)
+    return pl.pallas_call(
+        pack_kernel,
+        out_shape=(out, out),
+        grid=(1,),
+        in_specs=specs,
+        out_specs=(pl.BlockSpec(out.shape, lambda i: (0, 0, 0)),) * 2,
+    )(*args)
+
+
+def flow_kernel(flux_ref, link_ref, adj_hbm, jd_hbm, fw_hbm, below_hbm, above_hbm, left_ref, right_ref,
                 out_ref, tile_ref, buf0, buf1, sems):
     nf = out_ref.shape[0]
     rows_here = out_ref.shape[1]
@@ -49,15 +98,23 @@
         pltpu.make_async_copy(
             above_hbm, tile_ref.at[:, pad + rows_here : pad + rows_here + halo, 0:cols_here], sems.at[4]
         ),
-        pltpu.make_async_copy(edge_hbm, tile_ref.at[:, :, cols_here:width], sems.at[5]),
     ]
     for copy in copies:
         copy.start()
     for copy in copies:
         copy.wait()
-    zeros = jnp.zeros((n_fields, pad - halo, cols_here), jnp.float32)
-    tile_ref[:, 0 : pad - halo, 0:cols_here] = zeros
-    tile_ref[:, pad + rows_here + halo :, 0:cols_here] = zeros
+    zeros = jnp.zeros((n_fields, pad - halo, width), jnp.float32)
+    tile_ref[:, 0 : pad - halo, :] = zeros
+    tile_ref[:, pad + rows_here + halo :, :] = zeros
+    lanes = width - cols_here
+    strip = lanes // STRIPS
+    lane = lax.broadcasted_iota(jnp.int32, left_ref.shape[1:], 1)
+    for index in range(n_fields):
+        group, slot = divmod(index, STRIPS)
+        after = pltpu.roll(right_ref[group], (-strip * slot) % lanes, 1)
+        before = pltpu.roll(left_ref[group], (lanes - strip - strip * slot) % lanes, 1)
+        edge = jnp.where(lane < halo, after, jnp.where(lane >= lanes - halo, before, 0.0))
+        tile_ref[index, pad - halo : pad + rows_here + halo, cols_here:width] = edge
     link_above = link_ref[0]
     link_below = link_ref[1]
     bufs = (buf0, buf1)
@@ -109,7 +166,7 @@
     out_ref[...] = final[:, pad : pad + rows_here, 0:cols_here]
 
 
-def flow_iterations(flux_flat, links, adj, jd, fw, below, above, edge, width):
+def flow_iterations(flux_flat, links, adj, jd, fw, below, above, left, right, width):
     nf, rows_here, cols_here = adj.shape
     n_fields = below.shape[0]
     tile_shape = (n_fields, rows_here + 4 * TILE, width)
@@ -120,16 +177,17 @@
             pl.BlockSpec(memory_space=pltpu.SMEM),
             pl.BlockSpec(memory_space=pltpu.SMEM),
         ]
-        + [pl.BlockSpec(memory_space=pl.ANY)] * 6,
+        + [pl.BlockSpec(memory_space=pl.ANY)] * 5
+        + [pl.BlockSpec(memory_space=pltpu.VMEM)] * 2,
         out_specs=pl.BlockSpec(memory_space=pltpu.VMEM),
         scratch_shapes=[
             pltpu.VMEM(tile_shape, jnp.float32),
             pltpu.VMEM((nf,) + tile_shape[1:], jnp.float32),
             pltpu.VMEM((nf,) + tile_shape[1:], jnp.float32),
-            pltpu.SemaphoreType.DMA((6,)),
+            pltpu.SemaphoreType.DMA((5,)),
         ],
         compiler_params=pltpu.CompilerParams(vmem_limit_bytes=48 * 1024 * 1024),
-    )(flux_flat, links, adj, jd, fw, below, above, edge)
+    )(flux_flat, links, adj, jd, fw, below, above, left, right)
 
 
 def local(adj_source, jac_diag, face_weights, flux_jac, face_link, node_grad, stiffness):
@@ -152,19 +210,13 @@
     sub_count = lax.axis_size("sub")
     forward, backward = ring_pairs(sub_count, True)
 
-    def column_strip(lo, hi):
-        middle = jnp.concatenate([x[:, :, lo:hi] for x in fields], axis=0)
-        strip = jnp.concatenate([from_below[:, :, lo:hi], middle, from_above[:, :, lo:hi]], axis=1)
-        return jnp.swapaxes(strip, 1, 2)
-
-    from_left = lax.ppermute(column_strip(cols_here - deep, cols_here), "sub", forward)
-    from_right = lax.ppermute(column_strip(0, deep), "sub", backward)
-    gap = jnp.zeros(from_left.shape[:1] + from_left.shape[2:] + (width - cols_here - 2 * deep,), jnp.float32)
-    edge = jnp.concatenate([jnp.swapaxes(from_right, 1, 2), gap, jnp.swapaxes(from_left, 1, 2)], axis=2)
-    edge = jnp.pad(edge, ((0, 0), (2 * TILE - deep, 2 * TILE - deep), (0, 0)))
+    low_strips, high_strips = pack_strips(fields, from_below, from_above, deep)
+    from_left = lax.ppermute(high_strips, "sub", forward)
+    from_right = lax.ppermute(low_strips, "sub", backward)
     links = jnp.stack([link_above, link_below])
     adjoint = flow_iterations(
-        flux_jac.reshape(-1), links, fields[0], fields[1], fields[2], from_below, from_above, edge, width
+        flux_jac.reshape(-1), links, fields[0], fields[1], fields[2], from_below, from_above,
+        from_left, from_right, width
     )
 
     sensitivity = jnp.einsum(

time: 107 us -> 97.1 us (0.907)
  local copies, waits for them, and re-layouts: 15.1 us -> 6.33 us
  other arithmetic: 8.55 us -> 1.38 us
  Pallas kernels: 22.6 us -> 26.2 us
  blocking collectives: 7.92 us -> 9.28 us
    transpose x2 -> x0, local copies, waits for them, and re-layouts: 4.36 us -> none  [column_strip(): return jnp.swapaxes(strip, 1, 2)]
    ppermute x2 -> x0, local copies, waits for them, and re-layouts: 4.08 us -> none  [the longest x1 2.5 us: local(): from_right = lax.ppermute(column_strip(0, deep), 'sub', backward)]
    transpose x2 -> x0, other arithmetic: 3.29 us -> none  [column_strip(): return jnp.swapaxes(strip, 1, 2)]
    slice x5 -> x0, local copies, waits for them, and re-layouts: 3.22 us -> none  [the longest x3 2.3 us: column_strip(): middle = jnp.concatenate([x[:, :, lo:hi] for x in fields], axis=0)]
    unnamed x21 -> x29, local copies, waits for them, and re-layouts: 0.79 us -> 3.98 us
    pallas_call x0 -> x1, Pallas kernels: none -> 3.14 us  [pack_strips(): pl.pallas_call(pack_kernel, out_shape=(out, out), grid=(1,), in_specs=spe...]
    concatenate x1 -> x0, other arithmetic: 2.04 us -> none  [local(): jnp.concatenate([jnp.swapaxes(from_right, 1, 2), gap, jnp.swapaxes(from_l...]
    ppermute x1, waiting for transfers between devices: 0.01 us -> 1.91 us  [local(): lax.ppermute(jnp.concatenate([x[:, :deep] for x in fields], axis=0), 'blk...]
  transfers between devices with their start and end apart: 6 -> 6, of which waited for: 3 -> 5; matrix products, arithmetic and copies ran while one was open for 10% -> 1% of each run, Pallas kernels for 0% -> 0%
where the time goes in v4:
time: 97.1 us; the launch traced here: 96.5 us
  starting transfers between devices  40.1 us (41%)
  Pallas kernels  26.2 us (27%)
  waiting for transfers between devices  11 us (11%)
  blocking collectives  9.28 us (10%)
  local copies, waits for them, and re-layouts  6.33 us (7%)
  between operations  2.19 us (2%)
  other arithmetic  1.38 us (1%)
    pallas_call x1, Pallas kernels, flow_iterations(): pl.pallas_call(flow_kernel, out_shape=jax.ShapeDtypeStruct((nf, rows_here...  19.3 us
    ppermute x1, starting transfers between devices, local(): part_above = lax.ppermute(both, part_axis, backward)  17.4 us
    ppermute x1, starting transfers between devices, local(): lax.ppermute(jnp.concatenate([x[:, :deep] for x in fields], axis=0), 'blk...  9.75 us
    all_to_all x1, blocking collectives, local(): lax.all_to_all(sensitivity, 'sub', split_axis=1, concat_axis=2, tiled=True)  9.28 us
    ppermute x1, waiting for transfers between devices, local(): part_below = lax.ppermute(both, part_axis, forward)  5.6 us
    ppermute x1, starting transfers between devices, local(): lax.ppermute(jnp.concatenate([x[:, rows_here - deep:] for x in fields], a...  4.59 us
    unnamed x29, local copies, waits for them, and re-layouts  3.98 us
    pallas_call x1, Pallas kernels, warp_sweeps(): pl.pallas_call(functools.partial(warp_kernel, part_count), out_shape=jax....  3.76 us
  transfers between devices with their start and end apart: 6, of which 5 were waited for; matrix products, arithmetic and copies ran while one was open for 1% of the time, Pallas kernels for 0%

profile of v4, /device:TPU:1, one launch (start us, length us, event | category | flops | bytes accessed | tf_op | source)
XLA Modules:
  0.0 96.5 jit_solution(4928653462295750813)
XLA Ops:
  0.6 0.0 copy-start.3
  0.6 0.0 copy-start.5
  0.7 1.4 %fusion = (f32[36,8,512]{2,1,0:T(8,128)S(1)}, f32[36,8,512]{2,1,0:T(8,128)S(1)}) fusion(f32[36,32,512]{2,1,0:T(8,128)} %bitcast.13), kind=kLoop, calls=%fused_computation.6 | loop fusion | bytes 2359296 | tf_op jit(solution)/shard_map/slice | solution.py:209
  2.1 0.0 copy-done.3
  2.1 0.0 copy-done.5
  2.2 0.1 pad_maximum_fusion
  2.2 0.0 copy-start.13
  2.2 0.0 copy-start.12
  2.3 4.6 %collective-permute-start = (f32[50,8,512]{2,1,0:T(8,128)S(1)}, f32[50,8,512]{2,1,0:T(8,128)S(1)}, u32[]{:S(2)}, u32[]{:S(2)}) collective-permute-start(f32[50,8,512]{2,1,0:T(8,128)S(1)} %pad_maximum_fusion), channel_id=1, source_target_pairs={{0,4},{4,8},{8,12},{12,16},{16,20},{20,24},{24,28},{28,32},{32,36}... | collective-permute-start | bytes 2457608 | tf_op jit(solution)/shard_map/ppermute | solution.py:206
  6.9 0.1 pad_maximum_fusion.1
  6.9 9.8 %collective-permute-start.1 = (f32[50,8,512]{2,1,0:T(8,128)S(1)}, f32[50,8,512]{2,1,0:T(8,128)}, u32[]{:S(2)}, u32[]{:S(2)}) collective-permute-start(f32[50,8,512]{2,1,0:T(8,128)S(1)} %pad_maximum_fusion.1), channel_id=1, source_target_pairs={{4,0},{8,4},{12,8},{16,12},{20,16},{24,20},{28,24},{32,28},{36,32}... | collective-permute-start | bytes 2457608 | tf_op jit(solution)/shard_map/ppermute | solution.py:209
  16.7 0.0 copy-done.13
  16.7 0.6 fusion.3
  18.6 0.0 copy-done.12
  18.6 0.1 reshape.17.flux_ref
  18.8 0.0 collective-permute-done.below_lo.below_hi.below_hbm
  18.8 0.0 copy-start.1
  18.8 1.9 %collective-permute-done.1.above_lo.above_hi.above_hbm = f32[50,8,512]{2,1,0:T(8,128)} collective-permute-done((f32[50,8,512]{2,1,0:T(8,128)S(1)}, f32[50,8,512]{2,1,0:T(8,128)}, u32[]{:S(2)}, u32[]{:S(2)}) %collective-permute-start.1) | collective-permute-done | bytes 819232 | tf_op jit(solution)/shard_map/ppermute | solution.py:209
  20.7 0.0 copy-done.1
  20.7 0.0 copy-start
  20.7 3.1 %shard_map.86 = (f32[4,48,128]{2,1,0:T(8,128)}, f32[4,48,128]{2,1,0:T(8,128)}) custom-call(f32[6,32,512]{2,1,0:T(8,128)} %adj_hbm.1, f32[6,32,512]{2,1,0:T(8,128)} %adj_hbm.1, f32[36,32,512]{2,1,0:T(8,128)} %bitcast.14, f32[36,32,512]{2,1,0:T(8,128)} %bitcast.15, f32[8,32,512]{2,1,0:T(8,128)} %fw_hbm.1, f32[8,32,512]{2,1,0:T(8,128)} %fw_hbm.1, ...), custom_call_target="tpu_custom_call" | custom-call | tf_op jit(solution)/shard_map/pallas_call | solution.py:72
  23.8 3.1 %collective-permute-start.2 = (f32[4,48,128]{2,1,0:T(8,128)}, f32[4,48,128]{2,1,0:T(8,128)S(1)}, u32[]{:S(2)}, u32[]{:S(2)}) collective-permute-start(f32[4,48,128]{2,1,0:T(8,128)} %get-tuple-element.4), channel_id=1, source_target_pairs={{0,1},{1,2},{2,3},{3,0},{4,5},{5,6},{6,7},{7,4},{8,9},{9,10},{10,1... | collective-permute-start | bytes 294920 | tf_op jit(solution)/shard_map/ppermute | solution.py:214
  26.9 3.4 %collective-permute-start.3 = (f32[4,48,128]{2,1,0:T(8,128)}, f32[4,48,128]{2,1,0:T(8,128)S(1)}, u32[]{:S(2)}, u32[]{:S(2)}) collective-permute-start(f32[4,48,128]{2,1,0:T(8,128)} %get-tuple-element.5), channel_id=1, source_target_pairs={{1,0},{2,1},{3,2},{0,3},{5,4},{6,5},{7,6},{4,7},{9,8},{10,9},{11,1... | collective-permute-start | bytes 294920 | tf_op jit(solution)/shard_map/ppermute | solution.py:215
  30.3 0.1 pad_maximum_fusion.3.link_ref
  30.4 0.2 collective-permute-done.2.left_ref
  30.6 1.9 %collective-permute-done.3.right_ref = f32[4,48,128]{2,1,0:T(8,128)S(1)} collective-permute-done((f32[4,48,128]{2,1,0:T(8,128)}, f32[4,48,128]{2,1,0:T(8,128)S(1)}, u32[]{:S(2)}, u32[]{:S(2)}) %collective-permute-start.3) | collective-permute-done | bytes 98336 | tf_op jit(solution)/shard_map/ppermute | solution.py:215
  32.5 0.0 copy-done
  32.5 0.0 copy-start.2
  32.5 1.1 %copy-done.2 = f32[50,8,512]{2,1,0:T(8,128)S(1)} copy-done((f32[50,8,512]{2,1,0:T(8,128)S(1)}, f32[50,8,512]{2,1,0:T(8,128)}, u32[]{:S(2)}) %copy-start.2) | copy-done | bytes 819224
  33.7 1.0 %copy-done.4 = f32[8,32,512]{2,1,0:T(8,128)S(1)} copy-done((f32[8,32,512]{2,1,0:T(8,128)S(1)}, f32[8,32,512]{2,1,0:T(8,128)}, u32[]{:S(2)}) %copy-start.4) | copy-done | bytes 524312
  34.7 1.0 %copy-done.6 = f32[6,32,512]{2,1,0:T(8,128)S(1)} copy-done((f32[6,32,512]{2,1,0:T(8,128)S(1)}, f32[6,32,512]{2,1,0:T(8,128)}, u32[]{:S(2)}) %copy-start.6) | copy-done | bytes 393240
  35.7 19.3 %shard_map.87 = f32[6,32,512]{2,1,0:T(8,128)} custom-call(f32[288]{0:T(512)S(1)} %reshape.17.flux_ref, f32[2]{0:T(128)S(1)} %pad_maximum_fusion.3.link_ref, f32[6,32,512]{2,1,0:T(8,128)S(1)} %copy-done.6, f32[36,32,512]{2,1,0:T(8,128)S(1)} %bitcast.16, f32[8,32,512]{2,1,0:T(8,128)S(1)} %copy-done.4, f32[50,8,512]{2,1,0:T(8,128)S(1)} %copy-done.2, ...), custom_call_target="tpu_custom_call" | custom-call | tf_op jit(solution)/shard_map/pallas_call | solution.py:173
  55.1 0.0 copy-done.8
  55.1 0.0 copy-start.11
  55.1 1.2 %multiply_reduce_fusion = f32[32,512,3]{1,0,2:T(8,128)S(1)} fusion(f32[32,512,6]{1,0,2:T(8,128)} %bitcast.17, bf16[3,6,32,512]{3,2,1,0:T(8,128)(2,1)S(1)} %copy-done.8), kind=kLoop, calls=%fused_computation | loop fusion | flops 835584 | bytes 1179648
  56.3 0.1 copy.22
  56.4 9.3 %all_to_all.18 = f32[3,32,512]{2,0,1:T(4,128)S(1)} all-to-all(f32[3,32,512]{2,0,1:T(4,128)S(1)} %bitcast.18), channel_id=1, replica_groups=mesh['blk'=192,'sub'=4] {'sub'}, dimensions={1} | all-to-all | bytes 393216 | tf_op jit(solution)/shard_map/all_to_all | solution.py:225
  65.7 0.1 copy.11
  65.7 0.0 copy-done.11
  65.8 0.0 copy-start.7
  65.8 17.4 %collective-permute-start.4 = (f32[4,8,2048]{2,1,0:T(8,128)S(1)}, f32[4,8,2048]{2,1,0:T(8,128)S(1)}, u32[]{:S(2)}, u32[]{:S(2)}) collective-permute-start(f32[4,8,2048]{2,1,0:T(8,128)S(1)} %pad_maximum_fusion.2.mid_ref), channel_id=1, source_target_pairs={{1,0},{2,1},{3,2},{4,3},{5,4},{6,5},{7,6},{8,7},{9,8},{10,9},{11,1... | collective-permute-start | bytes 786440 | tf_op jit(solution)/shard_map/ppermute | solution.py:234
  83.2 1.9 %collective-permute-start.5 = (f32[4,8,2048]{2,1,0:T(8,128)S(1)}, f32[4,8,2048]{2,1,0:T(8,128)S(1)}, u32[]{:S(2)}, u32[]{:S(2)}) collective-permute-start(f32[4,8,2048]{2,1,0:T(8,128)S(1)} %pad_maximum_fusion.2.mid_ref), channel_id=1, source_target_pairs={{0,1},{1,2},{2,3},{3,4},{4,5},{5,6},{6,7},{7,8},{8,9},{9,10},{10,1... | collective-permute-start | bytes 786440 | tf_op jit(solution)/shard_map/ppermute | solution.py:233
  85.1 1.4 %collective-permute-done.4.above_ref = f32[4,8,2048]{2,1,0:T(8,128)S(1)} collective-permute-done((f32[4,8,2048]{2,1,0:T(8,128)S(1)}, f32[4,8,2048]{2,1,0:T(8,128)S(1)}, u32[]{:S(2)}, u32[]{:S(2)}) %collective-permute-start.4) | collective-permute-done | bytes 262176 | tf_op jit(solution)/shard_map/ppermute | solution.py:234
  86.5 5.6 %collective-permute-done.5.below_ref = f32[4,8,2048]{2,1,0:T(8,128)S(1)} collective-permute-done((f32[4,8,2048]{2,1,0:T(8,128)S(1)}, f32[4,8,2048]{2,1,0:T(8,128)S(1)}, u32[]{:S(2)}, u32[]{:S(2)}) %collective-permute-start.5) | collective-permute-done | bytes 262176 | tf_op jit(solution)/shard_map/ppermute | solution.py:233
  92.1 0.0 copy-done.7
  92.1 0.0 copy-done.9
  92.1 0.7 copy-done.10
  92.8 3.8 %shard_map.88 = f32[3,8,2048]{2,1,0:T(8,128)} custom-call(s32[1]{0:T(128)} %bitcast.3.index_ref, f32[4,8,2048]{2,1,0:T(8,128)} %copy-done.7, f32[4,8,2048]{2,1,0:T(8,128)} %copy-done.9, f32[4,8,2048]{2,1,0:T(8,128)} %copy-done.10), custom_call_target="tpu_custom_call" | custom-call | tf_op jit(solution)/shard_map/pallas_call | solution.py:273
  (9 shorter events, 0.1 us)
Async XLA Ops:
  0.6 1.4 %copy-start.3 = (f32[8,32,512]{2,1,0:T(8,128)S(1)}, f32[8,32,512]{2,1,0:T(8,128)}, u32[]{:S(2)}) copy-start(f32[8,32,512]{2,1,0:T(8,128)} %fw_hbm.1) | copy-start | bytes 1572868
  0.6 1.5 %copy-start.5 = (f32[6,32,512]{2,1,0:T(8,128)S(1)}, f32[6,32,512]{2,1,0:T(8,128)}, u32[]{:S(2)}) copy-start(f32[6,32,512]{2,1,0:T(8,128)} %adj_hbm.1) | copy-start | bytes 1179652
  2.2 14.5 %copy-start.13 = (s32[192]{0:T(256)S(1)}, s32[192]{0:T(256)}, u32[]{:S(2)}) copy-start(s32[192]{0:T(256)} %param.11) | copy-start | bytes 2308
  2.2 16.4 %copy-start.12 = (f32[8,6,6]{2,0,1:T(8,128)S(1)}, f32[8,6,6]{2,0,1:T(8,128)}, u32[]{:S(2)}) copy-start(f32[8,6,6]{2,0,1:T(8,128)} %param.10) | copy-start | bytes 3460
  2.3 16.5 %collective-permute-start = (f32[50,8,512]{2,1,0:T(8,128)S(1)}, f32[50,8,512]{2,1,0:T(8,128)S(1)}, u32[]{:S(2)}, u32[]{:S(2)}) collective-permute-start(f32[50,8,512]{2,1,0:T(8,128)S(1)} %pad_maximum_fusion), channel_id=1, source_target_pairs={{0,4},{4,8},{8,12},{12,16},{16,20},{20,24},{24,28},{28,32},{32,36}... | collective-permute-start | bytes 2457608 | tf_op jit(solution)/shard_map/ppermute | solution.py:206
  6.9 13.8 %collective-permute-start.1 = (f32[50,8,512]{2,1,0:T(8,128)S(1)}, f32[50,8,512]{2,1,0:T(8,128)}, u32[]{:S(2)}, u32[]{:S(2)}) collective-permute-start(f32[50,8,512]{2,1,0:T(8,128)S(1)} %pad_maximum_fusion.1), channel_id=1, source_target_pairs={{4,0},{8,4},{12,8},{16,12},{20,16},{24,20},{28,24},{32,28},{36,32}... | collective-permute-start | bytes 2457608 | tf_op jit(solution)/shard_map/ppermute | solution.py:209
  18.8 1.9 %copy-start.1 = (f32[50,8,512]{2,1,0:T(8,128)}, f32[50,8,512]{2,1,0:T(8,128)S(1)}, u32[]{:S(2)}) copy-start(f32[50,8,512]{2,1,0:T(8,128)S(1)} %collective-permute-done.below_lo.below_hi.below_hbm) | copy-start | bytes 2457604
  20.7 11.8 %copy-start = (f32[6,6,32,512]{3,2,1,0:T(8,128)S(1)}, f32[6,6,32,512]{3,2,1,0:T(8,128)}, u32[]{:S(2)}) copy-start(f32[6,6,32,512]{3,2,1,0:T(8,128)} %param.8) | copy-start | bytes 7077892
  23.8 6.8 %collective-permute-start.2 = (f32[4,48,128]{2,1,0:T(8,128)}, f32[4,48,128]{2,1,0:T(8,128)S(1)}, u32[]{:S(2)}, u32[]{:S(2)}) collective-permute-start(f32[4,48,128]{2,1,0:T(8,128)} %get-tuple-element.4), channel_id=1, source_target_pairs={{0,1},{1,2},{2,3},{3,0},{4,5},{5,6},{6,7},{7,4},{8,9},{9,10},{10,1... | collective-permute-start | bytes 294920 | tf_op jit(solution)/shard_map/ppermute | solution.py:214
  26.9 5.6 %collective-permute-start.3 = (f32[4,48,128]{2,1,0:T(8,128)}, f32[4,48,128]{2,1,0:T(8,128)S(1)}, u32[]{:S(2)}, u32[]{:S(2)}) collective-permute-start(f32[4,48,128]{2,1,0:T(8,128)} %get-tuple-element.5), channel_id=1, source_target_pairs={{1,0},{2,1},{3,2},{0,3},{5,4},{6,5},{7,6},{4,7},{9,8},{10,9},{11,1... | collective-permute-start | bytes 294920 | tf_op jit(solution)/shard_map/ppermute | solution.py:215
  32.5 1.1 %copy-start.2 = (f32[50,8,512]{2,1,0:T(8,128)S(1)}, f32[50,8,512]{2,1,0:T(8,128)}, u32[]{:S(2)}) copy-start(f32[50,8,512]{2,1,0:T(8,128)} %copy-done.1) | copy-start | bytes 2457604
  33.7 1.0 %copy-start.4 = (f32[8,32,512]{2,1,0:T(8,128)S(1)}, f32[8,32,512]{2,1,0:T(8,128)}, u32[]{:S(2)}) copy-start(f32[8,32,512]{2,1,0:T(8,128)} %fw_hbm.1) | copy-start | bytes 1572868
  34.7 1.0 %copy-start.6 = (f32[6,32,512]{2,1,0:T(8,128)S(1)}, f32[6,32,512]{2,1,0:T(8,128)}, u32[]{:S(2)}) copy-start(f32[6,32,512]{2,1,0:T(8,128)} %adj_hbm.1) | copy-start | bytes 1179652
  35.7 19.4 %copy-start.8 = (bf16[3,6,32,512]{3,2,1,0:T(8,128)(2,1)S(1)}, bf16[3,6,32,512]{3,2,1,0:T(8,128)(2,1)}, u32[]{:S(2)}) copy-start(bf16[3,6,32,512]{3,2,1,0:T(8,128)(2,1)} %param.12) | copy-start | bytes 1769476
  55.1 10.7 %copy-start.11 = (f32[8,2048]{1,0:T(8,128)S(1)}, f32[8,2048]{1,0:T(8,128)}, u32[]{:S(2)}) copy-start(f32[8,2048]{1,0:T(8,128)} %param.13) | copy-start | bytes 196612
  65.8 26.3 %copy-start.7 = (f32[4,8,2048]{2,1,0:T(8,128)}, f32[4,8,2048]{2,1,0:T(8,128)S(1)}, u32[]{:S(2)}) copy-start(f32[4,8,2048]{2,1,0:T(8,128)S(1)} %pad_maximum_fusion.2.mid_ref) | copy-start | bytes 786436
  65.8 20.7 %collective-permute-start.4 = (f32[4,8,2048]{2,1,0:T(8,128)S(1)}, f32[4,8,2048]{2,1,0:T(8,128)S(1)}, u32[]{:S(2)}, u32[]{:S(2)}) collective-permute-start(f32[4,8,2048]{2,1,0:T(8,128)S(1)} %pad_maximum_fusion.2.mid_ref), channel_id=1, source_target_pairs={{1,0},{2,1},{3,2},{4,3},{5,4},{6,5},{7,6},{8,7},{9,8},{10,9},{11,1... | collective-permute-start | bytes 786440 | tf_op jit(solution)/shard_map/ppermute | solution.py:234
  83.2 8.9 %collective-permute-start.5 = (f32[4,8,2048]{2,1,0:T(8,128)S(1)}, f32[4,8,2048]{2,1,0:T(8,128)S(1)}, u32[]{:S(2)}, u32[]{:S(2)}) collective-permute-start(f32[4,8,2048]{2,1,0:T(8,128)S(1)} %pad_maximum_fusion.2.mid_ref), channel_id=1, source_target_pairs={{0,1},{1,2},{2,3},{3,4},{4,5},{5,6},{6,7},{7,8},{8,9},{9,10},{10,1... | collective-permute-start | bytes 786440 | tf_op jit(solution)/shard_map/ppermute | solution.py:233
  86.5 5.6 %copy-start.9 = (f32[4,8,2048]{2,1,0:T(8,128)}, f32[4,8,2048]{2,1,0:T(8,128)S(1)}, u32[]{:S(2)}) copy-start(f32[4,8,2048]{2,1,0:T(8,128)S(1)} %collective-permute-done.4.above_ref) | copy-start | bytes 786436
  92.1 0.7 copy-start.10

commit v5 on v4

--- a/solution.py
+++ b/solution.py
@@ -79,7 +79,7 @@
 
 
 def flow_kernel(flux_ref, link_ref, adj_hbm, jd_hbm, fw_hbm, below_hbm, above_hbm, left_ref, right_ref,
-                out_ref, tile_ref, buf0, buf1, sems):
+                grad_ref, out_ref, sens_ref, tile_ref, buf0, buf1, sems):
     nf = out_ref.shape[0]
     rows_here = out_ref.shape[1]
     cols_here = out_ref.shape[2]
@@ -163,23 +163,33 @@
 
         lax.fori_loop(first, stop, body, 0)
     final = bufs[(ITERS - 1) % 2]
-    out_ref[...] = final[:, pad : pad + rows_here, 0:cols_here]
-
-
-def flow_iterations(flux_flat, links, adj, jd, fw, below, above, left, right, width):
+    adjoint = [final[f, pad : pad + rows_here, 0:cols_here] for f in range(nf)]
+    for f in range(nf):
+        out_ref[f] = adjoint[f]
+    for c in range(sens_ref.shape[0]):
+        acc = grad_ref[c * nf].astype(jnp.float32) * adjoint[0]
+        for f in range(1, nf):
+            acc = acc + grad_ref[c * nf + f].astype(jnp.float32) * adjoint[f]
+        sens_ref[c] = acc
+
+
+def flow_iterations(flux_flat, links, adj, jd, fw, below, above, left, right, grad, width):
     nf, rows_here, cols_here = adj.shape
     n_fields = below.shape[0]
     tile_shape = (n_fields, rows_here + 4 * TILE, width)
     return pl.pallas_call(
         flow_kernel,
-        out_shape=jax.ShapeDtypeStruct((nf, rows_here, cols_here), jnp.float32),
+        out_shape=(
+            jax.ShapeDtypeStruct((nf, rows_here, cols_here), jnp.float32),
+            jax.ShapeDtypeStruct((grad.shape[0] // nf, rows_here, cols_here), jnp.float32),
+        ),
         in_specs=[
             pl.BlockSpec(memory_space=pltpu.SMEM),
             pl.BlockSpec(memory_space=pltpu.SMEM),
         ]
         + [pl.BlockSpec(memory_space=pl.ANY)] * 5
-        + [pl.BlockSpec(memory_space=pltpu.VMEM)] * 2,
-        out_specs=pl.BlockSpec(memory_space=pltpu.VMEM),
+        + [pl.BlockSpec(memory_space=pltpu.VMEM)] * 3,
+        out_specs=(pl.BlockSpec(memory_space=pltpu.VMEM), pl.BlockSpec(memory_space=pltpu.VMEM)),
         scratch_shapes=[
             pltpu.VMEM(tile_shape, jnp.float32),
             pltpu.VMEM((nf,) + tile_shape[1:], jnp.float32),
@@ -187,7 +197,7 @@
             pltpu.SemaphoreType.DMA((5,)),
         ],
         compiler_params=pltpu.CompilerParams(vmem_limit_bytes=48 * 1024 * 1024),
-    )(flux_flat, links, adj, jd, fw, below, above, left, right)
+    )(flux_flat, links, adj, jd, fw, below, above, left, right, grad)
 
 
 def local(adj_source, jac_diag, face_weights, flux_jac, face_link, node_grad, stiffness):
@@ -214,14 +224,11 @@
     from_left = lax.ppermute(high_strips, "sub", forward)
     from_right = lax.ppermute(low_strips, "sub", backward)
     links = jnp.stack([link_above, link_below])
-    adjoint = flow_iterations(
+    adjoint, sensitivity = flow_iterations(
         flux_jac.reshape(-1), links, fields[0], fields[1], fields[2], from_below, from_above,
-        from_left, from_right, width
+        from_left, from_right, node_grad.reshape((-1,) + node_grad.shape[2:]), width
     )
 
-    sensitivity = jnp.einsum(
-        "cfij,fij->cij", node_grad.astype(jnp.float32), adjoint, precision=lax.Precision.HIGHEST
-    )
     moved = lax.all_to_all(sensitivity, "sub", split_axis=1, concat_axis=2, tiled=True)
 
     part_axis = ("blk", "sub")

time: 97.1 us -> 99 us (1.020)
  local copies, waits for them, and re-layouts: 6.33 us -> 7.36 us
    unnamed x1 -> x0, other arithmetic: 1.17 us -> none
    unnamed x29, local copies, waits for them, and re-layouts: 3.98 us -> 5.01 us
  transfers between devices with their start and end apart: 6 -> 6, of which waited for: 5 -> 5; matrix products, arithmetic and copies ran while one was open for 1% -> 2% of each run, Pallas kernels for 0% -> 0%
where the time goes in v5:
time: 99 us; the launch traced here: 98.4 us
  starting transfers between devices  40 us (40%)
  Pallas kernels  26.1 us (26%)
  waiting for transfers between devices  11.4 us (12%)
  blocking collectives  9.28 us (9%)
  local copies, waits for them, and re-layouts  7.36 us (7%)
  between operations  2.17 us (2%)
  other arithmetic  2.08 us (2%)
    pallas_call x1, Pallas kernels, flow_iterations(): pl.pallas_call(flow_kernel, out_shape=(jax.ShapeDtypeStruct((nf, rows_her...  19.4 us
    ppermute x1, starting transfers between devices, local(): part_above = lax.ppermute(both, part_axis, backward)  17.3 us
    ppermute x1, starting transfers between devices, local(): lax.ppermute(jnp.concatenate([x[:, :deep] for x in fields], axis=0), 'blk...  9.74 us
    all_to_all x1, blocking collectives, local(): lax.all_to_all(sensitivity, 'sub', split_axis=1, concat_axis=2, tiled=True)  9.28 us
    ppermute x1, waiting for transfers between devices, local(): part_below = lax.ppermute(both, part_axis, forward)  5.6 us
    unnamed x29, local copies, waits for them, and re-layouts  5.01 us
    ppermute x1, starting transfers between devices, local(): lax.ppermute(jnp.concatenate([x[:, rows_here - deep:] for x in fields], a...  4.58 us
    pallas_call x1, Pallas kernels, warp_sweeps(): pl.pallas_call(functools.partial(warp_kernel, part_count), out_shape=jax....  3.76 us
  transfers between devices with their start and end apart: 6, of which 5 were waited for; matrix products, arithmetic and copies ran while one was open for 2% of the time, Pallas kernels for 0%

profile of v5, /device:TPU:1, one launch (start us, length us, event | category | flops | bytes accessed | tf_op | source)
XLA Modules:
  0.0 98.4 jit_solution(12915852346435305526)
XLA Ops:
  0.6 0.0 copy-start.3
  0.6 0.0 copy-start.5
  0.7 1.4 %fusion = (f32[36,8,512]{2,1,0:T(8,128)S(1)}, f32[36,8,512]{2,1,0:T(8,128)S(1)}) fusion(f32[36,32,512]{2,1,0:T(8,128)} %bitcast.8), kind=kLoop, calls=%fused_computation.4 | loop fusion | bytes 2359296 | tf_op jit(solution)/shard_map/slice | solution.py:219
  2.1 0.0 copy-done.3
  2.1 0.0 copy-start.13
  2.1 0.0 copy-start.12
  2.1 0.0 copy-done.5
  2.2 1.0 pad_maximum_fusion
  3.1 4.6 %collective-permute-start = (f32[50,8,512]{2,1,0:T(8,128)}, f32[50,8,512]{2,1,0:T(8,128)S(1)}, u32[]{:S(2)}, u32[]{:S(2)}) collective-permute-start(f32[50,8,512]{2,1,0:T(8,128)} %pad_maximum_fusion), channel_id=1, source_target_pairs={{0,4},{4,8},{8,12},{12,16},{16,20},{20,24},{24,28},{28,32},{32,36}... | collective-permute-start | bytes 2457608 | tf_op jit(solution)/shard_map/ppermute | solution.py:216
  7.7 1.0 %pad_maximum_fusion.1 = f32[50,8,512]{2,1,0:T(8,128)} fusion(f32[8,8,512]{2,1,0:T(8,128)S(1)} %get-tuple-element.12, f32[36,8,512]{2,1,0:T(8,128)S(1)} %get-tuple-element.10, f32[6,8,512]{2,1,0:T(8,128)S(1)} %get-tuple-element.14), kind=kLoop, calls=%fused_computation.1 | loop fusion | flops 409600 | bytes 1638400 | tf_op jit(solution)/shard_map/concatenate | solution.py:219
  8.7 9.7 %collective-permute-start.1 = (f32[50,8,512]{2,1,0:T(8,128)}, f32[50,8,512]{2,1,0:T(8,128)}, u32[]{:S(2)}, u32[]{:S(2)}) collective-permute-start(f32[50,8,512]{2,1,0:T(8,128)} %pad_maximum_fusion.1), channel_id=1, source_target_pairs={{4,0},{8,4},{12,8},{16,12},{20,16},{24,20},{28,24},{32,28},{36,32}... | collective-permute-start | bytes 2457608 | tf_op jit(solution)/shard_map/ppermute | solution.py:219
  18.5 0.0 copy-done.13
  18.5 0.6 fusion.3
  20.4 0.0 copy-done.12
  20.4 0.1 reshape.20.flux_ref
  20.6 0.0 copy-start
  20.6 0.0 collective-permute-done.below_lo.below_hi.below_hbm
  20.6 0.0 copy-start.1
  20.6 2.3 %collective-permute-done.1.above_lo.above_hi.above_hbm = f32[50,8,512]{2,1,0:T(8,128)} collective-permute-done((f32[50,8,512]{2,1,0:T(8,128)}, f32[50,8,512]{2,1,0:T(8,128)}, u32[]{:S(2)}, u32[]{:S(2)}) %collective-permute-start.1) | collective-permute-done | bytes 819232 | tf_op jit(solution)/shard_map/ppermute | solution.py:219
  22.9 0.0 copy-done.1
  22.9 3.0 %shard_map.86 = (f32[4,48,128]{2,1,0:T(8,128)}, f32[4,48,128]{2,1,0:T(8,128)}) custom-call(f32[6,32,512]{2,1,0:T(8,128)} %adj_hbm.1, f32[6,32,512]{2,1,0:T(8,128)} %adj_hbm.1, f32[36,32,512]{2,1,0:T(8,128)} %bitcast.9, f32[36,32,512]{2,1,0:T(8,128)} %bitcast.10, f32[8,32,512]{2,1,0:T(8,128)} %fw_hbm.1, f32[8,32,512]{2,1,0:T(8,128)} %fw_hbm.1, ...), custom_call_target="tpu_custom_call" | custom-call | tf_op jit(solution)/shard_map/pallas_call | solution.py:72
  25.9 3.1 %collective-permute-start.2 = (f32[4,48,128]{2,1,0:T(8,128)}, f32[4,48,128]{2,1,0:T(8,128)S(1)}, u32[]{:S(2)}, u32[]{:S(2)}) collective-permute-start(f32[4,48,128]{2,1,0:T(8,128)} %get-tuple-element.6), channel_id=1, source_target_pairs={{0,1},{1,2},{2,3},{3,0},{4,5},{5,6},{6,7},{7,4},{8,9},{9,10},{10,1... | collective-permute-start | bytes 294920 | tf_op jit(solution)/shard_map/ppermute | solution.py:224
  29.0 3.4 %collective-permute-start.3 = (f32[4,48,128]{2,1,0:T(8,128)}, f32[4,48,128]{2,1,0:T(8,128)S(1)}, u32[]{:S(2)}, u32[]{:S(2)}) collective-permute-start(f32[4,48,128]{2,1,0:T(8,128)} %get-tuple-element.7), channel_id=1, source_target_pairs={{1,0},{2,1},{3,2},{0,3},{5,4},{6,5},{7,6},{4,7},{9,8},{10,9},{11,1... | collective-permute-start | bytes 294920 | tf_op jit(solution)/shard_map/ppermute | solution.py:225
  32.4 0.1 pad_maximum_fusion.3.link_ref
  32.5 0.2 collective-permute-done.2.left_ref
  32.7 1.9 %collective-permute-done.3.right_ref = f32[4,48,128]{2,1,0:T(8,128)S(1)} collective-permute-done((f32[4,48,128]{2,1,0:T(8,128)}, f32[4,48,128]{2,1,0:T(8,128)S(1)}, u32[]{:S(2)}, u32[]{:S(2)}) %collective-permute-start.3) | collective-permute-done | bytes 98336 | tf_op jit(solution)/shard_map/ppermute | solution.py:225
  34.6 0.0 copy-done
  34.6 0.0 copy-start.2
  34.6 1.1 %copy-done.2 = f32[50,8,512]{2,1,0:T(8,128)S(1)} copy-done((f32[50,8,512]{2,1,0:T(8,128)S(1)}, f32[50,8,512]{2,1,0:T(8,128)}, u32[]{:S(2)}) %copy-start.2) | copy-done | bytes 819224
  35.7 0.0 copy-start.4
  35.7 1.0 %copy-done.4 = f32[8,32,512]{2,1,0:T(8,128)S(1)} copy-done((f32[8,32,512]{2,1,0:T(8,128)S(1)}, f32[8,32,512]{2,1,0:T(8,128)}, u32[]{:S(2)}) %copy-start.4) | copy-done | bytes 524312
  36.8 0.0 copy-start.6
  36.8 1.0 %copy-done.6 = f32[6,32,512]{2,1,0:T(8,128)S(1)} copy-done((f32[6,32,512]{2,1,0:T(8,128)S(1)}, f32[6,32,512]{2,1,0:T(8,128)}, u32[]{:S(2)}) %copy-start.6) | copy-done | bytes 393240
  37.8 1.1 %copy-done.7 = bf16[3,6,32,512]{3,2,1,0:T(8,128)(2,1)S(1)} copy-done((bf16[3,6,32,512]{3,2,1,0:T(8,128)(2,1)S(1)}, bf16[3,6,32,512]{3,2,1,0:T(8,128)(2,1)}, u32[]{:S(2)}) %copy-start.7) | copy-done | bytes 589848
  38.8 19.4 %shard_map.87 = (f32[6,32,512]{2,1,0:T(8,128)}, f32[3,32,512]{2,1,0:T(8,128)S(1)}) custom-call(f32[288]{0:T(512)S(1)} %reshape.20.flux_ref, f32[2]{0:T(128)S(1)} %pad_maximum_fusion.3.link_ref, f32[6,32,512]{2,1,0:T(8,128)S(1)} %copy-done.6, f32[36,32,512]{2,1,0:T(8,128)S(1)} %bitcast.11, f32[8,32,512]{2,1,0:T(8,128)S(1)} %copy-done.4, ...), custom_call_target="tpu_custom_call" | custom-call | tf_op jit(solution)/shard_map/pallas_call | solution.py:180
  58.2 0.1 copy.11
  58.4 9.3 %all_to_all.18 = f32[3,32,512]{2,0,1:T(4,128)S(1)} all-to-all(f32[3,32,512]{2,0,1:T(4,128)S(1)} %copy.11), channel_id=1, replica_groups=mesh['blk'=192,'sub'=4] {'sub'}, dimensions={1} | all-to-all | bytes 393216 | tf_op jit(solution)/shard_map/all_to_all | solution.py:232
  67.6 0.1 copy.12
  67.7 0.0 copy-done.11
  67.7 0.0 copy-start.8
  67.8 17.3 %collective-permute-start.4 = (f32[4,8,2048]{2,1,0:T(8,128)S(1)}, f32[4,8,2048]{2,1,0:T(8,128)S(1)}, u32[]{:S(2)}, u32[]{:S(2)}) collective-permute-start(f32[4,8,2048]{2,1,0:T(8,128)S(1)} %pad_maximum_fusion.2.mid_ref), channel_id=1, source_target_pairs={{1,0},{2,1},{3,2},{4,3},{5,4},{6,5},{7,6},{8,7},{9,8},{10,9},{11,1... | collective-permute-start | bytes 786440 | tf_op jit(solution)/shard_map/ppermute | solution.py:241
  85.1 1.9 %collective-permute-start.5 = (f32[4,8,2048]{2,1,0:T(8,128)S(1)}, f32[4,8,2048]{2,1,0:T(8,128)S(1)}, u32[]{:S(2)}, u32[]{:S(2)}) collective-permute-start(f32[4,8,2048]{2,1,0:T(8,128)S(1)} %pad_maximum_fusion.2.mid_ref), channel_id=1, source_target_pairs={{0,1},{1,2},{2,3},{3,4},{4,5},{5,6},{6,7},{7,8},{8,9},{9,10},{10,1... | collective-permute-start | bytes 786440 | tf_op jit(solution)/shard_map/ppermute | solution.py:240
  87.0 1.4 %collective-permute-done.4.above_ref = f32[4,8,2048]{2,1,0:T(8,128)S(1)} collective-permute-done((f32[4,8,2048]{2,1,0:T(8,128)S(1)}, f32[4,8,2048]{2,1,0:T(8,128)S(1)}, u32[]{:S(2)}, u32[]{:S(2)}) %collective-permute-start.4) | collective-permute-done | bytes 262176 | tf_op jit(solution)/shard_map/ppermute | solution.py:241
  88.4 5.6 %collective-permute-done.5.below_ref = f32[4,8,2048]{2,1,0:T(8,128)S(1)} collective-permute-done((f32[4,8,2048]{2,1,0:T(8,128)S(1)}, f32[4,8,2048]{2,1,0:T(8,128)S(1)}, u32[]{:S(2)}, u32[]{:S(2)}) %collective-permute-start.5) | collective-permute-done | bytes 262176 | tf_op jit(solution)/shard_map/ppermute | solution.py:240
  94.0 0.0 copy-done.8
  94.0 0.0 copy-done.9
  94.0 0.7 copy-done.10
  94.7 3.8 %shard_map.88 = f32[3,8,2048]{2,1,0:T(8,128)} custom-call(s32[1]{0:T(128)} %bitcast.2.index_ref, f32[4,8,2048]{2,1,0:T(8,128)} %copy-done.8, f32[4,8,2048]{2,1,0:T(8,128)} %copy-done.9, f32[4,8,2048]{2,1,0:T(8,128)} %copy-done.10), custom_call_target="tpu_custom_call" | custom-call | tf_op jit(solution)/shard_map/pallas_call | solution.py:280
  (8 shorter events, 0.1 us)
Async XLA Ops:
  0.6 1.4 %copy-start.3 = (f32[8,32,512]{2,1,0:T(8,128)S(1)}, f32[8,32,512]{2,1,0:T(8,128)}, u32[]{:S(2)}) copy-start(f32[8,32,512]{2,1,0:T(8,128)} %fw_hbm.1) | copy-start | bytes 1572868
  0.6 1.5 %copy-start.5 = (f32[6,32,512]{2,1,0:T(8,128)S(1)}, f32[6,32,512]{2,1,0:T(8,128)}, u32[]{:S(2)}) copy-start(f32[6,32,512]{2,1,0:T(8,128)} %adj_hbm.1) | copy-start | bytes 1179652
  2.1 16.4 %copy-start.13 = (s32[192]{0:T(256)S(1)}, s32[192]{0:T(256)}, u32[]{:S(2)}) copy-start(s32[192]{0:T(256)} %param.11) | copy-start | bytes 2308
  2.1 18.3 %copy-start.12 = (f32[8,6,6]{2,0,1:T(8,128)S(1)}, f32[8,6,6]{2,0,1:T(8,128)}, u32[]{:S(2)}) copy-start(f32[8,6,6]{2,0,1:T(8,128)} %param.10) | copy-start | bytes 3460
  3.1 17.4 %collective-permute-start = (f32[50,8,512]{2,1,0:T(8,128)}, f32[50,8,512]{2,1,0:T(8,128)S(1)}, u32[]{:S(2)}, u32[]{:S(2)}) collective-permute-start(f32[50,8,512]{2,1,0:T(8,128)} %pad_maximum_fusion), channel_id=1, source_target_pairs={{0,4},{4,8},{8,12},{12,16},{16,20},{20,24},{24,28},{28,32},{32,36}... | collective-permute-start | bytes 2457608 | tf_op jit(solution)/shard_map/ppermute | solution.py:216
  8.7 14.2 %collective-permute-start.1 = (f32[50,8,512]{2,1,0:T(8,128)}, f32[50,8,512]{2,1,0:T(8,128)}, u32[]{:S(2)}, u32[]{:S(2)}) collective-permute-start(f32[50,8,512]{2,1,0:T(8,128)} %pad_maximum_fusion.1), channel_id=1, source_target_pairs={{4,0},{8,4},{12,8},{16,12},{20,16},{24,20},{28,24},{32,28},{36,32}... | collective-permute-start | bytes 2457608 | tf_op jit(solution)/shard_map/ppermute | solution.py:219
  20.6 14.0 %copy-start = (f32[6,6,32,512]{3,2,1,0:T(8,128)S(1)}, f32[6,6,32,512]{3,2,1,0:T(8,128)}, u32[]{:S(2)}) copy-start(f32[6,6,32,512]{3,2,1,0:T(8,128)} %param.8) | copy-start | bytes 7077892
  20.6 2.3 %copy-start.1 = (f32[50,8,512]{2,1,0:T(8,128)}, f32[50,8,512]{2,1,0:T(8,128)S(1)}, u32[]{:S(2)}) copy-start(f32[50,8,512]{2,1,0:T(8,128)S(1)} %collective-permute-done.below_lo.below_hi.below_hbm) | copy-start | bytes 2457604
  25.9 6.8 %collective-permute-start.2 = (f32[4,48,128]{2,1,0:T(8,128)}, f32[4,48,128]{2,1,0:T(8,128)S(1)}, u32[]{:S(2)}, u32[]{:S(2)}) collective-permute-start(f32[4,48,128]{2,1,0:T(8,128)} %get-tuple-element.6), channel_id=1, source_target_pairs={{0,1},{1,2},{2,3},{3,0},{4,5},{5,6},{6,7},{7,4},{8,9},{9,10},{10,1... | collective-permute-start | bytes 294920 | tf_op jit(solution)/shard_map/ppermute | solution.py:224
  29.0 5.6 %collective-permute-start.3 = (f32[4,48,128]{2,1,0:T(8,128)}, f32[4,48,128]{2,1,0:T(8,128)S(1)}, u32[]{:S(2)}, u32[]{:S(2)}) collective-permute-start(f32[4,48,128]{2,1,0:T(8,128)} %get-tuple-element.7), channel_id=1, source_target_pairs={{1,0},{2,1},{3,2},{0,3},{5,4},{6,5},{7,6},{4,7},{9,8},{10,9},{11,1... | collective-permute-start | bytes 294920 | tf_op jit(solution)/shard_map/ppermute | solution.py:225
  34.6 1.1 %copy-start.2 = (f32[50,8,512]{2,1,0:T(8,128)S(1)}, f32[50,8,512]{2,1,0:T(8,128)}, u32[]{:S(2)}) copy-start(f32[50,8,512]{2,1,0:T(8,128)} %copy-done.1) | copy-start | bytes 2457604
  35.7 1.0 %copy-start.4 = (f32[8,32,512]{2,1,0:T(8,128)S(1)}, f32[8,32,512]{2,1,0:T(8,128)}, u32[]{:S(2)}) copy-start(f32[8,32,512]{2,1,0:T(8,128)} %fw_hbm.1) | copy-start | bytes 1572868
  36.8 1.0 %copy-start.6 = (f32[6,32,512]{2,1,0:T(8,128)S(1)}, f32[6,32,512]{2,1,0:T(8,128)}, u32[]{:S(2)}) copy-start(f32[6,32,512]{2,1,0:T(8,128)} %adj_hbm.1) | copy-start | bytes 1179652
  37.8 1.1 %copy-start.7 = (bf16[3,6,32,512]{3,2,1,0:T(8,128)(2,1)S(1)}, bf16[3,6,32,512]{3,2,1,0:T(8,128)(2,1)}, u32[]{:S(2)}) copy-start(bf16[3,6,32,512]{3,2,1,0:T(8,128)(2,1)} %param.12) | copy-start | bytes 1769476
  38.8 28.9 %copy-start.11 = (f32[8,2048]{1,0:T(8,128)S(1)}, f32[8,2048]{1,0:T(8,128)}, u32[]{:S(2)}) copy-start(f32[8,2048]{1,0:T(8,128)} %param.13) | copy-start | bytes 196612
  67.7 26.2 %copy-start.8 = (f32[4,8,2048]{2,1,0:T(8,128)}, f32[4,8,2048]{2,1,0:T(8,128)S(1)}, u32[]{:S(2)}) copy-start(f32[4,8,2048]{2,1,0:T(8,128)S(1)} %pad_maximum_fusion.2.mid_ref) | copy-start | bytes 786436
  67.8 20.6 %collective-permute-start.4 = (f32[4,8,2048]{2,1,0:T(8,128)S(1)}, f32[4,8,2048]{2,1,0:T(8,128)S(1)}, u32[]{:S(2)}, u32[]{:S(2)}) collective-permute-start(f32[4,8,2048]{2,1,0:T(8,128)S(1)} %pad_maximum_fusion.2.mid_ref), channel_id=1, source_target_pairs={{1,0},{2,1},{3,2},{4,3},{5,4},{6,5},{7,6},{8,7},{9,8},{10,9},{11,1... | collective-permute-start | bytes 786440 | tf_op jit(solution)/shard_map/ppermute | solution.py:241
  85.1 8.9 %collective-permute-start.5 = (f32[4,8,2048]{2,1,0:T(8,128)S(1)}, f32[4,8,2048]{2,1,0:T(8,128)S(1)}, u32[]{:S(2)}, u32[]{:S(2)}) collective-permute-start(f32[4,8,2048]{2,1,0:T(8,128)S(1)} %pad_maximum_fusion.2.mid_ref), channel_id=1, source_target_pairs={{0,1},{1,2},{2,3},{3,4},{4,5},{5,6},{6,7},{7,8},{8,9},{9,10},{10,1... | collective-permute-start | bytes 786440 | tf_op jit(solution)/shard_map/ppermute | solution.py:240
  88.4 5.6 %copy-start.9 = (f32[4,8,2048]{2,1,0:T(8,128)}, f32[4,8,2048]{2,1,0:T(8,128)S(1)}, u32[]{:S(2)}) copy-start(f32[4,8,2048]{2,1,0:T(8,128)S(1)} %collective-permute-done.4.above_ref) | copy-start | bytes 786436
  94.0 0.7 copy-start.10

commit v6 on v4

--- a/solution.py
+++ b/solution.py
@@ -127,9 +127,11 @@
 
         def body(t, carry, pin=pin, pout=pout):
             r0 = pl.multiple_of(t * TILE, TILE)
-            win = [pin[g, pl.ds(r0 - TILE, 3 * TILE), :] for g in range(nf)]
-            centre = [w[TILE : 2 * TILE] for w in win]
-            rows = r0 - pad + lax.broadcasted_iota(jnp.int32, (TILE, width), 0)
+            centre = [pin[g, pl.ds(r0, TILE), :] for g in range(nf)]
+            prev = [pin[g, pl.ds(r0 - TILE, TILE), :] for g in range(nf)]
+            nxt = [pin[g, pl.ds(r0 + TILE, TILE), :] for g in range(nf)]
+            sub = lax.broadcasted_iota(jnp.int32, (TILE, width), 0)
+            rows = r0 - pad + sub
             here = (rows + 2 * rows_here) // rows_here
             acc = []
             for f in range(nf):
@@ -140,9 +142,17 @@
             for direction in range(len(offsets_table)):
                 row_step, col_step = offsets_table[direction]
                 if row_step != 0:
-                    shifted = [
-                        pltpu.roll(w, (-row_step) % (3 * TILE), 0)[TILE : 2 * TILE] for w in win
-                    ]
+                    turn = (-row_step) % TILE
+                    if row_step > 0:
+                        shifted = [
+                            jnp.where(sub < TILE - row_step, pltpu.roll(c, turn, 0), pltpu.roll(n, turn, 0))
+                            for c, n in zip(centre, nxt)
+                        ]
+                    else:
+                        shifted = [
+                            jnp.where(sub >= -row_step, pltpu.roll(c, turn, 0), pltpu.roll(b, turn, 0))
+                            for c, b in zip(centre, prev)
+                        ]
                     there = (rows + row_step + 2 * rows_here) // rows_here
                     link = jnp.where(jnp.minimum(here, there) < 2, link_below, link_above)
                     factor = jnp.where(here != there, link, 1.0)

time: 97.1 us -> 96.6 us (level)
  no operation moved by 1% of the time
where the time goes in v6:
time: 96.6 us; the launch traced here: 96 us
  starting transfers between devices  40.1 us (42%)
  Pallas kernels  25.7 us (27%)
  waiting for transfers between devices  11 us (11%)
  blocking collectives  9.28 us (10%)
  local copies, waits for them, and re-layouts  6.33 us (7%)
  between operations  2.19 us (2%)
  other arithmetic  1.38 us (1%)
    pallas_call x1, Pallas kernels, flow_iterations(): pl.pallas_call(flow_kernel, out_shape=jax.ShapeDtypeStruct((nf, rows_here...  18.8 us
    ppermute x1, starting transfers between devices, local(): part_above = lax.ppermute(both, part_axis, backward)  17.4 us
    ppermute x1, starting transfers between devices, local(): lax.ppermute(jnp.concatenate([x[:, :deep] for x in fields], axis=0), 'blk...  9.75 us
    all_to_all x1, blocking collectives, local(): lax.all_to_all(sensitivity, 'sub', split_axis=1, concat_axis=2, tiled=True)  9.28 us
    ppermute x1, waiting for transfers between devices, local(): part_below = lax.ppermute(both, part_axis, forward)  5.6 us
    ppermute x1, starting transfers between devices, local(): lax.ppermute(jnp.concatenate([x[:, rows_here - deep:] for x in fields], a...  4.59 us
    unnamed x29, local copies, waits for them, and re-layouts  3.98 us
    pallas_call x1, Pallas kernels, warp_sweeps(): pl.pallas_call(functools.partial(warp_kernel, part_count), out_shape=jax....  3.76 us
  transfers between devices with their start and end apart: 6, of which 5 were waited for; matrix products, arithmetic and copies ran while one was open for 1% of the time, Pallas kernels for 0%

profile of v6, /device:TPU:1, one launch (start us, length us, event | category | flops | bytes accessed | tf_op | source)
XLA Modules:
  0.0 96.0 jit_solution(2089650791979116472)
XLA Ops:
  0.6 0.0 copy-start.3
  0.6 0.0 copy-start.5
  0.7 1.4 %fusion = (f32[36,8,512]{2,1,0:T(8,128)S(1)}, f32[36,8,512]{2,1,0:T(8,128)S(1)}) fusion(f32[36,32,512]{2,1,0:T(8,128)} %bitcast.13), kind=kLoop, calls=%fused_computation.6 | loop fusion | bytes 2359296 | tf_op jit(solution)/shard_map/slice | solution.py:219
  2.1 0.0 copy-done.3
  2.1 0.0 copy-done.5
  2.2 0.1 pad_maximum_fusion
  2.2 0.0 copy-start.13
  2.2 0.0 copy-start.12
  2.3 4.6 %collective-permute-start = (f32[50,8,512]{2,1,0:T(8,128)S(1)}, f32[50,8,512]{2,1,0:T(8,128)S(1)}, u32[]{:S(2)}, u32[]{:S(2)}) collective-permute-start(f32[50,8,512]{2,1,0:T(8,128)S(1)} %pad_maximum_fusion), channel_id=1, source_target_pairs={{0,4},{4,8},{8,12},{12,16},{16,20},{20,24},{24,28},{28,32},{32,36}... | collective-permute-start | bytes 2457608 | tf_op jit(solution)/shard_map/ppermute | solution.py:216
  6.9 0.1 pad_maximum_fusion.1
  6.9 9.8 %collective-permute-start.1 = (f32[50,8,512]{2,1,0:T(8,128)S(1)}, f32[50,8,512]{2,1,0:T(8,128)}, u32[]{:S(2)}, u32[]{:S(2)}) collective-permute-start(f32[50,8,512]{2,1,0:T(8,128)S(1)} %pad_maximum_fusion.1), channel_id=1, source_target_pairs={{4,0},{8,4},{12,8},{16,12},{20,16},{24,20},{28,24},{32,28},{36,32}... | collective-permute-start | bytes 2457608 | tf_op jit(solution)/shard_map/ppermute | solution.py:219
  16.7 0.0 copy-done.13
  16.7 0.6 fusion.3
  18.6 0.0 copy-done.12
  18.6 0.1 reshape.17.flux_ref
  18.8 0.0 collective-permute-done.below_lo.below_hi.below_hbm
  18.8 0.0 copy-start.1
  18.8 1.9 %collective-permute-done.1.above_lo.above_hi.above_hbm = f32[50,8,512]{2,1,0:T(8,128)} collective-permute-done((f32[50,8,512]{2,1,0:T(8,128)S(1)}, f32[50,8,512]{2,1,0:T(8,128)}, u32[]{:S(2)}, u32[]{:S(2)}) %collective-permute-start.1) | collective-permute-done | bytes 819232 | tf_op jit(solution)/shard_map/ppermute | solution.py:219
  20.7 0.0 copy-done.1
  20.7 0.0 copy-start
  20.7 3.1 %shard_map.86 = (f32[4,48,128]{2,1,0:T(8,128)}, f32[4,48,128]{2,1,0:T(8,128)}) custom-call(f32[6,32,512]{2,1,0:T(8,128)} %adj_hbm.1, f32[6,32,512]{2,1,0:T(8,128)} %adj_hbm.1, f32[36,32,512]{2,1,0:T(8,128)} %bitcast.14, f32[36,32,512]{2,1,0:T(8,128)} %bitcast.15, f32[8,32,512]{2,1,0:T(8,128)} %fw_hbm.1, f32[8,32,512]{2,1,0:T(8,128)} %fw_hbm.1, ...), custom_call_target="tpu_custom_call" | custom-call | tf_op jit(solution)/shard_map/pallas_call | solution.py:72
  23.8 3.1 %collective-permute-start.2 = (f32[4,48,128]{2,1,0:T(8,128)}, f32[4,48,128]{2,1,0:T(8,128)S(1)}, u32[]{:S(2)}, u32[]{:S(2)}) collective-permute-start(f32[4,48,128]{2,1,0:T(8,128)} %get-tuple-element.4), channel_id=1, source_target_pairs={{0,1},{1,2},{2,3},{3,0},{4,5},{5,6},{6,7},{7,4},{8,9},{9,10},{10,1... | collective-permute-start | bytes 294920 | tf_op jit(solution)/shard_map/ppermute | solution.py:224
  26.9 3.4 %collective-permute-start.3 = (f32[4,48,128]{2,1,0:T(8,128)}, f32[4,48,128]{2,1,0:T(8,128)S(1)}, u32[]{:S(2)}, u32[]{:S(2)}) collective-permute-start(f32[4,48,128]{2,1,0:T(8,128)} %get-tuple-element.5), channel_id=1, source_target_pairs={{1,0},{2,1},{3,2},{0,3},{5,4},{6,5},{7,6},{4,7},{9,8},{10,9},{11,1... | collective-permute-start | bytes 294920 | tf_op jit(solution)/shard_map/ppermute | solution.py:225
  30.3 0.1 pad_maximum_fusion.3.link_ref
  30.4 0.2 collective-permute-done.2.left_ref
  30.6 1.9 %collective-permute-done.3.right_ref = f32[4,48,128]{2,1,0:T(8,128)S(1)} collective-permute-done((f32[4,48,128]{2,1,0:T(8,128)}, f32[4,48,128]{2,1,0:T(8,128)S(1)}, u32[]{:S(2)}, u32[]{:S(2)}) %collective-permute-start.3) | collective-permute-done | bytes 98336 | tf_op jit(solution)/shard_map/ppermute | solution.py:225
  32.5 0.0 copy-done
  32.5 0.0 copy-start.2
  32.5 1.1 %copy-done.2 = f32[50,8,512]{2,1,0:T(8,128)S(1)} copy-done((f32[50,8,512]{2,1,0:T(8,128)S(1)}, f32[50,8,512]{2,1,0:T(8,128)}, u32[]{:S(2)}) %copy-start.2) | copy-done | bytes 819224
  33.7 1.0 %copy-done.4 = f32[8,32,512]{2,1,0:T(8,128)S(1)} copy-done((f32[8,32,512]{2,1,0:T(8,128)S(1)}, f32[8,32,512]{2,1,0:T(8,128)}, u32[]{:S(2)}) %copy-start.4) | copy-done | bytes 524312
  34.7 1.0 %copy-done.6 = f32[6,32,512]{2,1,0:T(8,128)S(1)} copy-done((f32[6,32,512]{2,1,0:T(8,128)S(1)}, f32[6,32,512]{2,1,0:T(8,128)}, u32[]{:S(2)}) %copy-start.6) | copy-done | bytes 393240
  35.7 18.8 %shard_map.87 = f32[6,32,512]{2,1,0:T(8,128)} custom-call(f32[288]{0:T(512)S(1)} %reshape.17.flux_ref, f32[2]{0:T(128)S(1)} %pad_maximum_fusion.3.link_ref, f32[6,32,512]{2,1,0:T(8,128)S(1)} %copy-done.6, f32[36,32,512]{2,1,0:T(8,128)S(1)} %bitcast.16, f32[8,32,512]{2,1,0:T(8,128)S(1)} %copy-done.4, f32[50,8,512]{2,1,0:T(8,128)S(1)} %copy-done.2, ...), custom_call_target="tpu_custom_call" | custom-call | tf_op jit(solution)/shard_map/pallas_call | solution.py:183
  54.6 0.0 copy-done.8
  54.6 0.0 copy-start.11
  54.6 1.2 %multiply_reduce_fusion = f32[32,512,3]{1,0,2:T(8,128)S(1)} fusion(f32[32,512,6]{1,0,2:T(8,128)} %bitcast.17, bf16[3,6,32,512]{3,2,1,0:T(8,128)(2,1)S(1)} %copy-done.8), kind=kLoop, calls=%fused_computation | loop fusion | flops 835584 | bytes 1179648
  55.8 0.1 copy.22
  55.9 9.3 %all_to_all.18 = f32[3,32,512]{2,0,1:T(4,128)S(1)} all-to-all(f32[3,32,512]{2,0,1:T(4,128)S(1)} %bitcast.18), channel_id=1, replica_groups=mesh['blk'=192,'sub'=4] {'sub'}, dimensions={1} | all-to-all | bytes 393216 | tf_op jit(solution)/shard_map/all_to_all | solution.py:235
  65.2 0.1 copy.11
  65.2 0.0 copy-done.11
  65.3 0.0 copy-start.7
  65.3 17.4 %collective-permute-start.4 = (f32[4,8,2048]{2,1,0:T(8,128)S(1)}, f32[4,8,2048]{2,1,0:T(8,128)S(1)}, u32[]{:S(2)}, u32[]{:S(2)}) collective-permute-start(f32[4,8,2048]{2,1,0:T(8,128)S(1)} %pad_maximum_fusion.2.mid_ref), channel_id=1, source_target_pairs={{1,0},{2,1},{3,2},{4,3},{5,4},{6,5},{7,6},{8,7},{9,8},{10,9},{11,1... | collective-permute-start | bytes 786440 | tf_op jit(solution)/shard_map/ppermute | solution.py:244
  82.7 1.9 %collective-permute-start.5 = (f32[4,8,2048]{2,1,0:T(8,128)S(1)}, f32[4,8,2048]{2,1,0:T(8,128)S(1)}, u32[]{:S(2)}, u32[]{:S(2)}) collective-permute-start(f32[4,8,2048]{2,1,0:T(8,128)S(1)} %pad_maximum_fusion.2.mid_ref), channel_id=1, source_target_pairs={{0,1},{1,2},{2,3},{3,4},{4,5},{5,6},{6,7},{7,8},{8,9},{9,10},{10,1... | collective-permute-start | bytes 786440 | tf_op jit(solution)/shard_map/ppermute | solution.py:243
  84.6 1.4 %collective-permute-done.4.above_ref = f32[4,8,2048]{2,1,0:T(8,128)S(1)} collective-permute-done((f32[4,8,2048]{2,1,0:T(8,128)S(1)}, f32[4,8,2048]{2,1,0:T(8,128)S(1)}, u32[]{:S(2)}, u32[]{:S(2)}) %collective-permute-start.4) | collective-permute-done | bytes 262176 | tf_op jit(solution)/shard_map/ppermute | solution.py:244
  86.0 5.6 %collective-permute-done.5.below_ref = f32[4,8,2048]{2,1,0:T(8,128)S(1)} collective-permute-done((f32[4,8,2048]{2,1,0:T(8,128)S(1)}, f32[4,8,2048]{2,1,0:T(8,128)S(1)}, u32[]{:S(2)}, u32[]{:S(2)}) %collective-permute-start.5) | collective-permute-done | bytes 262176 | tf_op jit(solution)/shard_map/ppermute | solution.py:243
  91.6 0.0 copy-done.7
  91.6 0.0 copy-done.9
  91.6 0.7 copy-done.10
  92.3 3.8 %shard_map.88 = f32[3,8,2048]{2,1,0:T(8,128)} custom-call(s32[1]{0:T(128)} %bitcast.3.index_ref, f32[4,8,2048]{2,1,0:T(8,128)} %copy-done.7, f32[4,8,2048]{2,1,0:T(8,128)} %copy-done.9, f32[4,8,2048]{2,1,0:T(8,128)} %copy-done.10), custom_call_target="tpu_custom_call" | custom-call | tf_op jit(solution)/shard_map/pallas_call | solution.py:283
  (9 shorter events, 0.1 us)
Async XLA Ops:
  0.6 1.4 %copy-start.3 = (f32[8,32,512]{2,1,0:T(8,128)S(1)}, f32[8,32,512]{2,1,0:T(8,128)}, u32[]{:S(2)}) copy-start(f32[8,32,512]{2,1,0:T(8,128)} %fw_hbm.1) | copy-start | bytes 1572868
  0.6 1.5 %copy-start.5 = (f32[6,32,512]{2,1,0:T(8,128)S(1)}, f32[6,32,512]{2,1,0:T(8,128)}, u32[]{:S(2)}) copy-start(f32[6,32,512]{2,1,0:T(8,128)} %adj_hbm.1) | copy-start | bytes 1179652
  2.2 14.5 %copy-start.13 = (s32[192]{0:T(256)S(1)}, s32[192]{0:T(256)}, u32[]{:S(2)}) copy-start(s32[192]{0:T(256)} %param.11) | copy-start | bytes 2308
  2.2 16.4 %copy-start.12 = (f32[8,6,6]{2,0,1:T(8,128)S(1)}, f32[8,6,6]{2,0,1:T(8,128)}, u32[]{:S(2)}) copy-start(f32[8,6,6]{2,0,1:T(8,128)} %param.10) | copy-start | bytes 3460
  2.3 16.5 %collective-permute-start = (f32[50,8,512]{2,1,0:T(8,128)S(1)}, f32[50,8,512]{2,1,0:T(8,128)S(1)}, u32[]{:S(2)}, u32[]{:S(2)}) collective-permute-start(f32[50,8,512]{2,1,0:T(8,128)S(1)} %pad_maximum_fusion), channel_id=1, source_target_pairs={{0,4},{4,8},{8,12},{12,16},{16,20},{20,24},{24,28},{28,32},{32,36}... | collective-permute-start | bytes 2457608 | tf_op jit(solution)/shard_map/ppermute | solution.py:216
  6.9 13.8 %collective-permute-start.1 = (f32[50,8,512]{2,1,0:T(8,128)S(1)}, f32[50,8,512]{2,1,0:T(8,128)}, u32[]{:S(2)}, u32[]{:S(2)}) collective-permute-start(f32[50,8,512]{2,1,0:T(8,128)S(1)} %pad_maximum_fusion.1), channel_id=1, source_target_pairs={{4,0},{8,4},{12,8},{16,12},{20,16},{24,20},{28,24},{32,28},{36,32}... | collective-permute-start | bytes 2457608 | tf_op jit(solution)/shard_map/ppermute | solution.py:219
  18.8 1.9 %copy-start.1 = (f32[50,8,512]{2,1,0:T(8,128)}, f32[50,8,512]{2,1,0:T(8,128)S(1)}, u32[]{:S(2)}) copy-start(f32[50,8,512]{2,1,0:T(8,128)S(1)} %collective-permute-done.below_lo.below_hi.below_hbm) | copy-start | bytes 2457604
  20.7 11.8 %copy-start = (f32[6,6,32,512]{3,2,1,0:T(8,128)S(1)}, f32[6,6,32,512]{3,2,1,0:T(8,128)}, u32[]{:S(2)}) copy-start(f32[6,6,32,512]{3,2,1,0:T(8,128)} %param.8) | copy-start | bytes 7077892
  23.8 6.8 %collective-permute-start.2 = (f32[4,48,128]{2,1,0:T(8,128)}, f32[4,48,128]{2,1,0:T(8,128)S(1)}, u32[]{:S(2)}, u32[]{:S(2)}) collective-permute-start(f32[4,48,128]{2,1,0:T(8,128)} %get-tuple-element.4), channel_id=1, source_target_pairs={{0,1},{1,2},{2,3},{3,0},{4,5},{5,6},{6,7},{7,4},{8,9},{9,10},{10,1... | collective-permute-start | bytes 294920 | tf_op jit(solution)/shard_map/ppermute | solution.py:224
  26.9 5.6 %collective-permute-start.3 = (f32[4,48,128]{2,1,0:T(8,128)}, f32[4,48,128]{2,1,0:T(8,128)S(1)}, u32[]{:S(2)}, u32[]{:S(2)}) collective-permute-start(f32[4,48,128]{2,1,0:T(8,128)} %get-tuple-element.5), channel_id=1, source_target_pairs={{1,0},{2,1},{3,2},{0,3},{5,4},{6,5},{7,6},{4,7},{9,8},{10,9},{11,1... | collective-permute-start | bytes 294920 | tf_op jit(solution)/shard_map/ppermute | solution.py:225
  32.5 1.1 %copy-start.2 = (f32[50,8,512]{2,1,0:T(8,128)S(1)}, f32[50,8,512]{2,1,0:T(8,128)}, u32[]{:S(2)}) copy-start(f32[50,8,512]{2,1,0:T(8,128)} %copy-done.1) | copy-start | bytes 2457604
  33.7 1.0 %copy-start.4 = (f32[8,32,512]{2,1,0:T(8,128)S(1)}, f32[8,32,512]{2,1,0:T(8,128)}, u32[]{:S(2)}) copy-start(f32[8,32,512]{2,1,0:T(8,128)} %fw_hbm.1) | copy-start | bytes 1572868
  34.7 1.0 %copy-start.6 = (f32[6,32,512]{2,1,0:T(8,128)S(1)}, f32[6,32,512]{2,1,0:T(8,128)}, u32[]{:S(2)}) copy-start(f32[6,32,512]{2,1,0:T(8,128)} %adj_hbm.1) | copy-start | bytes 1179652
  35.7 18.9 %copy-start.8 = (bf16[3,6,32,512]{3,2,1,0:T(8,128)(2,1)S(1)}, bf16[3,6,32,512]{3,2,1,0:T(8,128)(2,1)}, u32[]{:S(2)}) copy-start(bf16[3,6,32,512]{3,2,1,0:T(8,128)(2,1)} %param.12) | copy-start | bytes 1769476
  54.6 10.7 %copy-start.11 = (f32[8,2048]{1,0:T(8,128)S(1)}, f32[8,2048]{1,0:T(8,128)}, u32[]{:S(2)}) copy-start(f32[8,2048]{1,0:T(8,128)} %param.13) | copy-start | bytes 196612
  65.3 26.3 %copy-start.7 = (f32[4,8,2048]{2,1,0:T(8,128)}, f32[4,8,2048]{2,1,0:T(8,128)S(1)}, u32[]{:S(2)}) copy-start(f32[4,8,2048]{2,1,0:T(8,128)S(1)} %pad_maximum_fusion.2.mid_ref) | copy-start | bytes 786436
  65.3 20.7 %collective-permute-start.4 = (f32[4,8,2048]{2,1,0:T(8,128)S(1)}, f32[4,8,2048]{2,1,0:T(8,128)S(1)}, u32[]{:S(2)}, u32[]{:S(2)}) collective-permute-start(f32[4,8,2048]{2,1,0:T(8,128)S(1)} %pad_maximum_fusion.2.mid_ref), channel_id=1, source_target_pairs={{1,0},{2,1},{3,2},{4,3},{5,4},{6,5},{7,6},{8,7},{9,8},{10,9},{11,1... | collective-permute-start | bytes 786440 | tf_op jit(solution)/shard_map/ppermute | solution.py:244
  82.7 8.9 %collective-permute-start.5 = (f32[4,8,2048]{2,1,0:T(8,128)S(1)}, f32[4,8,2048]{2,1,0:T(8,128)S(1)}, u32[]{:S(2)}, u32[]{:S(2)}) collective-permute-start(f32[4,8,2048]{2,1,0:T(8,128)S(1)} %pad_maximum_fusion.2.mid_ref), channel_id=1, source_target_pairs={{0,1},{1,2},{2,3},{3,4},{4,5},{5,6},{6,7},{7,8},{8,9},{9,10},{10,1... | collective-permute-start | bytes 786440 | tf_op jit(solution)/shard_map/ppermute | solution.py:243
  86.0 5.6 %copy-start.9 = (f32[4,8,2048]{2,1,0:T(8,128)}, f32[4,8,2048]{2,1,0:T(8,128)S(1)}, u32[]{:S(2)}) copy-start(f32[4,8,2048]{2,1,0:T(8,128)S(1)} %collective-permute-done.4.above_ref) | copy-start | bytes 786436
  91.6 0.7 copy-start.10

commit v7 on v6

--- a/solution.py
+++ b/solution.py
@@ -156,10 +156,11 @@
                     there = (rows + row_step + 2 * rows_here) // rows_here
                     link = jnp.where(jnp.minimum(here, there) < 2, link_below, link_above)
                     factor = jnp.where(here != there, link, 1.0)
-                    shifted = [x * factor for x in shifted]
                 else:
                     shifted = [pltpu.roll(c, (-col_step) % width, 1) for c in centre]
                 weight = tile_ref[fw0 + direction, pl.ds(r0, TILE), :]
+                if row_step != 0:
+                    weight = weight * factor
                 for f in range(nf):
                     base = direction * nf * nf + f * nf
                     mixed = flux_ref[base] * shifted[0]
@@ -263,8 +264,8 @@
     root_stiff = jnp.sqrt(stiff)
     scale_term = couple_factor / root_stiff
     base_term = [field(c) / stiff for c in range(ncomp)]
-    warp = [jnp.zeros((tall_rows, cols), jnp.float32) for c in range(ncomp)]
-    for sweep_index in range(SWEEPS):
+    warp = list(base_term)
+    for sweep_index in range(1, SWEEPS):
         for c in range(ncomp):
             spread = jnp.where(valid, root_stiff * warp[c], 0.0)
             beside_all = (

time: 96.6 us -> 96.1 us (level)
  no operation moved by 1% of the time
where the time goes in v7:
time: 96.1 us; the launch traced here: 95.5 us
  starting transfers between devices  40.1 us (42%)
  Pallas kernels  25.2 us (26%)
  waiting for transfers between devices  11 us (11%)
  blocking collectives  9.28 us (10%)
  local copies, waits for them, and re-layouts  6.33 us (7%)
  between operations  2.19 us (2%)
  other arithmetic  1.38 us (1%)
    pallas_call x1, Pallas kernels, flow_iterations(): pl.pallas_call(flow_kernel, out_shape=jax.ShapeDtypeStruct((nf, rows_here...  18.5 us
    ppermute x1, starting transfers between devices, local(): part_above = lax.ppermute(both, part_axis, backward)  17.4 us
    ppermute x1, starting transfers between devices, local(): lax.ppermute(jnp.concatenate([x[:, :deep] for x in fields], axis=0), 'blk...  9.75 us
    all_to_all x1, blocking collectives, local(): lax.all_to_all(sensitivity, 'sub', split_axis=1, concat_axis=2, tiled=True)  9.28 us
    ppermute x1, waiting for transfers between devices, local(): part_below = lax.ppermute(both, part_axis, forward)  5.6 us
    ppermute x1, starting transfers between devices, local(): lax.ppermute(jnp.concatenate([x[:, rows_here - deep:] for x in fields], a...  4.59 us
    unnamed x29, local copies, waits for them, and re-layouts  3.98 us
    pallas_call x1, Pallas kernels, warp_sweeps(): pl.pallas_call(functools.partial(warp_kernel, part_count), out_shape=jax....  3.6 us
  transfers between devices with their start and end apart: 6, of which 5 were waited for; matrix products, arithmetic and copies ran while one was open for 1% of the time, Pallas kernels for 0%

profile of v7, /device:TPU:1, one launch (start us, length us, event | category | flops | bytes accessed | tf_op | source)
XLA Modules:
  0.0 95.5 jit_solution(8541567760784209637)
XLA Ops:
  0.6 0.0 copy-start.3
  0.6 0.0 copy-start.5
  0.7 1.4 %fusion = (f32[36,8,512]{2,1,0:T(8,128)S(1)}, f32[36,8,512]{2,1,0:T(8,128)S(1)}) fusion(f32[36,32,512]{2,1,0:T(8,128)} %bitcast.13), kind=kLoop, calls=%fused_computation.6 | loop fusion | bytes 2359296 | tf_op jit(solution)/shard_map/slice | solution.py:220
  2.1 0.0 copy-done.3
  2.1 0.0 copy-done.5
  2.2 0.1 pad_maximum_fusion
  2.2 0.0 copy-start.13
  2.2 0.0 copy-start.12
  2.3 4.6 %collective-permute-start = (f32[50,8,512]{2,1,0:T(8,128)S(1)}, f32[50,8,512]{2,1,0:T(8,128)S(1)}, u32[]{:S(2)}, u32[]{:S(2)}) collective-permute-start(f32[50,8,512]{2,1,0:T(8,128)S(1)} %pad_maximum_fusion), channel_id=1, source_target_pairs={{0,4},{4,8},{8,12},{12,16},{16,20},{20,24},{24,28},{28,32},{32,36}... | collective-permute-start | bytes 2457608 | tf_op jit(solution)/shard_map/ppermute | solution.py:217
  6.9 0.1 pad_maximum_fusion.1
  6.9 9.8 %collective-permute-start.1 = (f32[50,8,512]{2,1,0:T(8,128)S(1)}, f32[50,8,512]{2,1,0:T(8,128)}, u32[]{:S(2)}, u32[]{:S(2)}) collective-permute-start(f32[50,8,512]{2,1,0:T(8,128)S(1)} %pad_maximum_fusion.1), channel_id=1, source_target_pairs={{4,0},{8,4},{12,8},{16,12},{20,16},{24,20},{28,24},{32,28},{36,32}... | collective-permute-start | bytes 2457608 | tf_op jit(solution)/shard_map/ppermute | solution.py:220
  16.7 0.0 copy-done.13
  16.7 0.6 fusion.3
  18.6 0.0 copy-done.12
  18.6 0.1 reshape.17.flux_ref
  18.8 0.0 collective-permute-done.below_lo.below_hi.below_hbm
  18.8 0.0 copy-start.1
  18.8 1.9 %collective-permute-done.1.above_lo.above_hi.above_hbm = f32[50,8,512]{2,1,0:T(8,128)} collective-permute-done((f32[50,8,512]{2,1,0:T(8,128)S(1)}, f32[50,8,512]{2,1,0:T(8,128)}, u32[]{:S(2)}, u32[]{:S(2)}) %collective-permute-start.1) | collective-permute-done | bytes 819232 | tf_op jit(solution)/shard_map/ppermute | solution.py:220
  20.7 0.0 copy-done.1
  20.7 0.0 copy-start
  20.7 3.1 %shard_map.86 = (f32[4,48,128]{2,1,0:T(8,128)}, f32[4,48,128]{2,1,0:T(8,128)}) custom-call(f32[6,32,512]{2,1,0:T(8,128)} %adj_hbm.1, f32[6,32,512]{2,1,0:T(8,128)} %adj_hbm.1, f32[36,32,512]{2,1,0:T(8,128)} %bitcast.14, f32[36,32,512]{2,1,0:T(8,128)} %bitcast.15, f32[8,32,512]{2,1,0:T(8,128)} %fw_hbm.1, f32[8,32,512]{2,1,0:T(8,128)} %fw_hbm.1, ...), custom_call_target="tpu_custom_call" | custom-call | tf_op jit(solution)/shard_map/pallas_call | solution.py:72
  23.8 3.1 %collective-permute-start.2 = (f32[4,48,128]{2,1,0:T(8,128)}, f32[4,48,128]{2,1,0:T(8,128)S(1)}, u32[]{:S(2)}, u32[]{:S(2)}) collective-permute-start(f32[4,48,128]{2,1,0:T(8,128)} %get-tuple-element.4), channel_id=1, source_target_pairs={{0,1},{1,2},{2,3},{3,0},{4,5},{5,6},{6,7},{7,4},{8,9},{9,10},{10,1... | collective-permute-start | bytes 294920 | tf_op jit(solution)/shard_map/ppermute | solution.py:225
  26.9 3.4 %collective-permute-start.3 = (f32[4,48,128]{2,1,0:T(8,128)}, f32[4,48,128]{2,1,0:T(8,128)S(1)}, u32[]{:S(2)}, u32[]{:S(2)}) collective-permute-start(f32[4,48,128]{2,1,0:T(8,128)} %get-tuple-element.5), channel_id=1, source_target_pairs={{1,0},{2,1},{3,2},{0,3},{5,4},{6,5},{7,6},{4,7},{9,8},{10,9},{11,1... | collective-permute-start | bytes 294920 | tf_op jit(solution)/shard_map/ppermute | solution.py:226
  30.3 0.1 pad_maximum_fusion.3.link_ref
  30.4 0.2 collective-permute-done.2.left_ref
  30.6 1.9 %collective-permute-done.3.right_ref = f32[4,48,128]{2,1,0:T(8,128)S(1)} collective-permute-done((f32[4,48,128]{2,1,0:T(8,128)}, f32[4,48,128]{2,1,0:T(8,128)S(1)}, u32[]{:S(2)}, u32[]{:S(2)}) %collective-permute-start.3) | collective-permute-done | bytes 98336 | tf_op jit(solution)/shard_map/ppermute | solution.py:226
  32.5 0.0 copy-done
  32.5 0.0 copy-start.2
  32.5 1.1 %copy-done.2 = f32[50,8,512]{2,1,0:T(8,128)S(1)} copy-done((f32[50,8,512]{2,1,0:T(8,128)S(1)}, f32[50,8,512]{2,1,0:T(8,128)}, u32[]{:S(2)}) %copy-start.2) | copy-done | bytes 819224
  33.7 1.0 %copy-done.4 = f32[8,32,512]{2,1,0:T(8,128)S(1)} copy-done((f32[8,32,512]{2,1,0:T(8,128)S(1)}, f32[8,32,512]{2,1,0:T(8,128)}, u32[]{:S(2)}) %copy-start.4) | copy-done | bytes 524312
  34.7 1.0 %copy-done.6 = f32[6,32,512]{2,1,0:T(8,128)S(1)} copy-done((f32[6,32,512]{2,1,0:T(8,128)S(1)}, f32[6,32,512]{2,1,0:T(8,128)}, u32[]{:S(2)}) %copy-start.6) | copy-done | bytes 393240
  35.7 18.5 %shard_map.87 = f32[6,32,512]{2,1,0:T(8,128)} custom-call(f32[288]{0:T(512)S(1)} %reshape.17.flux_ref, f32[2]{0:T(128)S(1)} %pad_maximum_fusion.3.link_ref, f32[6,32,512]{2,1,0:T(8,128)S(1)} %copy-done.6, f32[36,32,512]{2,1,0:T(8,128)S(1)} %bitcast.16, f32[8,32,512]{2,1,0:T(8,128)S(1)} %copy-done.4, f32[50,8,512]{2,1,0:T(8,128)S(1)} %copy-done.2, ...), custom_call_target="tpu_custom_call" | custom-call | tf_op jit(solution)/shard_map/pallas_call | solution.py:184
  54.2 0.0 copy-done.8
  54.2 0.0 copy-start.11
  54.2 1.2 %multiply_reduce_fusion = f32[32,512,3]{1,0,2:T(8,128)S(1)} fusion(f32[32,512,6]{1,0,2:T(8,128)} %bitcast.17, bf16[3,6,32,512]{3,2,1,0:T(8,128)(2,1)S(1)} %copy-done.8), kind=kLoop, calls=%fused_computation | loop fusion | flops 835584 | bytes 1179648
  55.4 0.1 copy.22
  55.5 9.3 %all_to_all.18 = f32[3,32,512]{2,0,1:T(4,128)S(1)} all-to-all(f32[3,32,512]{2,0,1:T(4,128)S(1)} %bitcast.18), channel_id=1, replica_groups=mesh['blk'=192,'sub'=4] {'sub'}, dimensions={1} | all-to-all | bytes 393216 | tf_op jit(solution)/shard_map/all_to_all | solution.py:236
  64.8 0.1 copy.11
  64.9 0.0 copy-done.11
  64.9 0.0 copy-start.7
  64.9 17.4 %collective-permute-start.4 = (f32[4,8,2048]{2,1,0:T(8,128)S(1)}, f32[4,8,2048]{2,1,0:T(8,128)S(1)}, u32[]{:S(2)}, u32[]{:S(2)}) collective-permute-start(f32[4,8,2048]{2,1,0:T(8,128)S(1)} %pad_maximum_fusion.2.mid_ref), channel_id=1, source_target_pairs={{1,0},{2,1},{3,2},{4,3},{5,4},{6,5},{7,6},{8,7},{9,8},{10,9},{11,1... | collective-permute-start | bytes 786440 | tf_op jit(solution)/shard_map/ppermute | solution.py:245
  82.3 1.9 %collective-permute-start.5 = (f32[4,8,2048]{2,1,0:T(8,128)S(1)}, f32[4,8,2048]{2,1,0:T(8,128)S(1)}, u32[]{:S(2)}, u32[]{:S(2)}) collective-permute-start(f32[4,8,2048]{2,1,0:T(8,128)S(1)} %pad_maximum_fusion.2.mid_ref), channel_id=1, source_target_pairs={{0,1},{1,2},{2,3},{3,4},{4,5},{5,6},{6,7},{7,8},{8,9},{9,10},{10,1... | collective-permute-start | bytes 786440 | tf_op jit(solution)/shard_map/ppermute | solution.py:244
  84.3 1.4 %collective-permute-done.4.above_ref = f32[4,8,2048]{2,1,0:T(8,128)S(1)} collective-permute-done((f32[4,8,2048]{2,1,0:T(8,128)S(1)}, f32[4,8,2048]{2,1,0:T(8,128)S(1)}, u32[]{:S(2)}, u32[]{:S(2)}) %collective-permute-start.4) | collective-permute-done | bytes 262176 | tf_op jit(solution)/shard_map/ppermute | solution.py:245
  85.6 5.6 %collective-permute-done.5.below_ref = f32[4,8,2048]{2,1,0:T(8,128)S(1)} collective-permute-done((f32[4,8,2048]{2,1,0:T(8,128)S(1)}, f32[4,8,2048]{2,1,0:T(8,128)S(1)}, u32[]{:S(2)}, u32[]{:S(2)}) %collective-permute-start.5) | collective-permute-done | bytes 262176 | tf_op jit(solution)/shard_map/ppermute | solution.py:244
  91.2 0.0 copy-done.7
  91.2 0.0 copy-done.9
  91.2 0.7 copy-done.10
  91.9 3.6 %shard_map.88 = f32[3,8,2048]{2,1,0:T(8,128)} custom-call(s32[1]{0:T(128)} %bitcast.3.index_ref, f32[4,8,2048]{2,1,0:T(8,128)} %copy-done.7, f32[4,8,2048]{2,1,0:T(8,128)} %copy-done.9, f32[4,8,2048]{2,1,0:T(8,128)} %copy-done.10), custom_call_target="tpu_custom_call" | custom-call | tf_op jit(solution)/shard_map/pallas_call | solution.py:284
  (9 shorter events, 0.1 us)
Async XLA Ops:
  0.6 1.4 %copy-start.3 = (f32[8,32,512]{2,1,0:T(8,128)S(1)}, f32[8,32,512]{2,1,0:T(8,128)}, u32[]{:S(2)}) copy-start(f32[8,32,512]{2,1,0:T(8,128)} %fw_hbm.1) | copy-start | bytes 1572868
  0.6 1.5 %copy-start.5 = (f32[6,32,512]{2,1,0:T(8,128)S(1)}, f32[6,32,512]{2,1,0:T(8,128)}, u32[]{:S(2)}) copy-start(f32[6,32,512]{2,1,0:T(8,128)} %adj_hbm.1) | copy-start | bytes 1179652
  2.2 14.5 %copy-start.13 = (s32[192]{0:T(256)S(1)}, s32[192]{0:T(256)}, u32[]{:S(2)}) copy-start(s32[192]{0:T(256)} %param.11) | copy-start | bytes 2308
  2.2 16.4 %copy-start.12 = (f32[8,6,6]{2,0,1:T(8,128)S(1)}, f32[8,6,6]{2,0,1:T(8,128)}, u32[]{:S(2)}) copy-start(f32[8,6,6]{2,0,1:T(8,128)} %param.10) | copy-start | bytes 3460
  2.3 16.5 %collective-permute-start = (f32[50,8,512]{2,1,0:T(8,128)S(1)}, f32[50,8,512]{2,1,0:T(8,128)S(1)}, u32[]{:S(2)}, u32[]{:S(2)}) collective-permute-start(f32[50,8,512]{2,1,0:T(8,128)S(1)} %pad_maximum_fusion), channel_id=1, source_target_pairs={{0,4},{4,8},{8,12},{12,16},{16,20},{20,24},{24,28},{28,32},{32,36}... | collective-permute-start | bytes 2457608 | tf_op jit(solution)/shard_map/ppermute | solution.py:217
  6.9 13.8 %collective-permute-start.1 = (f32[50,8,512]{2,1,0:T(8,128)S(1)}, f32[50,8,512]{2,1,0:T(8,128)}, u32[]{:S(2)}, u32[]{:S(2)}) collective-permute-start(f32[50,8,512]{2,1,0:T(8,128)S(1)} %pad_maximum_fusion.1), channel_id=1, source_target_pairs={{4,0},{8,4},{12,8},{16,12},{20,16},{24,20},{28,24},{32,28},{36,32}... | collective-permute-start | bytes 2457608 | tf_op jit(solution)/shard_map/ppermute | solution.py:220
  18.8 1.9 %copy-start.1 = (f32[50,8,512]{2,1,0:T(8,128)}, f32[50,8,512]{2,1,0:T(8,128)S(1)}, u32[]{:S(2)}) copy-start(f32[50,8,512]{2,1,0:T(8,128)S(1)} %collective-permute-done.below_lo.below_hi.below_hbm) | copy-start | bytes 2457604
  20.7 11.8 %copy-start = (f32[6,6,32,512]{3,2,1,0:T(8,128)S(1)}, f32[6,6,32,512]{3,2,1,0:T(8,128)}, u32[]{:S(2)}) copy-start(f32[6,6,32,512]{3,2,1,0:T(8,128)} %param.8) | copy-start | bytes 7077892
  23.8 6.8 %collective-permute-start.2 = (f32[4,48,128]{2,1,0:T(8,128)}, f32[4,48,128]{2,1,0:T(8,128)S(1)}, u32[]{:S(2)}, u32[]{:S(2)}) collective-permute-start(f32[4,48,128]{2,1,0:T(8,128)} %get-tuple-element.4), channel_id=1, source_target_pairs={{0,1},{1,2},{2,3},{3,0},{4,5},{5,6},{6,7},{7,4},{8,9},{9,10},{10,1... | collective-permute-start | bytes 294920 | tf_op jit(solution)/shard_map/ppermute | solution.py:225
  26.9 5.6 %collective-permute-start.3 = (f32[4,48,128]{2,1,0:T(8,128)}, f32[4,48,128]{2,1,0:T(8,128)S(1)}, u32[]{:S(2)}, u32[]{:S(2)}) collective-permute-start(f32[4,48,128]{2,1,0:T(8,128)} %get-tuple-element.5), channel_id=1, source_target_pairs={{1,0},{2,1},{3,2},{0,3},{5,4},{6,5},{7,6},{4,7},{9,8},{10,9},{11,1... | collective-permute-start | bytes 294920 | tf_op jit(solution)/shard_map/ppermute | solution.py:226
  32.5 1.1 %copy-start.2 = (f32[50,8,512]{2,1,0:T(8,128)S(1)}, f32[50,8,512]{2,1,0:T(8,128)}, u32[]{:S(2)}) copy-start(f32[50,8,512]{2,1,0:T(8,128)} %copy-done.1) | copy-start | bytes 2457604
  33.7 1.0 %copy-start.4 = (f32[8,32,512]{2,1,0:T(8,128)S(1)}, f32[8,32,512]{2,1,0:T(8,128)}, u32[]{:S(2)}) copy-start(f32[8,32,512]{2,1,0:T(8,128)} %fw_hbm.1) | copy-start | bytes 1572868
  34.7 1.0 %copy-start.6 = (f32[6,32,512]{2,1,0:T(8,128)S(1)}, f32[6,32,512]{2,1,0:T(8,128)}, u32[]{:S(2)}) copy-start(f32[6,32,512]{2,1,0:T(8,128)} %adj_hbm.1) | copy-start | bytes 1179652
  35.7 18.5 %copy-start.8 = (bf16[3,6,32,512]{3,2,1,0:T(8,128)(2,1)S(1)}, bf16[3,6,32,512]{3,2,1,0:T(8,128)(2,1)}, u32[]{:S(2)}) copy-start(bf16[3,6,32,512]{3,2,1,0:T(8,128)(2,1)} %param.12) | copy-start | bytes 1769476
  54.2 10.7 %copy-start.11 = (f32[8,2048]{1,0:T(8,128)S(1)}, f32[8,2048]{1,0:T(8,128)}, u32[]{:S(2)}) copy-start(f32[8,2048]{1,0:T(8,128)} %param.13) | copy-start | bytes 196612
  64.9 26.3 %copy-start.7 = (f32[4,8,2048]{2,1,0:T(8,128)}, f32[4,8,2048]{2,1,0:T(8,128)S(1)}, u32[]{:S(2)}) copy-start(f32[4,8,2048]{2,1,0:T(8,128)S(1)} %pad_maximum_fusion.2.mid_ref) | copy-start | bytes 786436
  64.9 20.7 %collective-permute-start.4 = (f32[4,8,2048]{2,1,0:T(8,128)S(1)}, f32[4,8,2048]{2,1,0:T(8,128)S(1)}, u32[]{:S(2)}, u32[]{:S(2)}) collective-permute-start(f32[4,8,2048]{2,1,0:T(8,128)S(1)} %pad_maximum_fusion.2.mid_ref), channel_id=1, source_target_pairs={{1,0},{2,1},{3,2},{4,3},{5,4},{6,5},{7,6},{8,7},{9,8},{10,9},{11,1... | collective-permute-start | bytes 786440 | tf_op jit(solution)/shard_map/ppermute | solution.py:245
  82.3 8.9 %collective-permute-start.5 = (f32[4,8,2048]{2,1,0:T(8,128)S(1)}, f32[4,8,2048]{2,1,0:T(8,128)S(1)}, u32[]{:S(2)}, u32[]{:S(2)}) collective-permute-start(f32[4,8,2048]{2,1,0:T(8,128)S(1)} %pad_maximum_fusion.2.mid_ref), channel_id=1, source_target_pairs={{0,1},{1,2},{2,3},{3,4},{4,5},{5,6},{6,7},{7,8},{8,9},{9,10},{10,1... | collective-permute-start | bytes 786440 | tf_op jit(solution)/shard_map/ppermute | solution.py:244
  85.6 5.6 %copy-start.9 = (f32[4,8,2048]{2,1,0:T(8,128)}, f32[4,8,2048]{2,1,0:T(8,128)S(1)}, u32[]{:S(2)}) copy-start(f32[4,8,2048]{2,1,0:T(8,128)S(1)} %collective-permute-done.4.above_ref) | copy-start | bytes 786436
  91.2 0.7 copy-start.10

commit v8 on v7

--- a/solution.py
+++ b/solution.py
@@ -34,24 +34,33 @@
                 low_ref, high_ref):
     strip = low_ref.shape[2] // STRIPS
     lanes = low_ref.shape[2]
-    lane = lax.broadcasted_iota(jnp.int32, low_ref.shape[1:], 1)
-    low = [jnp.zeros(low_ref.shape[1:], jnp.float32) for _ in range(low_ref.shape[0])]
-    high = [jnp.zeros(high_ref.shape[1:], jnp.float32) for _ in range(high_ref.shape[0])]
-    index = 0
-    for lo_ref, hi_ref in ((adj_lo, adj_hi), (jd_lo, jd_hi), (fw_lo, fw_hi)):
-        for f in range(lo_ref.shape[0]):
-            group, slot = divmod(index, STRIPS)
-            lo = jnp.concatenate([below_lo[index], lo_ref[f], above_lo[index]], axis=0)
-            hi = jnp.concatenate([below_hi[index], hi_ref[f], above_hi[index]], axis=0)
-            keep = (lane >= strip * slot) & (lane < strip * (slot + 1))
-            low[group] = jnp.where(keep, pltpu.roll(lo, (strip * slot) % lanes, 1), low[group])
-            high[group] = jnp.where(
-                keep, pltpu.roll(hi, (strip * slot - (lanes - strip)) % lanes, 1), high[group]
-            )
-            index += 1
-    for group in range(low_ref.shape[0]):
-        low_ref[group] = low[group]
-        high_ref[group] = high[group]
+    halo = below_lo.shape[1]
+    middle = adj_lo.shape[1]
+    pieces = ((0, halo), (halo, halo + middle), (halo + middle, 2 * halo + middle))
+    groups = low_ref.shape[0]
+    for part, (start, stop) in enumerate(pieces):
+        lane = lax.broadcasted_iota(jnp.int32, (stop - start, lanes), 1)
+        low = [jnp.zeros((stop - start, lanes), jnp.float32) for _ in range(groups)]
+        high = [jnp.zeros((stop - start, lanes), jnp.float32) for _ in range(groups)]
+        index = 0
+        for lo_ref, hi_ref in ((adj_lo, adj_hi), (jd_lo, jd_hi), (fw_lo, fw_hi)):
+            for f in range(lo_ref.shape[0]):
+                group, slot = divmod(index, STRIPS)
+                if part == 0:
+                    lo, hi = below_lo[index], below_hi[index]
+                elif part == 1:
+                    lo, hi = lo_ref[f], hi_ref[f]
+                else:
+                    lo, hi = above_lo[index], above_hi[index]
+                keep = (lane >= strip * slot) & (lane < strip * (slot + 1))
+                low[group] = jnp.where(keep, pltpu.roll(lo, (strip * slot) % lanes, 1), low[group])
+                high[group] = jnp.where(
+                    keep, pltpu.roll(hi, (strip * slot - (lanes - strip)) % lanes, 1), high[group]
+                )
+                index += 1
+        for group in range(groups):
+            low_ref[group, start:stop] = low[group]
+            high_ref[group, start:stop] = high[group]
 
 
 def pack_strips(fields, below, above, deep):

time: 96.1 us -> 96.1 us (level)
  no operation moved by 1% of the time
where the time goes in v8:
time: 96.1 us; the launch traced here: 95.5 us
  starting transfers between devices  40.1 us (42%)
  Pallas kernels  25.2 us (26%)
  waiting for transfers between devices  11 us (11%)
  blocking collectives  9.28 us (10%)
  local copies, waits for them, and re-layouts  6.33 us (7%)
  between operations  2.19 us (2%)
  other arithmetic  1.38 us (1%)
    pallas_call x1, Pallas kernels, flow_iterations(): pl.pallas_call(flow_kernel, out_shape=jax.ShapeDtypeStruct((nf, rows_here...  18.5 us
    ppermute x1, starting transfers between devices, local(): part_above = lax.ppermute(both, part_axis, backward)  17.4 us
    ppermute x1, starting transfers between devices, local(): lax.ppermute(jnp.concatenate([x[:, :deep] for x in fields], axis=0), 'blk...  9.75 us
    all_to_all x1, blocking collectives, local(): lax.all_to_all(sensitivity, 'sub', split_axis=1, concat_axis=2, tiled=True)  9.28 us
    ppermute x1, waiting for transfers between devices, local(): part_below = lax.ppermute(both, part_axis, forward)  5.6 us
    ppermute x1, starting transfers between devices, local(): lax.ppermute(jnp.concatenate([x[:, rows_here - deep:] for x in fields], a...  4.59 us
    unnamed x29, local copies, waits for them, and re-layouts  3.98 us
    pallas_call x1, Pallas kernels, warp_sweeps(): pl.pallas_call(functools.partial(warp_kernel, part_count), out_shape=jax....  3.6 us
  transfers between devices with their start and end apart: 6, of which 5 were waited for; matrix products, arithmetic and copies ran while one was open for 1% of the time, Pallas kernels for 0%

profile of v8, /device:TPU:1, one launch (start us, length us, event | category | flops | bytes accessed | tf_op | source)
XLA Modules:
  0.0 95.5 jit_solution(11094889207422849300)
XLA Ops:
  0.6 0.0 copy-start.3
  0.6 0.0 copy-start.5
  0.7 1.4 %fusion = (f32[36,8,512]{2,1,0:T(8,128)S(1)}, f32[36,8,512]{2,1,0:T(8,128)S(1)}) fusion(f32[36,32,512]{2,1,0:T(8,128)} %bitcast.13), kind=kLoop, calls=%fused_computation.6 | loop fusion | bytes 2359296 | tf_op jit(solution)/shard_map/slice | solution.py:229
  2.1 0.0 copy-done.3
  2.1 0.0 copy-done.5
  2.2 0.1 pad_maximum_fusion
  2.2 0.0 copy-start.13
  2.2 0.0 copy-start.12
  2.3 4.6 %collective-permute-start = (f32[50,8,512]{2,1,0:T(8,128)S(1)}, f32[50,8,512]{2,1,0:T(8,128)S(1)}, u32[]{:S(2)}, u32[]{:S(2)}) collective-permute-start(f32[50,8,512]{2,1,0:T(8,128)S(1)} %pad_maximum_fusion), channel_id=1, source_target_pairs={{0,4},{4,8},{8,12},{12,16},{16,20},{20,24},{24,28},{28,32},{32,36}... | collective-permute-start | bytes 2457608 | tf_op jit(solution)/shard_map/ppermute | solution.py:226
  6.9 0.1 pad_maximum_fusion.1
  6.9 9.8 %collective-permute-start.1 = (f32[50,8,512]{2,1,0:T(8,128)S(1)}, f32[50,8,512]{2,1,0:T(8,128)}, u32[]{:S(2)}, u32[]{:S(2)}) collective-permute-start(f32[50,8,512]{2,1,0:T(8,128)S(1)} %pad_maximum_fusion.1), channel_id=1, source_target_pairs={{4,0},{8,4},{12,8},{16,12},{20,16},{24,20},{28,24},{32,28},{36,32}... | collective-permute-start | bytes 2457608 | tf_op jit(solution)/shard_map/ppermute | solution.py:229
  16.7 0.0 copy-done.13
  16.7 0.6 fusion.3
  18.6 0.0 copy-done.12
  18.6 0.1 reshape.17.flux_ref
  18.8 0.0 collective-permute-done.below_lo.below_hi.below_hbm
  18.8 0.0 copy-start.1
  18.8 1.9 %collective-permute-done.1.above_lo.above_hi.above_hbm = f32[50,8,512]{2,1,0:T(8,128)} collective-permute-done((f32[50,8,512]{2,1,0:T(8,128)S(1)}, f32[50,8,512]{2,1,0:T(8,128)}, u32[]{:S(2)}, u32[]{:S(2)}) %collective-permute-start.1) | collective-permute-done | bytes 819232 | tf_op jit(solution)/shard_map/ppermute | solution.py:229
  20.7 0.0 copy-done.1
  20.7 0.0 copy-start
  20.7 3.1 %shard_map.86 = (f32[4,48,128]{2,1,0:T(8,128)}, f32[4,48,128]{2,1,0:T(8,128)}) custom-call(f32[6,32,512]{2,1,0:T(8,128)} %adj_hbm.1, f32[6,32,512]{2,1,0:T(8,128)} %adj_hbm.1, f32[36,32,512]{2,1,0:T(8,128)} %bitcast.14, f32[36,32,512]{2,1,0:T(8,128)} %bitcast.15, f32[8,32,512]{2,1,0:T(8,128)} %fw_hbm.1, f32[8,32,512]{2,1,0:T(8,128)} %fw_hbm.1, ...), custom_call_target="tpu_custom_call" | custom-call | tf_op jit(solution)/shard_map/pallas_call | solution.py:81
  23.8 3.1 %collective-permute-start.2 = (f32[4,48,128]{2,1,0:T(8,128)}, f32[4,48,128]{2,1,0:T(8,128)S(1)}, u32[]{:S(2)}, u32[]{:S(2)}) collective-permute-start(f32[4,48,128]{2,1,0:T(8,128)} %get-tuple-element.4), channel_id=1, source_target_pairs={{0,1},{1,2},{2,3},{3,0},{4,5},{5,6},{6,7},{7,4},{8,9},{9,10},{10,1... | collective-permute-start | bytes 294920 | tf_op jit(solution)/shard_map/ppermute | solution.py:234
  26.9 3.4 %collective-permute-start.3 = (f32[4,48,128]{2,1,0:T(8,128)}, f32[4,48,128]{2,1,0:T(8,128)S(1)}, u32[]{:S(2)}, u32[]{:S(2)}) collective-permute-start(f32[4,48,128]{2,1,0:T(8,128)} %get-tuple-element.5), channel_id=1, source_target_pairs={{1,0},{2,1},{3,2},{0,3},{5,4},{6,5},{7,6},{4,7},{9,8},{10,9},{11,1... | collective-permute-start | bytes 294920 | tf_op jit(solution)/shard_map/ppermute | solution.py:235
  30.3 0.1 pad_maximum_fusion.3.link_ref
  30.4 0.2 collective-permute-done.2.left_ref
  30.6 1.9 %collective-permute-done.3.right_ref = f32[4,48,128]{2,1,0:T(8,128)S(1)} collective-permute-done((f32[4,48,128]{2,1,0:T(8,128)}, f32[4,48,128]{2,1,0:T(8,128)S(1)}, u32[]{:S(2)}, u32[]{:S(2)}) %collective-permute-start.3) | collective-permute-done | bytes 98336 | tf_op jit(solution)/shard_map/ppermute | solution.py:235
  32.5 0.0 copy-done
  32.5 0.0 copy-start.2
  32.5 1.1 %copy-done.2 = f32[50,8,512]{2,1,0:T(8,128)S(1)} copy-done((f32[50,8,512]{2,1,0:T(8,128)S(1)}, f32[50,8,512]{2,1,0:T(8,128)}, u32[]{:S(2)}) %copy-start.2) | copy-done | bytes 819224
  33.7 1.0 %copy-done.4 = f32[8,32,512]{2,1,0:T(8,128)S(1)} copy-done((f32[8,32,512]{2,1,0:T(8,128)S(1)}, f32[8,32,512]{2,1,0:T(8,128)}, u32[]{:S(2)}) %copy-start.4) | copy-done | bytes 524312
  34.7 1.0 %copy-done.6 = f32[6,32,512]{2,1,0:T(8,128)S(1)} copy-done((f32[6,32,512]{2,1,0:T(8,128)S(1)}, f32[6,32,512]{2,1,0:T(8,128)}, u32[]{:S(2)}) %copy-start.6) | copy-done | bytes 393240
  35.7 18.5 %shard_map.87 = f32[6,32,512]{2,1,0:T(8,128)} custom-call(f32[288]{0:T(512)S(1)} %reshape.17.flux_ref, f32[2]{0:T(128)S(1)} %pad_maximum_fusion.3.link_ref, f32[6,32,512]{2,1,0:T(8,128)S(1)} %copy-done.6, f32[36,32,512]{2,1,0:T(8,128)S(1)} %bitcast.16, f32[8,32,512]{2,1,0:T(8,128)S(1)} %copy-done.4, f32[50,8,512]{2,1,0:T(8,128)S(1)} %copy-done.2, ...), custom_call_target="tpu_custom_call" | custom-call | tf_op jit(solution)/shard_map/pallas_call | solution.py:193
  54.2 0.0 copy-done.8
  54.2 0.0 copy-start.11
  54.2 1.2 %multiply_reduce_fusion = f32[32,512,3]{1,0,2:T(8,128)S(1)} fusion(f32[32,512,6]{1,0,2:T(8,128)} %bitcast.17, bf16[3,6,32,512]{3,2,1,0:T(8,128)(2,1)S(1)} %copy-done.8), kind=kLoop, calls=%fused_computation | loop fusion | flops 835584 | bytes 1179648
  55.4 0.1 copy.22
  55.5 9.3 %all_to_all.18 = f32[3,32,512]{2,0,1:T(4,128)S(1)} all-to-all(f32[3,32,512]{2,0,1:T(4,128)S(1)} %bitcast.18), channel_id=1, replica_groups=mesh['blk'=192,'sub'=4] {'sub'}, dimensions={1} | all-to-all | bytes 393216 | tf_op jit(solution)/shard_map/all_to_all | solution.py:245
  64.8 0.1 copy.11
  64.9 0.0 copy-done.11
  64.9 0.0 copy-start.7
  64.9 17.4 %collective-permute-start.4 = (f32[4,8,2048]{2,1,0:T(8,128)S(1)}, f32[4,8,2048]{2,1,0:T(8,128)S(1)}, u32[]{:S(2)}, u32[]{:S(2)}) collective-permute-start(f32[4,8,2048]{2,1,0:T(8,128)S(1)} %pad_maximum_fusion.2.mid_ref), channel_id=1, source_target_pairs={{1,0},{2,1},{3,2},{4,3},{5,4},{6,5},{7,6},{8,7},{9,8},{10,9},{11,1... | collective-permute-start | bytes 786440 | tf_op jit(solution)/shard_map/ppermute | solution.py:254
  82.3 1.9 %collective-permute-start.5 = (f32[4,8,2048]{2,1,0:T(8,128)S(1)}, f32[4,8,2048]{2,1,0:T(8,128)S(1)}, u32[]{:S(2)}, u32[]{:S(2)}) collective-permute-start(f32[4,8,2048]{2,1,0:T(8,128)S(1)} %pad_maximum_fusion.2.mid_ref), channel_id=1, source_target_pairs={{0,1},{1,2},{2,3},{3,4},{4,5},{5,6},{6,7},{7,8},{8,9},{9,10},{10,1... | collective-permute-start | bytes 786440 | tf_op jit(solution)/shard_map/ppermute | solution.py:253
  84.3 1.4 %collective-permute-done.4.above_ref = f32[4,8,2048]{2,1,0:T(8,128)S(1)} collective-permute-done((f32[4,8,2048]{2,1,0:T(8,128)S(1)}, f32[4,8,2048]{2,1,0:T(8,128)S(1)}, u32[]{:S(2)}, u32[]{:S(2)}) %collective-permute-start.4) | collective-permute-done | bytes 262176 | tf_op jit(solution)/shard_map/ppermute | solution.py:254
  85.6 5.6 %collective-permute-done.5.below_ref = f32[4,8,2048]{2,1,0:T(8,128)S(1)} collective-permute-done((f32[4,8,2048]{2,1,0:T(8,128)S(1)}, f32[4,8,2048]{2,1,0:T(8,128)S(1)}, u32[]{:S(2)}, u32[]{:S(2)}) %collective-permute-start.5) | collective-permute-done | bytes 262176 | tf_op jit(solution)/shard_map/ppermute | solution.py:253
  91.2 0.0 copy-done.7
  91.2 0.0 copy-done.9
  91.2 0.7 copy-done.10
  91.9 3.6 %shard_map.88 = f32[3,8,2048]{2,1,0:T(8,128)} custom-call(s32[1]{0:T(128)} %bitcast.3.index_ref, f32[4,8,2048]{2,1,0:T(8,128)} %copy-done.7, f32[4,8,2048]{2,1,0:T(8,128)} %copy-done.9, f32[4,8,2048]{2,1,0:T(8,128)} %copy-done.10), custom_call_target="tpu_custom_call" | custom-call | tf_op jit(solution)/shard_map/pallas_call | solution.py:293
  (9 shorter events, 0.1 us)
Async XLA Ops:
  0.6 1.4 %copy-start.3 = (f32[8,32,512]{2,1,0:T(8,128)S(1)}, f32[8,32,512]{2,1,0:T(8,128)}, u32[]{:S(2)}) copy-start(f32[8,32,512]{2,1,0:T(8,128)} %fw_hbm.1) | copy-start | bytes 1572868
  0.6 1.5 %copy-start.5 = (f32[6,32,512]{2,1,0:T(8,128)S(1)}, f32[6,32,512]{2,1,0:T(8,128)}, u32[]{:S(2)}) copy-start(f32[6,32,512]{2,1,0:T(8,128)} %adj_hbm.1) | copy-start | bytes 1179652
  2.2 14.5 %copy-start.13 = (s32[192]{0:T(256)S(1)}, s32[192]{0:T(256)}, u32[]{:S(2)}) copy-start(s32[192]{0:T(256)} %param.11) | copy-start | bytes 2308
  2.2 16.4 %copy-start.12 = (f32[8,6,6]{2,0,1:T(8,128)S(1)}, f32[8,6,6]{2,0,1:T(8,128)}, u32[]{:S(2)}) copy-start(f32[8,6,6]{2,0,1:T(8,128)} %param.10) | copy-start | bytes 3460
  2.3 16.5 %collective-permute-start = (f32[50,8,512]{2,1,0:T(8,128)S(1)}, f32[50,8,512]{2,1,0:T(8,128)S(1)}, u32[]{:S(2)}, u32[]{:S(2)}) collective-permute-start(f32[50,8,512]{2,1,0:T(8,128)S(1)} %pad_maximum_fusion), channel_id=1, source_target_pairs={{0,4},{4,8},{8,12},{12,16},{16,20},{20,24},{24,28},{28,32},{32,36}... | collective-permute-start | bytes 2457608 | tf_op jit(solution)/shard_map/ppermute | solution.py:226
  6.9 13.8 %collective-permute-start.1 = (f32[50,8,512]{2,1,0:T(8,128)S(1)}, f32[50,8,512]{2,1,0:T(8,128)}, u32[]{:S(2)}, u32[]{:S(2)}) collective-permute-start(f32[50,8,512]{2,1,0:T(8,128)S(1)} %pad_maximum_fusion.1), channel_id=1, source_target_pairs={{4,0},{8,4},{12,8},{16,12},{20,16},{24,20},{28,24},{32,28},{36,32}... | collective-permute-start | bytes 2457608 | tf_op jit(solution)/shard_map/ppermute | solution.py:229
  18.8 1.9 %copy-start.1 = (f32[50,8,512]{2,1,0:T(8,128)}, f32[50,8,512]{2,1,0:T(8,128)S(1)}, u32[]{:S(2)}) copy-start(f32[50,8,512]{2,1,0:T(8,128)S(1)} %collective-permute-done.below_lo.below_hi.below_hbm) | copy-start | bytes 2457604
  20.7 11.8 %copy-start = (f32[6,6,32,512]{3,2,1,0:T(8,128)S(1)}, f32[6,6,32,512]{3,2,1,0:T(8,128)}, u32[]{:S(2)}) copy-start(f32[6,6,32,512]{3,2,1,0:T(8,128)} %param.8) | copy-start | bytes 7077892
  23.8 6.8 %collective-permute-start.2 = (f32[4,48,128]{2,1,0:T(8,128)}, f32[4,48,128]{2,1,0:T(8,128)S(1)}, u32[]{:S(2)}, u32[]{:S(2)}) collective-permute-start(f32[4,48,128]{2,1,0:T(8,128)} %get-tuple-element.4), channel_id=1, source_target_pairs={{0,1},{1,2},{2,3},{3,0},{4,5},{5,6},{6,7},{7,4},{8,9},{9,10},{10,1... | collective-permute-start | bytes 294920 | tf_op jit(solution)/shard_map/ppermute | solution.py:234
  26.9 5.6 %collective-permute-start.3 = (f32[4,48,128]{2,1,0:T(8,128)}, f32[4,48,128]{2,1,0:T(8,128)S(1)}, u32[]{:S(2)}, u32[]{:S(2)}) collective-permute-start(f32[4,48,128]{2,1,0:T(8,128)} %get-tuple-element.5), channel_id=1, source_target_pairs={{1,0},{2,1},{3,2},{0,3},{5,4},{6,5},{7,6},{4,7},{9,8},{10,9},{11,1... | collective-permute-start | bytes 294920 | tf_op jit(solution)/shard_map/ppermute | solution.py:235
  32.5 1.1 %copy-start.2 = (f32[50,8,512]{2,1,0:T(8,128)S(1)}, f32[50,8,512]{2,1,0:T(8,128)}, u32[]{:S(2)}) copy-start(f32[50,8,512]{2,1,0:T(8,128)} %copy-done.1) | copy-start | bytes 2457604
  33.7 1.0 %copy-start.4 = (f32[8,32,512]{2,1,0:T(8,128)S(1)}, f32[8,32,512]{2,1,0:T(8,128)}, u32[]{:S(2)}) copy-start(f32[8,32,512]{2,1,0:T(8,128)} %fw_hbm.1) | copy-start | bytes 1572868
  34.7 1.0 %copy-start.6 = (f32[6,32,512]{2,1,0:T(8,128)S(1)}, f32[6,32,512]{2,1,0:T(8,128)}, u32[]{:S(2)}) copy-start(f32[6,32,512]{2,1,0:T(8,128)} %adj_hbm.1) | copy-start | bytes 1179652
  35.7 18.5 %copy-start.8 = (bf16[3,6,32,512]{3,2,1,0:T(8,128)(2,1)S(1)}, bf16[3,6,32,512]{3,2,1,0:T(8,128)(2,1)}, u32[]{:S(2)}) copy-start(bf16[3,6,32,512]{3,2,1,0:T(8,128)(2,1)} %param.12) | copy-start | bytes 1769476
  54.2 10.7 %copy-start.11 = (f32[8,2048]{1,0:T(8,128)S(1)}, f32[8,2048]{1,0:T(8,128)}, u32[]{:S(2)}) copy-start(f32[8,2048]{1,0:T(8,128)} %param.13) | copy-start | bytes 196612
  64.9 26.3 %copy-start.7 = (f32[4,8,2048]{2,1,0:T(8,128)}, f32[4,8,2048]{2,1,0:T(8,128)S(1)}, u32[]{:S(2)}) copy-start(f32[4,8,2048]{2,1,0:T(8,128)S(1)} %pad_maximum_fusion.2.mid_ref) | copy-start | bytes 786436
  64.9 20.7 %collective-permute-start.4 = (f32[4,8,2048]{2,1,0:T(8,128)S(1)}, f32[4,8,2048]{2,1,0:T(8,128)S(1)}, u32[]{:S(2)}, u32[]{:S(2)}) collective-permute-start(f32[4,8,2048]{2,1,0:T(8,128)S(1)} %pad_maximum_fusion.2.mid_ref), channel_id=1, source_target_pairs={{1,0},{2,1},{3,2},{4,3},{5,4},{6,5},{7,6},{8,7},{9,8},{10,9},{11,1... | collective-permute-start | bytes 786440 | tf_op jit(solution)/shard_map/ppermute | solution.py:254
  82.3 8.9 %collective-permute-start.5 = (f32[4,8,2048]{2,1,0:T(8,128)S(1)}, f32[4,8,2048]{2,1,0:T(8,128)S(1)}, u32[]{:S(2)}, u32[]{:S(2)}) collective-permute-start(f32[4,8,2048]{2,1,0:T(8,128)S(1)} %pad_maximum_fusion.2.mid_ref), channel_id=1, source_target_pairs={{0,1},{1,2},{2,3},{3,4},{4,5},{5,6},{6,7},{7,8},{8,9},{9,10},{10,1... | collective-permute-start | bytes 786440 | tf_op jit(solution)/shard_map/ppermute | solution.py:253
  85.6 5.6 %copy-start.9 = (f32[4,8,2048]{2,1,0:T(8,128)}, f32[4,8,2048]{2,1,0:T(8,128)S(1)}, u32[]{:S(2)}) copy-start(f32[4,8,2048]{2,1,0:T(8,128)S(1)} %collective-permute-done.4.above_ref) | copy-start | bytes 786436
  91.2 0.7 copy-start.10
